TPU v7x, 256 devices: a whole 4x4x8 slice. The times are simulated.
256 devices in a mesh: expert: 64 (over z, y, x_hi), tensor: 4 (over x_lo, core).
Axes of the slice: x: 4 (x_hi: 2, x_lo: 2; x = x_hi * 2 + x_lo), y: 4, z: 8, core: 2. Of those that a mesh axis runs over, the one named last changes fastest.
Arguments:
- attn_partial: bfloat16 [4, 8192, 4096], P('tensor', 'expert'), may hold values from -4 to 4
- residual: bfloat16 [8192, 4096], P('expert', 'tensor'), may hold values from -40 to 40
- norm_gain: float32 [4096], P('tensor'), may hold values from 0.1 to 1.9
- expert_ids: int32 [8192, 4], P('expert'), may hold values from 0 to 63, all different within a row; in each aligned block of 128 rows (0 to 127, 128 to 255, ...) at most 10 rows name the same one
- route_weight: float32 [8192, 4], P('expert'), may hold values from 0.1 to 1
- w_in: bfloat16 [64, 4096, 2048], P('expert', 'tensor'), may hold values from -0.09375 to 0.09375
- w_down: bfloat16 [64, 1024, 4096], P('expert', None, 'tensor'), may hold values from -0.1875 to 0.1875
Outputs:
- layer_out: bfloat16 [8192, 4096], P('expert', 'tensor')
Inputs may be any that keep to these rules, and one draw needn't show every extreme that they name: `expert_ids`: in each aligned block of 128 rows (the tokens of one index of expert) no expert is named by more than 10 rows, a bound that some block reaches. A row names 4 different experts.
All inputs are finite; a program needn't handle non-finite values.
Results may differ from a plain program's by a relative error of at most 0.01.
Values may be sent and summed in bfloat16 or wider, within the bound.
No kernel may reach another device: no remote copies, remote signals or barrier semaphores. Data moves between devices by JAX's collectives and lax.ppermute only.
A program may use at most 64 MiB of HBM per device.

v0:
```python
import jax
import jax.numpy as jnp
from jax import lax
from jax.sharding import PartitionSpec as P


def body(attn_partial, residual, norm_gain, expert_ids, route_weight, w_in, w_down):
    token_count = expert_ids.shape[0]
    topk_count = expert_ids.shape[1]
    feature_local = residual.shape[1]
    feature_count = feature_local * lax.axis_size("tensor")
    hidden_width = w_down.shape[1]
    expert_count = lax.axis_size("expert")
    capacity = 5 * token_count * topk_count // (4 * expert_count)
    attention = lax.psum_scatter(
        attn_partial[0].astype(jnp.float32).astype(jnp.bfloat16),
        "tensor",
        scatter_dimension=1,
        tiled=True,
    ).astype(jnp.float32)
    stream = residual.astype(jnp.float32) + attention
    squares = lax.psum(jnp.sum(stream * stream, axis=1), "tensor")
    inverse = lax.rsqrt(squares / feature_count + 1e-06)[:, None]
    normed = stream * inverse * norm_gain[None, :]
    rows = normed.astype(jnp.bfloat16)
    flat_ids = expert_ids.reshape(-1)
    one_hot = (flat_ids[:, None] == jnp.arange(expert_count, dtype=jnp.int32)[None, :]).astype(
        jnp.int32
    )
    earlier = jnp.cumsum(one_hot, axis=0) - one_hot
    slot_index = jnp.sum(earlier * one_hot, axis=1)
    positions = (flat_ids * capacity + slot_index).reshape(token_count, topk_count)
    places = jnp.arange(expert_count * capacity, dtype=jnp.int32)
    matches = positions[None, :, :] == places[:, None, None]
    dispatch = jnp.any(matches, axis=2)
    sent_rows = jnp.dot(dispatch.astype(jnp.bfloat16), rows, preferred_element_type=jnp.float32)
    sent_rows = sent_rows.astype(jnp.bfloat16).reshape(expert_count, capacity, feature_local)
    weights_table = jnp.sum(jnp.where(matches, route_weight[None, :, :], 0.0), axis=2).T
    in_rows = lax.all_to_all(sent_rows, "expert", split_axis=0, concat_axis=0, tiled=True)
    source_count = in_rows.shape[0]
    item_count = in_rows.shape[1]
    row_total = source_count * item_count
    flat_rows = in_rows.reshape(row_total, feature_local)
    partial_value = jnp.dot(flat_rows, w_in[0], preferred_element_type=jnp.float32)
    total = lax.psum(partial_value.astype(jnp.bfloat16), "tensor").astype(jnp.float32)
    hidden = (jax.nn.silu(total[:, :hidden_width]) * total[:, hidden_width:]).astype(jnp.bfloat16)
    produced = jnp.dot(hidden, w_down[0], preferred_element_type=jnp.float32).astype(jnp.bfloat16)
    results = produced.reshape(source_count, item_count, feature_local)
    returned = lax.all_to_all(results, "expert", split_axis=0, concat_axis=0, tiled=True)
    routed = jnp.dot(
        weights_table,
        returned.reshape(expert_count * capacity, feature_local).astype(jnp.float32),
        precision=lax.Precision.HIGHEST,
    )
    return (stream + routed).astype(jnp.bfloat16)


def solution(mesh):
    in_specs = (
        P("tensor", "expert", None),
        P("expert", "tensor"),
        P("tensor"),
        P("expert", None),
        P("expert", None),
        P("expert", "tensor", None),
        P("expert", None, "tensor"),
    )
    out_specs = P("expert", "tensor")
    return jax.shard_map(body, mesh=mesh, in_specs=in_specs, out_specs=out_specs, check_vma=False)
```

profile of v0, /device:TPU:32, one launch (start us, length us, event | category | flops | bytes accessed | tf_op | source)
XLA Modules:
  0.0 268.0 jit_solution(16076275313622663819)
XLA Ops:
  6.5 0.0 copy-start
  6.5 0.0 reduce-scatter.2.cloned.1.call-start
  6.5 0.7 reduce-scatter.2.cloned.1.call-update
  7.3 0.0 all-reduce.2.cloned.1.call-start
  7.3 0.8 copy.22
  8.1 0.1 eq.42
  8.2 0.1 eq.38
  8.3 1.2 reduce-window.6
  9.5 0.2 slice_reduce_fusion
  9.8 0.1 fusion.18
  9.9 0.1 reduce_sum.30
  10.1 0.1 copy.25
  10.1 0.7 multiply_add_fusion
  10.8 0.2 fusion.11
  11.0 24.3 %reduce-scatter.2.cloned.1.call-done = bf16[128,1024]{1,0:T(8,128)(2,1)} async-done(((bf16[128,4096]{1,0:T(8,128)(2,1)}), bf16[128,1024]{1,0:T(8,128)(2,1)}) %reduce-scatter.2.cloned.1.call-update) | async-done | bytes 262160 | tf_op jit(solution)/shard_map/reduce_scatter | solution.py:15
  35.2 1.1 multiply_reduce_fusion
  36.4 6.4 %psum.14 = f32[128]{0:T(128)S(1)} all-reduce(f32[128]{0:T(128)S(1)} %multiply_reduce_fusion), channel_id=1, replica_groups=mesh['expert'=64,'tensor'=4] {'tensor'}, use_global_device_ids=true, to_apply=%region_7.8 | all-reduce | flops 128 | bytes 1024 | tf_op jit(solution)/shard_map/psum | solution.py:22
  42.8 1.6 convolution_convert_fusion
  44.4 1.6 reshape.40
  46.0 64.5 %all_to_all.10 = bf16[64,10,1024]{2,1,0:T(8,128)(2,1)} all-to-all(bf16[64,10,1024]{2,1,0:T(8,128)(2,1)} %reshape.40), channel_id=1, replica_groups=mesh['expert'=64,'tensor'=4] {'expert'}, dimensions={0} | all-to-all | bytes 2621440 | tf_op jit(solution)/shard_map/all_to_all | solution.py:39
  110.5 2.6 reshape.41
  113.0 6.4 %fusion.2 = bf16[640,2048]{1,0:T(8,128)(2,1)} fusion(bf16[640,1024]{1,0:T(8,128)(2,1)S(1)} %reshape.41, bf16[1,1024,2048]{2,1,0:T(8,128)(2,1)} %param.12), kind=kOutput, calls=%fused_computation.2 | convolution fusion | flops 2685665280 | bytes 8126464 | tf_op jit(solution)/shard_map/dot_general | solution.py:44
  119.4 0.0 all-reduce.2.cloned.1.call-update
  119.4 65.5 %all-reduce.2.cloned.1.call-done = bf16[640,2048]{1,0:T(8,128)(2,1)} async-done(((bf16[640,2048]{1,0:T(8,128)(2,1)}), bf16[640,2048]{1,0:T(8,128)(2,1)}) %all-reduce.2.cloned.1.call-update) | async-done | bytes 2621456 | tf_op jit(solution)/shard_map/psum | solution.py:45
  184.9 2.4 convert_element_type.45
  187.4 1.6 fusion.8
  189.0 1.5 reshape.42
  190.5 12.9 %all-to-all-start.1 = ((bf16[64,10,1024]{2,1,0:T(8,128)(2,1)}), bf16[64,10,1024]{2,1,0:T(8,128)(2,1)}, u32[]{:S(2)}, u32[]{:S(2)}) async-start(bf16[64,10,1024]{2,1,0:T(8,128)(2,1)} %reshape.42), calls=%async_computation.2 | async-start | bytes 4194304 | tf_op jit(solution)/shard_map/all_to_all | solution.py:49
  203.4 0.9 select_reduce_fusion
  204.3 51.6 %all-to-all-done.1 = bf16[64,10,1024]{2,1,0:T(8,128)(2,1)} async-done(((bf16[64,10,1024]{2,1,0:T(8,128)(2,1)}), bf16[64,10,1024]{2,1,0:T(8,128)(2,1)}, u32[]{:S(2)}, u32[]{:S(2)}) %all-to-all-start.1) | async-done | bytes 1310752 | tf_op jit(solution)/shard_map/all_to_all | solution.py:49
  255.9 2.6 reshape.43
  258.5 2.7 %fusion.13 = bf16[128,1024]{1,0:T(8,128)(2,1)} fusion(f32[640,128]{1,0:T(8,128)} %select_reduce_fusion, bf16[640,1024]{1,0:T(8,128)(2,1)S(1)} %reshape.43, bf16[128,1024]{1,0:T(8,128)(2,1)} %reduce-scatter.2.cloned.1.call-done, bf16[128,1024]{1,0:T(8,128)(2,1)} %param.8), kind=kOutput, calls=%fused_computation.13 | convolution fusion | flops 1007288320 | bytes 2424832 | tf_op jit(solution)/shard_map/dot_general | solution.py:50
  (11 shorter events, 0.1 us)
Async XLA Ops:
  6.5 180.8 %copy-start = (bf16[1,1024,1024]{2,1,0:T(8,128)(2,1)S(1)}, bf16[1,1024,1024]{2,1,0:T(8,128)(2,1)}, u32[]{:S(2)}) copy-start(bf16[1,1024,1024]{2,1,0:T(8,128)(2,1)} %param.13) | copy-start | bytes 6291460
  6.5 28.7 %copy-start.1 = (bf16[128,1024]{1,0:T(8,128)(2,1)S(1)}, bf16[128,1024]{1,0:T(8,128)(2,1)}, u32[]{:S(2)}) copy-start(bf16[128,1024]{1,0:T(8,128)(2,1)} %param.8) | copy-start | bytes 786436
  6.5 36.2 %copy-start.2 = (f32[1024]{0:T(1024)S(1)}, f32[1024]{0:T(1024)}, u32[]{:S(2)}) copy-start(f32[1024]{0:T(1024)} %param.9) | copy-start | bytes 12292
  6.5 28.7 %reduce-scatter.2.cloned.1.call-start = ((), (), s32[]{:S(2)}) async-start(), calls=%async_computation.3 | async-start | bytes 1310720 | tf_op jit(solution)/shard_map/reduce_scatter | solution.py:15
  7.3 177.7 %all-reduce.2.cloned.1.call-start = ((), (), s32[]{:S(2)}) async-start(), calls=%async_computation.4 | async-start | bytes 5242880 | tf_op jit(solution)/shard_map/psum | solution.py:45
  190.5 12.9 %copy-start.3 = (f32[128,4]{0,1:T(4,128)S(1)}, f32[128,4]{0,1:T(4,128)}, u32[]{:S(2)}) copy-start(f32[128,4]{0,1:T(4,128)} %param.11) | copy-start | bytes 6148
  190.5 65.4 %all-to-all-start.1 = ((bf16[64,10,1024]{2,1,0:T(8,128)(2,1)}), bf16[64,10,1024]{2,1,0:T(8,128)(2,1)}, u32[]{:S(2)}, u32[]{:S(2)}) async-start(bf16[64,10,1024]{2,1,0:T(8,128)(2,1)} %reshape.42), calls=%async_computation.2 | async-start | bytes 4194304 | tf_op jit(solution)/shard_map/all_to_all | solution.py:49
Sparse Core Ops, SparseCore 0:
  9.9 25.3 reduce-scatter.1
  119.5 65.3 all-reduce.1
where the time goes:
time: 269 us; the launch traced here: 268 us
  waiting for transfers between devices  142 us (53%)
  blocking collectives  70.9 us (26%)
  between operations  13.5 us (5%)
  starting transfers between devices  13 us (5%)
  matrix products  12.2 us (5%)
  local copies, waits for them, and re-layouts  9.65 us (4%)
  other arithmetic  6.66 us (2%)
    psum x1, waiting for transfers between devices, body(): lax.psum(partial_value.astype(jnp.bfloat16), 'tensor').astype(jnp.float32)  65.5 us
    all_to_all x1, blocking collectives, body(): lax.all_to_all(sent_rows, 'expert', split_axis=0, concat_axis=0, tiled=True)  64.5 us
    all_to_all x1, waiting for transfers between devices, body(): lax.all_to_all(results, 'expert', split_axis=0, concat_axis=0, tiled=True)  51.6 us
    reduce_scatter x1, waiting for transfers between devices, body(): lax.psum_scatter(attn_partial[0].astype(jnp.float32).astype(jnp.bfloat16)...  24.3 us
    all_to_all x1, starting transfers between devices, body(): lax.all_to_all(results, 'expert', split_axis=0, concat_axis=0, tiled=True)  12.9 us
    psum x1, blocking collectives, body(): squares = lax.psum(jnp.sum(stream * stream, axis=1), 'tensor')  6.38 us
    dot_general x1, matrix products, body(): jnp.dot(flat_rows, w_in[0], preferred_element_type=jnp.float32)  6.35 us
  transfers between devices with their start and end apart: 3, of which 3 were waited for; matrix products, arithmetic and copies ran while one was open for 2% of the time, Pallas kernels for 0%

commit v1 on v0

--- a/solution.py
+++ b/solution.py
@@ -42,8 +42,11 @@
     row_total = source_count * item_count
     flat_rows = in_rows.reshape(row_total, feature_local)
     partial_value = jnp.dot(flat_rows, w_in[0], preferred_element_type=jnp.float32)
-    total = lax.psum(partial_value.astype(jnp.bfloat16), "tensor").astype(jnp.float32)
+    total = lax.psum_scatter(
+        partial_value.astype(jnp.bfloat16), "tensor", scatter_dimension=0, tiled=True
+    ).astype(jnp.float32)
     hidden = (jax.nn.silu(total[:, :hidden_width]) * total[:, hidden_width:]).astype(jnp.bfloat16)
+    hidden = lax.all_gather(hidden, "tensor", axis=0, tiled=True)
     produced = jnp.dot(hidden, w_down[0], preferred_element_type=jnp.float32).astype(jnp.bfloat16)
     results = produced.reshape(source_count, item_count, feature_local)
     returned = lax.all_to_all(results, "expert", split_axis=0, concat_axis=0, tiled=True)

time: 269 us -> 260 us (0.967)
  waiting for transfers between devices: 142 us -> 133 us
    psum x1 -> x0, waiting for transfers between devices: 65.5 us -> none  [body(): lax.psum(partial_value.astype(jnp.bfloat16), 'tensor').astype(jnp.float32)]
    reduce_scatter x0 -> x1, waiting for transfers between devices: none -> 29.7 us  [body(): lax.psum_scatter(partial_value.astype(jnp.bfloat16), 'tensor', scatter_di...]
    all_gather x0 -> x1, waiting for transfers between devices: none -> 26.1 us  [body(): hidden = lax.all_gather(hidden, 'tensor', axis=0, tiled=True)]
  transfers between devices with their start and end apart: 3 -> 4, of which waited for: 3 -> 4; matrix products, arithmetic and copies ran while one was open for 2% -> 1% of each run, Pallas kernels for 0% -> 0%
where the time goes in v1:
time: 260 us; the launch traced here: 259 us
  waiting for transfers between devices  133 us (51%)
  blocking collectives  70.9 us (27%)
  matrix products  13.5 us (5%)
  between operations  13.2 us (5%)
  starting transfers between devices  13 us (5%)
  local copies, waits for them, and re-layouts  9.65 us (4%)
  other arithmetic  5.72 us (2%)
    all_to_all x1, blocking collectives, body(): lax.all_to_all(sent_rows, 'expert', split_axis=0, concat_axis=0, tiled=True)  64.5 us
    all_to_all x1, waiting for transfers between devices, body(): lax.all_to_all(results, 'expert', split_axis=0, concat_axis=0, tiled=True)  51.7 us
    reduce_scatter x1, waiting for transfers between devices, body(): lax.psum_scatter(partial_value.astype(jnp.bfloat16), 'tensor', scatter_di...  29.7 us
    all_gather x1, waiting for transfers between devices, body(): hidden = lax.all_gather(hidden, 'tensor', axis=0, tiled=True)  26.1 us
    reduce_scatter x1, waiting for transfers between devices, body(): lax.psum_scatter(attn_partial[0].astype(jnp.float32).astype(jnp.bfloat16)...  24.9 us
    all_to_all x1, starting transfers between devices, body(): lax.all_to_all(results, 'expert', split_axis=0, concat_axis=0, tiled=True)  12.9 us
    psum x1, blocking collectives, body(): squares = lax.psum(jnp.sum(stream * stream, axis=1), 'tensor')  6.38 us
    dot_general x1, matrix products, body(): jnp.dot(flat_rows, w_in[0], preferred_element_type=jnp.float32)  6.35 us
  transfers between devices with their start and end apart: 4, of which 4 were waited for; matrix products, arithmetic and copies ran while one was open for 1% of the time, Pallas kernels for 0%

profile of v1, /device:TPU:32, one launch (start us, length us, event | category | flops | bytes accessed | tf_op | source)
XLA Modules:
  0.0 259.2 jit_solution(11429051957058724072)
XLA Ops:
  6.6 0.7 reduce-scatter.3.cloned.1.call-update
  7.3 0.0 reduce-scatter.5.cloned.1.call-start
  7.3 0.8 copy.22
  8.1 0.1 eq.42
  8.2 0.1 eq.38
  8.3 1.2 reduce-window.6
  9.5 0.2 slice_reduce_fusion
  9.8 0.1 fusion.17
  9.9 0.1 reduce_sum.30
  10.1 0.1 copy.25
  10.1 0.2 fusion.10
  10.3 24.9 %reduce-scatter.3.cloned.1.call-done = bf16[128,1024]{1,0:T(8,128)(2,1)} async-done(((bf16[128,4096]{1,0:T(8,128)(2,1)}), bf16[128,1024]{1,0:T(8,128)(2,1)}) %reduce-scatter.3.cloned.1.call-update) | async-done | bytes 262160 | tf_op jit(solution)/shard_map/reduce_scatter | solution.py:15
  35.2 1.1 multiply_reduce_fusion
  36.4 6.4 %psum.7 = f32[128]{0:T(128)S(1)} all-reduce(f32[128]{0:T(128)S(1)} %multiply_reduce_fusion), channel_id=1, replica_groups=mesh['expert'=64,'tensor'=4] {'tensor'}, use_global_device_ids=true, to_apply=%region_7.8 | all-reduce | flops 128 | bytes 1024 | tf_op jit(solution)/shard_map/psum | solution.py:22
  42.8 1.6 convolution_convert_fusion
  44.4 1.6 reshape.40
  46.0 64.5 %all_to_all.10 = bf16[64,10,1024]{2,1,0:T(8,128)(2,1)} all-to-all(bf16[64,10,1024]{2,1,0:T(8,128)(2,1)} %reshape.40), channel_id=1, replica_groups=mesh['expert'=64,'tensor'=4] {'expert'}, dimensions={0} | all-to-all | bytes 2621440 | tf_op jit(solution)/shard_map/all_to_all | solution.py:39
  110.5 2.6 reshape.41
  113.0 6.3 %fusion.2 = bf16[640,2048]{1,0:T(8,128)(2,1)} fusion(bf16[640,1024]{1,0:T(8,128)(2,1)S(1)} %reshape.41, bf16[1,1024,2048]{2,1,0:T(8,128)(2,1)} %param.12), kind=kOutput, calls=%fused_computation.2 | convolution fusion | flops 2685665280 | bytes 8126464 | tf_op jit(solution)/shard_map/dot_general | solution.py:44
  119.4 0.0 reduce-scatter.5.cloned.1.call-update
  119.4 0.0 all-gather.2.cloned.1.call-start
  119.5 29.7 %reduce-scatter.5.cloned.1.call-done = bf16[160,2048]{1,0:T(8,128)(2,1)} async-done(((bf16[640,2048]{1,0:T(8,128)(2,1)}), bf16[160,2048]{1,0:T(8,128)(2,1)}) %reduce-scatter.5.cloned.1.call-update) | async-done | bytes 655376 | tf_op jit(solution)/shard_map/reduce_scatter | solution.py:45
  149.1 1.2 convert_element_type.45
  150.4 0.9 fusion.12
  151.3 26.1 %all-gather.2.cloned.1.call-done = bf16[640,1024]{1,0:T(8,128)(2,1)} async-done(((bf16[160,1024]{1,0:T(8,128)(2,1)}), bf16[640,1024]{1,0:T(8,128)(2,1)}) %all-gather.2.cloned.1.call-update) | async-done | bytes 1310736 | tf_op jit(solution)/shard_map/all_gather | solution.py:49
  177.5 2.8 %fusion.7 = bf16[640,1024]{1,0:T(8,128)(2,1)S(1)} fusion(bf16[640,1024]{1,0:T(8,128)(2,1)} %all-gather.2.cloned.1.call-done, bf16[1,1024,1024]{2,1,0:T(8,128)(2,1)S(1)} %copy-done), kind=kOutput, calls=%fused_computation.5 | convolution fusion | flops 1342832640 | bytes 4718592 | tf_op jit(solution)/shard_map/dot_general | solution.py:50
  180.3 1.5 reshape.42
  181.8 12.9 %all-to-all-start.1 = ((bf16[64,10,1024]{2,1,0:T(8,128)(2,1)}), bf16[64,10,1024]{2,1,0:T(8,128)(2,1)}, u32[]{:S(2)}, u32[]{:S(2)}) async-start(bf16[64,10,1024]{2,1,0:T(8,128)(2,1)} %reshape.42), calls=%async_computation.3 | async-start | bytes 4194304 | tf_op jit(solution)/shard_map/all_to_all | solution.py:52
  194.8 0.9 select_reduce_fusion
  195.6 51.7 %all-to-all-done.1 = bf16[64,10,1024]{2,1,0:T(8,128)(2,1)} async-done(((bf16[64,10,1024]{2,1,0:T(8,128)(2,1)}), bf16[64,10,1024]{2,1,0:T(8,128)(2,1)}, u32[]{:S(2)}, u32[]{:S(2)}) %all-to-all-start.1) | async-done | bytes 1310752 | tf_op jit(solution)/shard_map/all_to_all | solution.py:52
  247.4 2.6 reshape.43
  250.0 2.7 %fusion.11 = bf16[128,1024]{1,0:T(8,128)(2,1)} fusion(f32[640,128]{1,0:T(8,128)} %select_reduce_fusion, bf16[640,1024]{1,0:T(8,128)(2,1)S(1)} %reshape.43, bf16[128,1024]{1,0:T(8,128)(2,1)} %reduce-scatter.3.cloned.1.call-done, bf16[128,1024]{1,0:T(8,128)(2,1)} %param.8), kind=kOutput, calls=%fused_computation.11 | convolution fusion | flops 1007288320 | bytes 2424832 | tf_op jit(solution)/shard_map/dot_general | solution.py:53
  (17 shorter events, 0.1 us)
Async XLA Ops:
  6.5 170.9 %copy-start = (bf16[1,1024,1024]{2,1,0:T(8,128)(2,1)S(1)}, bf16[1,1024,1024]{2,1,0:T(8,128)(2,1)}, u32[]{:S(2)}) copy-start(bf16[1,1024,1024]{2,1,0:T(8,128)(2,1)} %param.13) | copy-start | bytes 6291460
  6.5 3.6 %copy-start.2 = (s32[128,4]{0,1:T(4,128)S(1)}, s32[128,4]{0,1:T(4,128)}, u32[]{:S(2)}) copy-start(s32[128,4]{0,1:T(4,128)} %param.10) | copy-start | bytes 6148
  6.5 28.7 %copy-start.1 = (bf16[128,1024]{1,0:T(8,128)(2,1)S(1)}, bf16[128,1024]{1,0:T(8,128)(2,1)}, u32[]{:S(2)}) copy-start(bf16[128,1024]{1,0:T(8,128)(2,1)} %param.8) | copy-start | bytes 786436
  6.5 28.7 %reduce-scatter.3.cloned.1.call-start = ((), (), s32[]{:S(2)}) async-start(), calls=%async_computation.4 | async-start | bytes 1310720 | tf_op jit(solution)/shard_map/reduce_scatter | solution.py:15
  6.5 36.2 %copy-start.3 = (f32[1024]{0:T(1024)S(1)}, f32[1024]{0:T(1024)}, u32[]{:S(2)}) copy-start(f32[1024]{0:T(1024)} %param.9) | copy-start | bytes 12292
  7.3 141.9 %reduce-scatter.5.cloned.1.call-start = ((), (), s32[]{:S(2)}) async-start(), calls=%async_computation.5 | async-start | bytes 3276800 | tf_op jit(solution)/shard_map/reduce_scatter | solution.py:45
  119.4 58.0 %all-gather.2.cloned.1.call-start = ((), (), s32[]{:S(2)}) async-start(), calls=%async_computation.6 | async-start | bytes 1638400 | tf_op jit(solution)/shard_map/all_gather | solution.py:49
  181.8 12.9 %copy-start.4 = (f32[128,4]{0,1:T(4,128)S(1)}, f32[128,4]{0,1:T(4,128)}, u32[]{:S(2)}) copy-start(f32[128,4]{0,1:T(4,128)} %param.11) | copy-start | bytes 6148
  181.8 65.6 %all-to-all-start.1 = ((bf16[64,10,1024]{2,1,0:T(8,128)(2,1)}), bf16[64,10,1024]{2,1,0:T(8,128)(2,1)}, u32[]{:S(2)}, u32[]{:S(2)}) async-start(bf16[64,10,1024]{2,1,0:T(8,128)(2,1)} %reshape.42), calls=%async_computation.3 | async-start | bytes 4194304 | tf_op jit(solution)/shard_map/all_to_all | solution.py:52
Sparse Core Ops, SparseCore 0:
  9.9 25.3 reduce-scatter.2
  119.5 29.5 reduce-scatter.4
  151.5 25.9 all-gather.1

commit v2 on v0

--- a/solution.py
+++ b/solution.py
@@ -2,6 +2,46 @@
 import jax.numpy as jnp
 from jax import lax
 from jax.sharding import PartitionSpec as P
+
+
+def _exchange(value, flip):
+    size = lax.axis_size("tensor")
+    return lax.ppermute(value, "tensor", [(j, j ^ flip) for j in range(size)])
+
+
+def _pick(value, axis, index):
+    return lax.dynamic_index_in_dim(value, index, axis=axis, keepdims=False)
+
+
+def _reduce_scatter(value, axis):
+    t = lax.axis_index("tensor")
+    core = t % 2
+    high = t // 2
+    shape = value.shape
+    split = value.reshape(shape[:axis] + (2, 2, shape[axis] // 4) + shape[axis + 1:])
+    sent = _pick(split, axis + 1, 1 - core).astype(jnp.bfloat16)
+    kept = _pick(split, axis + 1, core).astype(jnp.float32)
+    half = kept + _exchange(sent, 1).astype(jnp.float32)
+    sent = _pick(half, axis, 1 - high).astype(jnp.bfloat16)
+    kept = _pick(half, axis, high)
+    return kept + _exchange(sent, 2).astype(jnp.float32)
+
+
+def _all_gather(value, axis):
+    t = lax.axis_index("tensor")
+    core = t % 2
+    high = t // 2
+    other = _exchange(value, 2)
+    pair = jnp.where(high == 0, jnp.stack([value, other], axis), jnp.stack([other, value], axis))
+    other = _exchange(pair, 1)
+    quad = jnp.where(core == 0, jnp.stack([pair, other], axis + 1), jnp.stack([other, pair], axis + 1))
+    shape = quad.shape
+    return quad.reshape(shape[:axis] + (shape[axis] * shape[axis + 1] * shape[axis + 2],) + shape[axis + 3:])
+
+
+def _psum(value):
+    value = value + _exchange(value, 1)
+    return value + _exchange(value, 2)
 
 
 def body(attn_partial, residual, norm_gain, expert_ids, route_weight, w_in, w_down):
@@ -12,14 +52,9 @@
     hidden_width = w_down.shape[1]
     expert_count = lax.axis_size("expert")
     capacity = 5 * token_count * topk_count // (4 * expert_count)
-    attention = lax.psum_scatter(
-        attn_partial[0].astype(jnp.float32).astype(jnp.bfloat16),
-        "tensor",
-        scatter_dimension=1,
-        tiled=True,
-    ).astype(jnp.float32)
+    attention = _reduce_scatter(attn_partial[0], 1)
     stream = residual.astype(jnp.float32) + attention
-    squares = lax.psum(jnp.sum(stream * stream, axis=1), "tensor")
+    squares = _psum(jnp.sum(stream * stream, axis=1))
     inverse = lax.rsqrt(squares / feature_count + 1e-06)[:, None]
     normed = stream * inverse * norm_gain[None, :]
     rows = normed.astype(jnp.bfloat16)
@@ -42,8 +77,9 @@
     row_total = source_count * item_count
     flat_rows = in_rows.reshape(row_total, feature_local)
     partial_value = jnp.dot(flat_rows, w_in[0], preferred_element_type=jnp.float32)
-    total = lax.psum(partial_value.astype(jnp.bfloat16), "tensor").astype(jnp.float32)
+    total = _reduce_scatter(partial_value.astype(jnp.bfloat16), 0)
     hidden = (jax.nn.silu(total[:, :hidden_width]) * total[:, hidden_width:]).astype(jnp.bfloat16)
+    hidden = _all_gather(hidden, 0)
     produced = jnp.dot(hidden, w_down[0], preferred_element_type=jnp.float32).astype(jnp.bfloat16)
     results = produced.reshape(source_count, item_count, feature_local)
     returned = lax.all_to_all(results, "expert", split_axis=0, concat_axis=0, tiled=True)

time: 269 us -> 204 us (0.76)
  waiting for transfers between devices: 142 us -> 89 us
  between operations: 13.5 us -> 0.26 us
  local copies, waits for them, and re-layouts: 9.65 us -> 15 us
  other arithmetic: 6.66 us -> 11.7 us
  blocking collectives: 70.9 us -> 66 us
    psum x1 -> x0, waiting for transfers between devices: 65.5 us -> none  [body(): lax.psum(partial_value.astype(jnp.bfloat16), 'tensor').astype(jnp.float32)]
    ppermute x0 -> x8, waiting for transfers between devices: none -> 37.8 us  [_exchange(): return lax.ppermute(value, 'tensor', [(j, j ^ flip) for j in range(size)])]
    reduce_scatter x1 -> x0, waiting for transfers between devices: 24.3 us -> none  [body(): lax.psum_scatter(attn_partial[0].astype(jnp.float32).astype(jnp.bfloat16)...]
    psum x1 -> x0, blocking collectives: 6.38 us -> none  [body(): squares = lax.psum(jnp.sum(stream * stream, axis=1), 'tensor')]
    all_to_all x1, starting transfers between devices: 12.9 us -> 6.58 us  [body(): lax.all_to_all(results, 'expert', split_axis=0, concat_axis=0, tiled=True)]
    select_n x0 -> x3, other arithmetic: none -> 4.75 us  [the longest x2 3.19 us: _all_gather(): jnp.where(high == 0, jnp.stack([value, other], axis), jnp.stack([other, v...]
    ppermute x0 -> x8, starting transfers between devices: none -> 4.54 us  [_exchange(): return lax.ppermute(value, 'tensor', [(j, j ^ flip) for j in range(size)])]
  transfers between devices with their start and end apart: 3 -> 9, of which waited for: 3 -> 9; matrix products, arithmetic and copies ran while one was open for 2% -> 3% of each run, Pallas kernels for 0% -> 0%
where the time goes in v2:
time: 204 us; the launch traced here: 203 us
  waiting for transfers between devices  89 us (44%)
  blocking collectives  66 us (32%)
  local copies, waits for them, and re-layouts  15 us (7%)
  other arithmetic  11.7 us (6%)
  starting transfers between devices  11.1 us (5%)
  matrix products  10.1 us (5%)
    all_to_all x1, blocking collectives, body(): lax.all_to_all(sent_rows, 'expert', split_axis=0, concat_axis=0, tiled=True)  66 us
    all_to_all x1, waiting for transfers between devices, body(): lax.all_to_all(results, 'expert', split_axis=0, concat_axis=0, tiled=True)  51.2 us
    ppermute x8, waiting for transfers between devices, _exchange(): return lax.ppermute(value, 'tensor', [(j, j ^ flip) for j in range(size)])  37.8 us
    all_to_all x1, starting transfers between devices, body(): lax.all_to_all(results, 'expert', split_axis=0, concat_axis=0, tiled=True)  6.58 us
    dot_general x1, matrix products, body(): jnp.dot(flat_rows, w_in[0], preferred_element_type=jnp.float32)  5.27 us
    ppermute x8, starting transfers between devices, _exchange(): return lax.ppermute(value, 'tensor', [(j, j ^ flip) for j in range(size)])  4.54 us
  transfers between devices with their start and end apart: 9, of which 9 were waited for; matrix products, arithmetic and copies ran while one was open for 3% of the time, Pallas kernels for 0%

profile of v2, /device:TPU:32, one launch (start us, length us, event | category | flops | bytes accessed | tf_op | source)
XLA Modules:
  0.0 203.1 jit_solution(17196901078666991058)
XLA Ops:
  0.0 1.8 copy.30
  1.8 1.1 constant_dynamic-slice_fusion.1
  2.9 1.3 copy.32
  4.3 1.0 copy.38
  5.5 0.8 collective-permute-done
  6.3 1.4 convert_add_fusion.1
  8.4 1.5 collective-permute-start.1
  10.0 1.2 reduce-window.6
  11.8 5.3 %collective-permute-done.1 = bf16[128,1024]{1,0:T(8,128)(2,1)} collective-permute-done((bf16[128,1024]{1,0:T(8,128)(2,1)}, bf16[128,1024]{1,0:T(8,128)(2,1)}, u32[]{:S(2)}, u32[]{:S(2)}) %collective-permute-start.1) | collective-permute-done | bytes 262176 | tf_op jit(solution)/shard_map/ppermute | solution.py:9
  17.1 1.2 multiply_reduce_fusion
  18.4 1.1 collective-permute-done.2
  19.6 1.5 collective-permute-start.3
  21.2 1.9 collective-permute-done.3
  23.7 1.6 reshape.121
  25.3 66.0 %all_to_all.10 = bf16[64,10,1024]{2,1,0:T(8,128)(2,1)} all-to-all(bf16[64,10,1024]{2,1,0:T(8,128)(2,1)} %reshape.121), channel_id=1, replica_groups=mesh['expert'=64,'tensor'=4] {'expert'}, dimensions={0} | all-to-all | bytes 2621440 | tf_op jit(solution)/shard_map/all_to_all | solution.py:74
  91.3 2.6 %reshape.122 = bf16[640,1024]{1,0:T(8,128)(2,1)S(1)} reshape(bf16[64,10,1024]{2,1,0:T(8,128)(2,1)} %all_to_all.10) | data formatting | bytes 2621440 | tf_op jit(solution)/shard_map/reshape | solution.py:78
  93.8 5.3 %fusion.2 = bf16[640,2048]{1,0:T(8,128)(2,1)S(1)} fusion(bf16[640,1024]{1,0:T(8,128)(2,1)S(1)} %reshape.122, bf16[1,1024,2048]{2,1,0:T(8,128)(2,1)} %param.12), kind=kOutput, calls=%fused_computation.2 | convolution fusion | flops 2685665280 | bytes 8126464 | tf_op jit(solution)/shard_map/dot_general | solution.py:79
  99.3 3.0 %collective-permute-done.4 = bf16[2,160,2048]{2,1,0:T(8,128)(2,1)S(1)} collective-permute-done((bf16[2,160,2048]{2,1,0:T(8,128)(2,1)S(1)}, bf16[2,160,2048]{2,1,0:T(8,128)(2,1)S(1)}, u32[]{:S(2)}, u32[]{:S(2)}) %collective-permute-start.4) | collective-permute-done | bytes 1310752 | tf_op jit(solution)/shard_map/ppermute | solution.py:9
  103.6 16.2 %collective-permute-done.5 = bf16[160,2048]{1,0:T(8,128)(2,1)S(1)} collective-permute-done((bf16[160,2048]{1,0:T(8,128)(2,1)S(1)}, bf16[160,2048]{1,0:T(8,128)(2,1)S(1)}, u32[]{:S(2)}, u32[]{:S(2)}) %collective-permute-start.5) | collective-permute-done | bytes 655392 | tf_op jit(solution)/shard_map/ppermute | solution.py:9
  119.9 0.9 fusion.13
  121.6 8.4 %collective-permute-done.6 = bf16[160,1024]{1,0:T(8,128)(2,1)} collective-permute-done((bf16[160,1024]{1,0:T(8,128)(2,1)}, bf16[160,1024]{1,0:T(8,128)(2,1)}, u32[]{:S(2)}, u32[]{:S(2)}) %collective-permute-start.6) | collective-permute-done | bytes 327712 | tf_op jit(solution)/shard_map/ppermute | solution.py:9
  130.1 2.0 maximum_select_fusion.2
  132.3 1.2 maximum_select_fusion.1
  133.4 1.1 collective-permute-done.7
  134.5 1.6 maximum_select_fusion
  136.1 1.5 fusion.7
  137.6 1.5 reshape.124
  139.1 6.6 %all-to-all-start.1 = ((bf16[64,10,1024]{2,1,0:T(8,128)(2,1)}), bf16[64,10,1024]{2,1,0:T(8,128)(2,1)}, u32[]{:S(2)}, u32[]{:S(2)}) async-start(bf16[64,10,1024]{2,1,0:T(8,128)(2,1)} %reshape.124), calls=%async_computation.1 | async-start | bytes 4194304 | tf_op jit(solution)/shard_map/all_to_all | solution.py:85
  145.7 0.9 select_reduce_fusion
  146.6 51.2 %all-to-all-done.1 = bf16[64,10,1024]{2,1,0:T(8,128)(2,1)} async-done(((bf16[64,10,1024]{2,1,0:T(8,128)(2,1)}), bf16[64,10,1024]{2,1,0:T(8,128)(2,1)}, u32[]{:S(2)}, u32[]{:S(2)}) %all-to-all-start.1) | async-done | bytes 1310752 | tf_op jit(solution)/shard_map/all_to_all | solution.py:85
  197.8 2.6 %reshape.125 = bf16[640,1024]{1,0:T(8,128)(2,1)S(1)} reshape(bf16[64,10,1024]{2,1,0:T(8,128)(2,1)} %all-to-all-done.1) | data formatting | bytes 2621440 | tf_op jit(solution)/shard_map/reshape | solution.py:88
  200.4 2.7 %fusion.11 = bf16[128,1024]{1,0:T(8,128)(2,1)} fusion(f32[128,1024]{1,0:T(8,128)} %copy-done.1, f32[640,128]{1,0:T(8,128)} %select_reduce_fusion, bf16[640,1024]{1,0:T(8,128)(2,1)S(1)} %reshape.125), kind=kOutput, calls=%fused_computation.16 | convolution fusion | flops 1006895104 | bytes 2424832 | tf_op jit(solution)/shard_map/dot_general | solution.py:86
  (40 shorter events, 5.1 us)
Async XLA Ops:
  0.0 136.1 %copy-start = (bf16[1,1024,1024]{2,1,0:T(8,128)(2,1)S(1)}, bf16[1,1024,1024]{2,1,0:T(8,128)(2,1)}, u32[]{:S(2)}) copy-start(bf16[1,1024,1024]{2,1,0:T(8,128)(2,1)} %param.13) | copy-start | bytes 6291460
  2.9 1.4 copy-start.2
  2.9 2.4 %copy-start.3 = (s32[128,4]{0,1:T(4,128)S(1)}, s32[128,4]{0,1:T(4,128)}, u32[]{:S(2)}) copy-start(s32[128,4]{0,1:T(4,128)} %param.10) | copy-start | bytes 6148
  4.2 2.1 %collective-permute-start = (bf16[128,2,1024]{2,0,1:T(8,128)(2,1)S(1)}, bf16[128,2,1024]{2,0,1:T(8,128)(2,1)}, u32[]{:S(2)}, u32[]{:S(2)}) collective-permute-start(bf16[128,2,1024]{2,0,1:T(8,128)(2,1)S(1)} %bitcast.70), channel_id=1, source_target_pairs={{0,1},{1,0},{2,3},{3,2},{4,5},{5,4},{6,7},{7,6},{8,9},{9,8},{10,11... | collective-permute-start | bytes 1572872 | tf_op jit(solution)/shard_map/ppermute | solution.py:9
  8.4 14.7 %copy-start.4 = (f32[1024]{0:T(1024)S(1)}, f32[1024]{0:T(1024)}, u32[]{:S(2)}) copy-start(f32[1024]{0:T(1024)} %param.9) | copy-start | bytes 12292
  8.4 8.7 %collective-permute-start.1 = (bf16[128,1024]{1,0:T(8,128)(2,1)}, bf16[128,1024]{1,0:T(8,128)(2,1)}, u32[]{:S(2)}, u32[]{:S(2)}) collective-permute-start(bf16[128,1024]{1,0:T(8,128)(2,1)} %fusion.15), channel_id=1, source_target_pairs={{0,2},{1,3},{2,0},{3,1},{4,6},{5,7},{6,4},{7,5},{8,10},{9,11},{10,... | collective-permute-start | bytes 786440 | tf_op jit(solution)/shard_map/ppermute | solution.py:9
  18.3 4.8 %copy-start.1 = (f32[128,1024]{1,0:T(8,128)}, f32[128,1024]{1,0:T(8,128)S(1)}, u32[]{:S(2)}) copy-start(f32[128,1024]{1,0:T(8,128)S(1)} %get-tuple-element.6) | copy-start | bytes 1572868
  18.3 1.2 collective-permute-start.2
  19.6 3.6 %collective-permute-start.3 = (f32[128]{0:T(128)S(1)}, f32[128]{0:T(128)S(1)}, u32[]{:S(2)}, u32[]{:S(2)}) collective-permute-start(f32[128]{0:T(128)S(1)} %add.77), channel_id=1, source_target_pairs={{0,2},{1,3},{2,0},{3,1},{4,6},{5,7},{6,4},{7,5},{8,10},{9,11},{10,... | collective-permute-start | bytes 1544 | tf_op jit(solution)/shard_map/ppermute | solution.py:9
  99.2 3.1 %collective-permute-start.4 = (bf16[2,160,2048]{2,1,0:T(8,128)(2,1)S(1)}, bf16[2,160,2048]{2,1,0:T(8,128)(2,1)S(1)}, u32[]{:S(2)}, u32[]{:S(2)}) collective-permute-start(bf16[2,160,2048]{2,1,0:T(8,128)(2,1)S(1)} %dynamic-slice_bitcast_fusion), channel_id=1, source_target_pairs={{0,1},{1,0},{2,3},{3,2},{4,5},{5,4},{6,7},{7,6},{8,9},{9,8},{10,11... | collective-permute-start | bytes 3932168 | tf_op jit(solution)/shard_map/ppermute | solution.py:9
  102.9 16.9 %collective-permute-start.5 = (bf16[160,2048]{1,0:T(8,128)(2,1)S(1)}, bf16[160,2048]{1,0:T(8,128)(2,1)S(1)}, u32[]{:S(2)}, u32[]{:S(2)}) collective-permute-start(bf16[160,2048]{1,0:T(8,128)(2,1)S(1)} %fusion.12), channel_id=1, source_target_pairs={{0,2},{1,3},{2,0},{3,1},{4,6},{5,7},{6,4},{7,5},{8,10},{9,11},{10,... | collective-permute-start | bytes 1966088 | tf_op jit(solution)/shard_map/ppermute | solution.py:9
  120.8 9.2 %collective-permute-start.6 = (bf16[160,1024]{1,0:T(8,128)(2,1)}, bf16[160,1024]{1,0:T(8,128)(2,1)}, u32[]{:S(2)}, u32[]{:S(2)}) collective-permute-start(bf16[160,1024]{1,0:T(8,128)(2,1)} %fusion.13), channel_id=1, source_target_pairs={{0,2},{1,3},{2,0},{3,1},{4,6},{5,7},{6,4},{7,5},{8,10},{9,11},{10,... | collective-permute-start | bytes 983048 | tf_op jit(solution)/shard_map/ppermute | solution.py:9
  132.1 2.4 %collective-permute-start.7 = (bf16[2,160,1024]{2,1,0:T(8,128)(2,1)}, bf16[2,160,1024]{2,1,0:T(8,128)(2,1)}, u32[]{:S(2)}, u32[]{:S(2)}) collective-permute-start(bf16[2,160,1024]{2,1,0:T(8,128)(2,1)} %maximum_select_fusion.2), channel_id=1, source_target_pairs={{0,1},{1,0},{2,3},{3,2},{4,5},{5,4},{6,7},{7,6},{8,9},{9,8},{10,11... | collective-permute-start | bytes 1966088 | tf_op jit(solution)/shard_map/ppermute | solution.py:9
  139.1 6.6 %copy-start.5 = (f32[128,4]{0,1:T(4,128)S(1)}, f32[128,4]{0,1:T(4,128)}, u32[]{:S(2)}) copy-start(f32[128,4]{0,1:T(4,128)} %param.11) | copy-start | bytes 6148
  139.1 58.7 %all-to-all-start.1 = ((bf16[64,10,1024]{2,1,0:T(8,128)(2,1)}), bf16[64,10,1024]{2,1,0:T(8,128)(2,1)}, u32[]{:S(2)}, u32[]{:S(2)}) async-start(bf16[64,10,1024]{2,1,0:T(8,128)(2,1)} %reshape.124), calls=%async_computation.1 | async-start | bytes 4194304 | tf_op jit(solution)/shard_map/all_to_all | solution.py:85

commit v3 on v2

--- a/solution.py
+++ b/solution.py
@@ -39,6 +39,16 @@
     return quad.reshape(shape[:axis] + (shape[axis] * shape[axis + 1] * shape[axis + 2],) + shape[axis + 3:])
 
 
+def _exchange_rows(value):
+    experts, slots, features = value.shape
+    lanes = features
+    while lanes > 128 and (slots * features // lanes) % 8 != 0:
+        lanes //= 2
+    packed = value.reshape(experts, slots * features // lanes, lanes)
+    moved = lax.all_to_all(packed, "expert", split_axis=0, concat_axis=0, tiled=True)
+    return moved.reshape(experts, slots, features)
+
+
 def _psum(value):
     value = value + _exchange(value, 1)
     return value + _exchange(value, 2)
@@ -71,7 +81,7 @@
     sent_rows = jnp.dot(dispatch.astype(jnp.bfloat16), rows, preferred_element_type=jnp.float32)
     sent_rows = sent_rows.astype(jnp.bfloat16).reshape(expert_count, capacity, feature_local)
     weights_table = jnp.sum(jnp.where(matches, route_weight[None, :, :], 0.0), axis=2).T
-    in_rows = lax.all_to_all(sent_rows, "expert", split_axis=0, concat_axis=0, tiled=True)
+    in_rows = _exchange_rows(sent_rows)
     source_count = in_rows.shape[0]
     item_count = in_rows.shape[1]
     row_total = source_count * item_count
@@ -82,7 +92,7 @@
     hidden = _all_gather(hidden, 0)
     produced = jnp.dot(hidden, w_down[0], preferred_element_type=jnp.float32).astype(jnp.bfloat16)
     results = produced.reshape(source_count, item_count, feature_local)
-    returned = lax.all_to_all(results, "expert", split_axis=0, concat_axis=0, tiled=True)
+    returned = _exchange_rows(results)
     routed = jnp.dot(
         weights_table,
         returned.reshape(expert_count * capacity, feature_local).astype(jnp.float32),

time: 204 us -> 169 us (0.83)
  blocking collectives: 66 us -> 49.2 us
  waiting for transfers between devices: 89 us -> 72.8 us
    all_to_all x1, blocking collectives: 66 us -> 49.2 us  [_exchange_rows(): lax.all_to_all(packed, 'expert', split_axis=0, concat_axis=0, tiled=True)]
    all_to_all x1, waiting for transfers between devices: 51.2 us -> 35.1 us  [_exchange_rows(): lax.all_to_all(packed, 'expert', split_axis=0, concat_axis=0, tiled=True)]
    reshape x4 -> x0, local copies, waits for them, and re-layouts: 8.23 us -> none  [the longest x1 2.57 us: body(): flat_rows = in_rows.reshape(row_total, feature_local)]
    another operation x1 -> x5, local copies, waits for them, and re-layouts: 0.01 us -> 6.62 us  [the longest x2 3.33 us: _exchange_rows(): packed = value.reshape(experts, slots * features // lanes, lanes)]
where the time goes in v3:
time: 169 us
  waiting for transfers between devices  72.8 us (43%)
  blocking collectives  49.2 us (29%)
  local copies, waits for them, and re-layouts  13.4 us (8%)
  other arithmetic  11.6 us (7%)
  starting transfers between devices  10.8 us (6%)
  matrix products  10.6 us (6%)
    all_to_all x1, blocking collectives, _exchange_rows(): lax.all_to_all(packed, 'expert', split_axis=0, concat_axis=0, tiled=True)  49.2 us
    ppermute x8, waiting for transfers between devices, _exchange(): return lax.ppermute(value, 'tensor', [(j, j ^ flip) for j in range(size)])  37.8 us
    all_to_all x1, waiting for transfers between devices, _exchange_rows(): lax.all_to_all(packed, 'expert', split_axis=0, concat_axis=0, tiled=True)  35.1 us
    all_to_all x1, starting transfers between devices, _exchange_rows(): lax.all_to_all(packed, 'expert', split_axis=0, concat_axis=0, tiled=True)  6.23 us
    dot_general x1, matrix products, body(): jnp.dot(flat_rows, w_in[0], preferred_element_type=jnp.float32)  5.46 us
    ppermute x8, starting transfers between devices, _exchange(): return lax.ppermute(value, 'tensor', [(j, j ^ flip) for j in range(size)])  4.54 us
  transfers between devices with their start and end apart: 9, of which 9 were waited for; matrix products, arithmetic and copies ran while one was open for 3% of the time, Pallas kernels for 0%

profile of v3, /device:TPU:32, one launch (start us, length us, event | category | flops | bytes accessed | tf_op | source)
XLA Modules:
  0.0 168.7 jit_solution(15663827100435823266)
XLA Ops:
  0.0 1.8 %copy.30 = bf16[1,128,4096]{1,2,0:T(8,128)(2,1)S(1)} copy(bf16[1,128,4096]{2,1,0:T(8,128)(2,1)} %param.7) | data formatting | bytes 2097152 | tf_op args[0]
  1.8 1.1 constant_dynamic-slice_fusion.1
  2.9 1.3 copy.32
  4.3 1.0 copy.38
  5.5 0.8 collective-permute-done
  6.3 1.4 convert_add_fusion.1
  8.4 1.5 collective-permute-start.1
  10.0 1.2 reduce-window.6
  11.8 5.3 %collective-permute-done.1 = bf16[128,1024]{1,0:T(8,128)(2,1)} collective-permute-done((bf16[128,1024]{1,0:T(8,128)(2,1)}, bf16[128,1024]{1,0:T(8,128)(2,1)}, u32[]{:S(2)}, u32[]{:S(2)}) %collective-permute-start.1) | collective-permute-done | bytes 262176 | tf_op jit(solution)/shard_map/ppermute | solution.py:9
  17.1 1.2 multiply_reduce_fusion
  18.4 1.1 collective-permute-done.2
  19.6 1.5 collective-permute-start.3
  21.2 1.9 %collective-permute-done.3 = f32[128]{0:T(128)S(1)} collective-permute-done((f32[128]{0:T(128)S(1)}, f32[128]{0:T(128)S(1)}, u32[]{:S(2)}, u32[]{:S(2)}) %collective-permute-start.3) | collective-permute-done | bytes 544 | tf_op jit(solution)/shard_map/ppermute | solution.py:9
  23.7 1.7 reshape_reshape.12
  25.4 49.2 %all_to_all.10 = bf16[64,40,256]{2,1,0:T(8,128)(2,1)S(1)} all-to-all(bf16[64,40,256]{2,1,0:T(8,128)(2,1)} %reshape_reshape.12), channel_id=1, replica_groups=mesh['expert'=64,'tensor'=4] {'expert'}, dimensions={0} | all-to-all | bytes 2621440 | tf_op jit(solution)/shard_map/all_to_all | solution.py:48
  74.6 1.6 reshape_reshape.13
  76.2 5.5 %fusion.2 = bf16[640,2048]{1,0:T(8,128)(2,1)S(1)} fusion(bf16[640,1024]{1,0:T(8,128)(2,1)} %reshape_reshape.13, bf16[1,1024,2048]{2,1,0:T(8,128)(2,1)} %param.12), kind=kOutput, calls=%fused_computation.2 | convolution fusion | flops 2685665280 | bytes 8126464 | tf_op jit(solution)/shard_map/dot_general | solution.py:89
  81.9 3.0 %collective-permute-done.4 = bf16[2,160,2048]{2,1,0:T(8,128)(2,1)S(1)} collective-permute-done((bf16[2,160,2048]{2,1,0:T(8,128)(2,1)S(1)}, bf16[2,160,2048]{2,1,0:T(8,128)(2,1)S(1)}, u32[]{:S(2)}, u32[]{:S(2)}) %collective-permute-start.4) | collective-permute-done | bytes 1310752 | tf_op jit(solution)/shard_map/ppermute | solution.py:9
  86.1 16.2 %collective-permute-done.5 = bf16[160,2048]{1,0:T(8,128)(2,1)S(1)} collective-permute-done((bf16[160,2048]{1,0:T(8,128)(2,1)S(1)}, bf16[160,2048]{1,0:T(8,128)(2,1)S(1)}, u32[]{:S(2)}, u32[]{:S(2)}) %collective-permute-start.5) | collective-permute-done | bytes 655392 | tf_op jit(solution)/shard_map/ppermute | solution.py:9
  102.5 0.9 fusion.13
  104.2 8.4 %collective-permute-done.6 = bf16[160,1024]{1,0:T(8,128)(2,1)} collective-permute-done((bf16[160,1024]{1,0:T(8,128)(2,1)}, bf16[160,1024]{1,0:T(8,128)(2,1)}, u32[]{:S(2)}, u32[]{:S(2)}) %collective-permute-start.6) | collective-permute-done | bytes 327712 | tf_op jit(solution)/shard_map/ppermute | solution.py:9
  112.6 2.0 %maximum_select_fusion.2 = bf16[2,160,1024]{2,1,0:T(8,128)(2,1)} fusion(bf16[1,160,1024]{2,1,0:T(8,128)(2,1)} %bitcast.15, bf16[1,160,1024]{2,1,0:T(8,128)(2,1)S(1)} %fusion.29, pred[]{:T(512)S(6)} %eq.60), kind=kLoop, calls=%fused_computation.22 | loop fusion | flops 983040 | bytes 1310721 | tf_op jit(solution)/shard_map/jit(_where)/select_n | solution.py:35
  114.8 1.2 maximum_select_fusion.1
  116.0 1.1 collective-permute-done.7
  117.0 1.6 maximum_select_fusion
  118.6 1.5 fusion.7
  120.2 1.7 reshape_reshape.14
  121.8 6.2 %all-to-all-start.1 = ((bf16[64,40,256]{2,1,0:T(8,128)(2,1)}), bf16[64,40,256]{2,1,0:T(8,128)(2,1)S(1)}, u32[]{:S(2)}, u32[]{:S(2)}) async-start(bf16[64,40,256]{2,1,0:T(8,128)(2,1)} %reshape_reshape.14), calls=%async_computation.1 | async-start | bytes 2621440 | tf_op jit(solution)/shard_map/all_to_all | solution.py:48
  128.1 0.9 select_reduce_fusion
  129.0 35.1 %all-to-all-done.1 = bf16[64,40,256]{2,1,0:T(8,128)(2,1)S(1)} async-done(((bf16[64,40,256]{2,1,0:T(8,128)(2,1)}), bf16[64,40,256]{2,1,0:T(8,128)(2,1)S(1)}, u32[]{:S(2)}, u32[]{:S(2)}) %all-to-all-start.1) | async-done | bytes 1310752 | tf_op jit(solution)/shard_map/all_to_all | solution.py:48
  164.0 1.6 reshape_reshape.15
  165.7 3.1 %fusion.11 = bf16[128,1024]{1,0:T(8,128)(2,1)} fusion(f32[128,1024]{1,0:T(8,128)} %copy-done.1, f32[640,128]{1,0:T(8,128)} %select_reduce_fusion, bf16[640,1024]{1,0:T(8,128)(2,1)} %reshape_reshape.15), kind=kOutput, calls=%fused_computation.16 | convolution fusion | flops 1006895104 | bytes 2424832 | tf_op jit(solution)/shard_map/dot_general | solution.py:96
  (40 shorter events, 5.1 us)
Async XLA Ops:
  0.0 118.6 %copy-start = (bf16[1,1024,1024]{2,1,0:T(8,128)(2,1)S(1)}, bf16[1,1024,1024]{2,1,0:T(8,128)(2,1)}, u32[]{:S(2)}) copy-start(bf16[1,1024,1024]{2,1,0:T(8,128)(2,1)} %param.13) | copy-start | bytes 6291460
  2.9 1.4 copy-start.2
  2.9 2.4 %copy-start.3 = (s32[128,4]{0,1:T(4,128)S(1)}, s32[128,4]{0,1:T(4,128)}, u32[]{:S(2)}) copy-start(s32[128,4]{0,1:T(4,128)} %param.10) | copy-start | bytes 6148
  4.2 2.1 %collective-permute-start = (bf16[128,2,1024]{2,0,1:T(8,128)(2,1)S(1)}, bf16[128,2,1024]{2,0,1:T(8,128)(2,1)}, u32[]{:S(2)}, u32[]{:S(2)}) collective-permute-start(bf16[128,2,1024]{2,0,1:T(8,128)(2,1)S(1)} %bitcast.70), channel_id=1, source_target_pairs={{0,1},{1,0},{2,3},{3,2},{4,5},{5,4},{6,7},{7,6},{8,9},{9,8},{10,11... | collective-permute-start | bytes 1572872 | tf_op jit(solution)/shard_map/ppermute | solution.py:9
  8.4 14.7 %copy-start.4 = (f32[1024]{0:T(1024)S(1)}, f32[1024]{0:T(1024)}, u32[]{:S(2)}) copy-start(f32[1024]{0:T(1024)} %param.9) | copy-start | bytes 12292
  8.4 8.7 %collective-permute-start.1 = (bf16[128,1024]{1,0:T(8,128)(2,1)}, bf16[128,1024]{1,0:T(8,128)(2,1)}, u32[]{:S(2)}, u32[]{:S(2)}) collective-permute-start(bf16[128,1024]{1,0:T(8,128)(2,1)} %fusion.15), channel_id=1, source_target_pairs={{0,2},{1,3},{2,0},{3,1},{4,6},{5,7},{6,4},{7,5},{8,10},{9,11},{10,... | collective-permute-start | bytes 786440 | tf_op jit(solution)/shard_map/ppermute | solution.py:9
  18.3 4.8 %copy-start.1 = (f32[128,1024]{1,0:T(8,128)}, f32[128,1024]{1,0:T(8,128)S(1)}, u32[]{:S(2)}) copy-start(f32[128,1024]{1,0:T(8,128)S(1)} %get-tuple-element.6) | copy-start | bytes 1572868
  18.3 1.2 collective-permute-start.2
  19.6 3.6 %collective-permute-start.3 = (f32[128]{0:T(128)S(1)}, f32[128]{0:T(128)S(1)}, u32[]{:S(2)}, u32[]{:S(2)}) collective-permute-start(f32[128]{0:T(128)S(1)} %add.77), channel_id=1, source_target_pairs={{0,2},{1,3},{2,0},{3,1},{4,6},{5,7},{6,4},{7,5},{8,10},{9,11},{10,... | collective-permute-start | bytes 1544 | tf_op jit(solution)/shard_map/ppermute | solution.py:9
  81.8 3.1 %collective-permute-start.4 = (bf16[2,160,2048]{2,1,0:T(8,128)(2,1)S(1)}, bf16[2,160,2048]{2,1,0:T(8,128)(2,1)S(1)}, u32[]{:S(2)}, u32[]{:S(2)}) collective-permute-start(bf16[2,160,2048]{2,1,0:T(8,128)(2,1)S(1)} %dynamic-slice_bitcast_fusion), channel_id=1, source_target_pairs={{0,1},{1,0},{2,3},{3,2},{4,5},{5,4},{6,7},{7,6},{8,9},{9,8},{10,11... | collective-permute-start | bytes 3932168 | tf_op jit(solution)/shard_map/ppermute | solution.py:9
  85.5 16.9 %collective-permute-start.5 = (bf16[160,2048]{1,0:T(8,128)(2,1)S(1)}, bf16[160,2048]{1,0:T(8,128)(2,1)S(1)}, u32[]{:S(2)}, u32[]{:S(2)}) collective-permute-start(bf16[160,2048]{1,0:T(8,128)(2,1)S(1)} %fusion.12), channel_id=1, source_target_pairs={{0,2},{1,3},{2,0},{3,1},{4,6},{5,7},{6,4},{7,5},{8,10},{9,11},{10,... | collective-permute-start | bytes 1966088 | tf_op jit(solution)/shard_map/ppermute | solution.py:9
  103.4 9.2 %collective-permute-start.6 = (bf16[160,1024]{1,0:T(8,128)(2,1)}, bf16[160,1024]{1,0:T(8,128)(2,1)}, u32[]{:S(2)}, u32[]{:S(2)}) collective-permute-start(bf16[160,1024]{1,0:T(8,128)(2,1)} %fusion.13), channel_id=1, source_target_pairs={{0,2},{1,3},{2,0},{3,1},{4,6},{5,7},{6,4},{7,5},{8,10},{9,11},{10,... | collective-permute-start | bytes 983048 | tf_op jit(solution)/shard_map/ppermute | solution.py:9
  114.6 2.4 %collective-permute-start.7 = (bf16[2,160,1024]{2,1,0:T(8,128)(2,1)}, bf16[2,160,1024]{2,1,0:T(8,128)(2,1)}, u32[]{:S(2)}, u32[]{:S(2)}) collective-permute-start(bf16[2,160,1024]{2,1,0:T(8,128)(2,1)} %maximum_select_fusion.2), channel_id=1, source_target_pairs={{0,1},{1,0},{2,3},{3,2},{4,5},{5,4},{6,7},{7,6},{8,9},{9,8},{10,11... | collective-permute-start | bytes 1966088 | tf_op jit(solution)/shard_map/ppermute | solution.py:9
  121.8 6.2 %copy-start.5 = (f32[128,4]{0,1:T(4,128)S(1)}, f32[128,4]{0,1:T(4,128)}, u32[]{:S(2)}) copy-start(f32[128,4]{0,1:T(4,128)} %param.11) | copy-start | bytes 6148
  121.8 42.2 %all-to-all-start.1 = ((bf16[64,40,256]{2,1,0:T(8,128)(2,1)}), bf16[64,40,256]{2,1,0:T(8,128)(2,1)S(1)}, u32[]{:S(2)}, u32[]{:S(2)}) async-start(bf16[64,40,256]{2,1,0:T(8,128)(2,1)} %reshape_reshape.14), calls=%async_computation.1 | async-start | bytes 2621440 | tf_op jit(solution)/shard_map/all_to_all | solution.py:48

commit v4 on v3

--- a/solution.py
+++ b/solution.py
@@ -13,17 +13,22 @@
     return lax.dynamic_index_in_dim(value, index, axis=axis, keepdims=False)
 
 
+def _slab(value, start, size, axis):
+    return lax.dynamic_slice_in_dim(value, start, size, axis=axis)
+
+
 def _reduce_scatter(value, axis):
     t = lax.axis_index("tensor")
     core = t % 2
     high = t // 2
-    shape = value.shape
-    split = value.reshape(shape[:axis] + (2, 2, shape[axis] // 4) + shape[axis + 1:])
-    sent = _pick(split, axis + 1, 1 - core).astype(jnp.bfloat16)
-    kept = _pick(split, axis + 1, core).astype(jnp.float32)
-    half = kept + _exchange(sent, 1).astype(jnp.float32)
-    sent = _pick(half, axis, 1 - high).astype(jnp.bfloat16)
-    kept = _pick(half, axis, high)
+    n = value.shape[axis] // 4
+    sent = jnp.concatenate(
+        [_slab(value, (1 - core) * n, n, axis), _slab(value, (3 - core) * n, n, axis)], axis
+    ).astype(jnp.bfloat16)
+    kept = jnp.concatenate([_slab(value, core * n, n, axis), _slab(value, (2 + core) * n, n, axis)], axis)
+    half = kept.astype(jnp.float32) + _exchange(sent, 1).astype(jnp.float32)
+    sent = _slab(half, (1 - high) * n, n, axis).astype(jnp.bfloat16)
+    kept = _slab(half, high * n, n, axis)
     return kept + _exchange(sent, 2).astype(jnp.float32)
 
 
@@ -31,12 +36,19 @@
     t = lax.axis_index("tensor")
     core = t % 2
     high = t // 2
-    other = _exchange(value, 2)
-    pair = jnp.where(high == 0, jnp.stack([value, other], axis), jnp.stack([other, value], axis))
+    n = value.shape[axis]
+    shape = list(value.shape)
+    shape[axis] = 2 * n
+    pair = jnp.zeros(shape, value.dtype)
+    pair = lax.dynamic_update_slice_in_dim(pair, value, high * n, axis)
+    pair = lax.dynamic_update_slice_in_dim(pair, _exchange(value, 2), (1 - high) * n, axis)
     other = _exchange(pair, 1)
-    quad = jnp.where(core == 0, jnp.stack([pair, other], axis + 1), jnp.stack([other, pair], axis + 1))
-    shape = quad.shape
-    return quad.reshape(shape[:axis] + (shape[axis] * shape[axis + 1] * shape[axis + 2],) + shape[axis + 3:])
+    shape[axis] = 4 * n
+    full = jnp.zeros(shape, value.dtype)
+    for part, side in ((pair, core), (other, 1 - core)):
+        for a in range(2):
+            full = lax.dynamic_update_slice_in_dim(full, _slab(part, a * n, n, axis), (2 * a + side) * n, axis)
+    return full
 
 
 def _exchange_rows(value):

time: 169 us -> 169 us (level)
  blocking collectives: 49.2 us -> 0 us
  waiting for transfers between devices: 72.8 us -> 110 us
  starting transfers between devices: 10.8 us -> 25.3 us
  other arithmetic: 11.6 us -> 9.48 us
    all_to_all x1 -> x0, blocking collectives: 49.2 us -> none  [_exchange_rows(): lax.all_to_all(packed, 'expert', split_axis=0, concat_axis=0, tiled=True)]
    all_to_all x1 -> x2, waiting for transfers between devices: 35.1 us -> 70 us  [_exchange_rows(): lax.all_to_all(packed, 'expert', split_axis=0, concat_axis=0, tiled=True)]
    all_to_all x1 -> x2, starting transfers between devices: 6.23 us -> 20.5 us  [_exchange_rows(): lax.all_to_all(packed, 'expert', split_axis=0, concat_axis=0, tiled=True)]
    select_n x3 -> x0, other arithmetic: 4.74 us -> none  [the longest x2 3.18 us: _all_gather(): jnp.where(high == 0, jnp.stack([value, other], axis), jnp.stack([other, v...]
    ppermute x8, waiting for transfers between devices: 37.8 us -> 39.7 us  [_exchange(): return lax.ppermute(value, 'tensor', [(j, j ^ flip) for j in range(size)])]
  transfers between devices with their start and end apart: 9 -> 10, of which waited for: 9 -> 10; matrix products, arithmetic and copies ran while one was open for 3% -> 2% of each run, Pallas kernels for 0% -> 0%
where the time goes in v4:
time: 169 us
  waiting for transfers between devices  110 us (65%)
  starting transfers between devices  25.3 us (15%)
  local copies, waits for them, and re-layouts  13.2 us (8%)
  matrix products  10.7 us (6%)
  other arithmetic  9.48 us (6%)
    all_to_all x2, waiting for transfers between devices, _exchange_rows(): lax.all_to_all(packed, 'expert', split_axis=0, concat_axis=0, tiled=True)  70 us
    ppermute x8, waiting for transfers between devices, _exchange(): return lax.ppermute(value, 'tensor', [(j, j ^ flip) for j in range(size)])  39.7 us
    all_to_all x2, starting transfers between devices, _exchange_rows(): lax.all_to_all(packed, 'expert', split_axis=0, concat_axis=0, tiled=True)  20.5 us
    dot_general x1, matrix products, body(): jnp.dot(flat_rows, w_in[0], preferred_element_type=jnp.float32)  5.46 us
    ppermute x8, starting transfers between devices, _exchange(): return lax.ppermute(value, 'tensor', [(j, j ^ flip) for j in range(size)])  4.8 us
  transfers between devices with their start and end apart: 10, of which 10 were waited for; matrix products, arithmetic and copies ran while one was open for 2% of the time, Pallas kernels for 0%

profile of v4, /device:TPU:32, one launch (start us, length us, event | category | flops | bytes accessed | tf_op | source)
XLA Modules:
  0.0 168.6 jit_solution(12694439242531734587)
XLA Ops:
  0.0 2.1 %dynamic-slice_bitcast_fusion.3 = (bf16[128,1024]{1,0:T(8,128)(2,1)S(1)}, bf16[128,1024]{1,0:T(8,128)(2,1)}, bf16[128,1024]{1,0:T(8,128)(2,1)S(1)}, bf16[128,1024]{1,0:T(8,128)(2,1)S(1)}) fusion(bf16[1,128,4096]{2,1,0:T(8,128)(2,1)} %param.7, s32[]{:T(128)S(6)} %select_n.64, s32[]{:T(128)S(6)} %select_n.65, s32[]{:T(128)S(6)} %select_n.67, s32[]{:T(128)S(6)} %select_n.66), kind=kLoop, calls=%fused_computation.33 | loop fusion | bytes 2097168 | tf_op jit(solution)/shard_map/dynamic_slice | solution.py:17
  2.5 1.6 collective-permute-done
  4.2 0.8 copy-done.3
  5.0 1.2 convert_add_fusion.2
  6.2 0.7 dynamic-slice_convert_fusion.1
  6.9 1.5 collective-permute-start.1
  8.6 1.2 reduce-window.6
  10.4 5.3 %collective-permute-done.1 = bf16[128,1024]{1,0:T(8,128)(2,1)} collective-permute-done((bf16[128,1024]{1,0:T(8,128)(2,1)}, bf16[128,1024]{1,0:T(8,128)(2,1)}, u32[]{:S(2)}, u32[]{:S(2)}) %collective-permute-start.1) | collective-permute-done | bytes 262176 | tf_op jit(solution)/shard_map/ppermute | solution.py:9
  15.6 1.2 multiply_reduce_fusion
  16.9 1.1 collective-permute-done.2
  18.1 1.5 collective-permute-start.3
  19.7 1.9 %collective-permute-done.3 = f32[128]{0:T(128)S(1)} collective-permute-done((f32[128]{0:T(128)S(1)}, f32[128]{0:T(128)S(1)}, u32[]{:S(2)}, u32[]{:S(2)}) %collective-permute-start.3) | collective-permute-done | bytes 544 | tf_op jit(solution)/shard_map/ppermute | solution.py:9
  22.3 1.7 reshape_reshape.12
  23.9 14.2 %all-to-all-start = ((bf16[64,40,256]{2,1,0:T(8,128)(2,1)}), bf16[64,40,256]{2,1,0:T(8,128)(2,1)S(1)}, u32[]{:S(2)}, u32[]{:S(2)}) async-start(bf16[64,40,256]{2,1,0:T(8,128)(2,1)} %reshape_reshape.12), calls=%async_computation | async-start | bytes 2621440 | tf_op jit(solution)/shard_map/all_to_all | solution.py:60
  38.2 34.9 %all-to-all-done = bf16[64,40,256]{2,1,0:T(8,128)(2,1)S(1)} async-done(((bf16[64,40,256]{2,1,0:T(8,128)(2,1)}), bf16[64,40,256]{2,1,0:T(8,128)(2,1)S(1)}, u32[]{:S(2)}, u32[]{:S(2)}) %all-to-all-start) | async-done | bytes 1310752 | tf_op jit(solution)/shard_map/all_to_all | solution.py:60
  73.1 1.6 reshape_reshape.13
  74.7 5.5 %fusion.2 = bf16[640,2048]{1,0:T(8,128)(2,1)S(1)} fusion(bf16[640,1024]{1,0:T(8,128)(2,1)} %reshape_reshape.13, bf16[1,1024,2048]{2,1,0:T(8,128)(2,1)} %param.12), kind=kOutput, calls=%fused_computation.2 | convolution fusion | flops 2685665280 | bytes 8126464 | tf_op jit(solution)/shard_map/dot_general | solution.py:101
  80.5 1.1 pad_maximum_fusion
  81.6 3.4 %collective-permute-done.4 = bf16[320,2048]{1,0:T(8,128)(2,1)} collective-permute-done((bf16[320,2048]{1,0:T(8,128)(2,1)}, bf16[320,2048]{1,0:T(8,128)(2,1)}, u32[]{:S(2)}, u32[]{:S(2)}) %collective-permute-start.4) | collective-permute-done | bytes 1310752 | tf_op jit(solution)/shard_map/ppermute | solution.py:9
  85.0 1.8 %convert_add_fusion = f32[320,2048]{1,0:T(8,128)S(1)} fusion(bf16[320,2048]{1,0:T(8,128)(2,1)} %collective-permute-done.4, bf16[160,2048]{1,0:T(8,128)(2,1)S(1)} %get-tuple-element.12, bf16[160,2048]{1,0:T(8,128)(2,1)S(1)} %get-tuple-element.9), kind=kLoop, calls=%fused_computation.3 | loop fusion | flops 3932160 | bytes 5242880 | tf_op jit(solution)/shard_map/add | solution.py:29
  86.8 1.5 copy-done.1
  89.0 16.2 %collective-permute-done.5 = bf16[160,2048]{1,0:T(8,128)(2,1)S(1)} collective-permute-done((bf16[160,2048]{1,0:T(8,128)(2,1)S(1)}, bf16[160,2048]{1,0:T(8,128)(2,1)S(1)}, u32[]{:S(2)}, u32[]{:S(2)}) %collective-permute-start.5) | collective-permute-done | bytes 655392 | tf_op jit(solution)/shard_map/ppermute | solution.py:9
  105.2 1.5 convert_add_fusion.1
  107.6 8.3 %collective-permute-done.6 = bf16[160,1024]{1,0:T(8,128)(2,1)S(1)} collective-permute-done((bf16[160,1024]{1,0:T(8,128)(2,1)S(1)}, bf16[160,1024]{1,0:T(8,128)(2,1)S(1)}, u32[]{:S(2)}, u32[]{:S(2)}) %collective-permute-start.6) | collective-permute-done | bytes 327712 | tf_op jit(solution)/shard_map/ppermute | solution.py:9
  116.5 1.8 %collective-permute-done.7 = bf16[320,1024]{1,0:T(8,128)(2,1)S(1)} collective-permute-done((bf16[320,1024]{1,0:T(8,128)(2,1)S(1)}, bf16[320,1024]{1,0:T(8,128)(2,1)S(1)}, u32[]{:S(2)}, u32[]{:S(2)}) %collective-permute-start.7) | collective-permute-done | bytes 655392 | tf_op jit(solution)/shard_map/ppermute | solution.py:9
  118.4 1.5 fusion.7
  120.0 1.7 reshape_reshape.14
  121.6 6.2 %all-to-all-start.1 = ((bf16[64,40,256]{2,1,0:T(8,128)(2,1)}), bf16[64,40,256]{2,1,0:T(8,128)(2,1)S(1)}, u32[]{:S(2)}, u32[]{:S(2)}) async-start(bf16[64,40,256]{2,1,0:T(8,128)(2,1)} %reshape_reshape.14), calls=%async_computation.1 | async-start | bytes 2621440 | tf_op jit(solution)/shard_map/all_to_all | solution.py:60
  127.9 0.9 select_reduce_fusion
  128.8 35.1 %all-to-all-done.1 = bf16[64,40,256]{2,1,0:T(8,128)(2,1)S(1)} async-done(((bf16[64,40,256]{2,1,0:T(8,128)(2,1)}), bf16[64,40,256]{2,1,0:T(8,128)(2,1)S(1)}, u32[]{:S(2)}, u32[]{:S(2)}) %all-to-all-start.1) | async-done | bytes 1310752 | tf_op jit(solution)/shard_map/all_to_all | solution.py:60
  163.8 1.6 reshape_reshape.15
  165.5 3.1 %fusion.11 = bf16[128,1024]{1,0:T(8,128)(2,1)} fusion(f32[128,1024]{1,0:T(8,128)} %copy-done.2, f32[640,128]{1,0:T(8,128)} %select_reduce_fusion, bf16[640,1024]{1,0:T(8,128)(2,1)} %reshape_reshape.15), kind=kOutput, calls=%fused_computation.15 | convolution fusion | flops 1006895104 | bytes 2424832 | tf_op jit(solution)/shard_map/dot_general | solution.py:108
  (44 shorter events, 4.4 us)
Async XLA Ops:
  0.0 118.4 %copy-start = (bf16[1,1024,1024]{2,1,0:T(8,128)(2,1)S(1)}, bf16[1,1024,1024]{2,1,0:T(8,128)(2,1)}, u32[]{:S(2)}) copy-start(bf16[1,1024,1024]{2,1,0:T(8,128)(2,1)} %param.13) | copy-start | bytes 6291460
  0.0 2.3 %copy-start.4 = (s32[128,4]{0,1:T(4,128)S(1)}, s32[128,4]{0,1:T(4,128)}, u32[]{:S(2)}) copy-start(s32[128,4]{0,1:T(4,128)} %param.10) | copy-start | bytes 6148
  2.2 2.0 %collective-permute-start = (bf16[128,2048]{1,0:T(8,128)(2,1)S(1)}, bf16[128,2048]{1,0:T(8,128)(2,1)S(1)}, u32[]{:S(2)}, u32[]{:S(2)}) collective-permute-start(bf16[128,2048]{1,0:T(8,128)(2,1)S(1)} %pad_maximum_fusion.1), channel_id=1, source_target_pairs={{0,1},{1,0},{2,3},{3,2},{4,5},{5,4},{6,7},{7,6},{8,9},{9,8},{10,11... | collective-permute-start | bytes 1572872 | tf_op jit(solution)/shard_map/ppermute | solution.py:9
  4.2 0.8 copy-start.3
  6.9 14.7 %copy-start.5 = (f32[1024]{0:T(1024)S(1)}, f32[1024]{0:T(1024)}, u32[]{:S(2)}) copy-start(f32[1024]{0:T(1024)} %param.9) | copy-start | bytes 12292
  6.9 8.7 %collective-permute-start.1 = (bf16[128,1024]{1,0:T(8,128)(2,1)}, bf16[128,1024]{1,0:T(8,128)(2,1)}, u32[]{:S(2)}, u32[]{:S(2)}) collective-permute-start(bf16[128,1024]{1,0:T(8,128)(2,1)} %dynamic-slice_convert_fusion.1), channel_id=1, source_target_pairs={{0,2},{1,3},{2,0},{3,1},{4,6},{5,7},{6,4},{7,5},{8,10},{9,11},{10,... | collective-permute-start | bytes 786440 | tf_op jit(solution)/shard_map/ppermute | solution.py:9
  16.8 4.8 %copy-start.2 = (f32[128,1024]{1,0:T(8,128)}, f32[128,1024]{1,0:T(8,128)S(1)}, u32[]{:S(2)}) copy-start(f32[128,1024]{1,0:T(8,128)S(1)} %get-tuple-element.8) | copy-start | bytes 1572868
  16.8 1.2 collective-permute-start.2
  18.1 3.6 %collective-permute-start.3 = (f32[128]{0:T(128)S(1)}, f32[128]{0:T(128)S(1)}, u32[]{:S(2)}, u32[]{:S(2)}) collective-permute-start(f32[128]{0:T(128)S(1)} %add.107), channel_id=1, source_target_pairs={{0,2},{1,3},{2,0},{3,1},{4,6},{5,7},{6,4},{7,5},{8,10},{9,11},{10,... | collective-permute-start | bytes 1544 | tf_op jit(solution)/shard_map/ppermute | solution.py:9
  23.9 49.2 %all-to-all-start = ((bf16[64,40,256]{2,1,0:T(8,128)(2,1)}), bf16[64,40,256]{2,1,0:T(8,128)(2,1)S(1)}, u32[]{:S(2)}, u32[]{:S(2)}) async-start(bf16[64,40,256]{2,1,0:T(8,128)(2,1)} %reshape_reshape.12), calls=%async_computation | async-start | bytes 2621440 | tf_op jit(solution)/shard_map/all_to_all | solution.py:60
  81.6 3.4 %collective-permute-start.4 = (bf16[320,2048]{1,0:T(8,128)(2,1)}, bf16[320,2048]{1,0:T(8,128)(2,1)}, u32[]{:S(2)}, u32[]{:S(2)}) collective-permute-start(bf16[320,2048]{1,0:T(8,128)(2,1)} %pad_maximum_fusion), channel_id=1, source_target_pairs={{0,1},{1,0},{2,3},{3,2},{4,5},{5,4},{6,7},{7,6},{8,9},{9,8},{10,11... | collective-permute-start | bytes 3932168 | tf_op jit(solution)/shard_map/ppermute | solution.py:9
  86.8 1.5 copy-start.1
  88.3 16.9 %collective-permute-start.5 = (bf16[160,2048]{1,0:T(8,128)(2,1)S(1)}, bf16[160,2048]{1,0:T(8,128)(2,1)S(1)}, u32[]{:S(2)}, u32[]{:S(2)}) collective-permute-start(bf16[160,2048]{1,0:T(8,128)(2,1)S(1)} %dynamic-slice_convert_fusion), channel_id=1, source_target_pairs={{0,2},{1,3},{2,0},{3,1},{4,6},{5,7},{6,4},{7,5},{8,10},{9,11},{10,... | collective-permute-start | bytes 1966088 | tf_op jit(solution)/shard_map/ppermute | solution.py:9
  107.0 9.0 %collective-permute-start.6 = (bf16[160,1024]{1,0:T(8,128)(2,1)S(1)}, bf16[160,1024]{1,0:T(8,128)(2,1)S(1)}, u32[]{:S(2)}, u32[]{:S(2)}) collective-permute-start(bf16[160,1024]{1,0:T(8,128)(2,1)S(1)} %get-tuple-element.6), channel_id=1, source_target_pairs={{0,2},{1,3},{2,0},{3,1},{4,6},{5,7},{6,4},{7,5},{8,10},{9,11},{10,... | collective-permute-start | bytes 983048 | tf_op jit(solution)/shard_map/ppermute | solution.py:9
  116.0 2.4 %collective-permute-start.7 = (bf16[320,1024]{1,0:T(8,128)(2,1)S(1)}, bf16[320,1024]{1,0:T(8,128)(2,1)S(1)}, u32[]{:S(2)}, u32[]{:S(2)}) collective-permute-start(bf16[320,1024]{1,0:T(8,128)(2,1)S(1)} %constant_dynamic-update-slice_fusion), channel_id=1, source_target_pairs={{0,1},{1,0},{2,3},{3,2},{4,5},{5,4},{6,7},{7,6},{8,9},{9,8},{10,11... | collective-permute-start | bytes 1966088 | tf_op jit(solution)/shard_map/ppermute | solution.py:9
  121.6 6.2 %copy-start.6 = (f32[128,4]{0,1:T(4,128)S(1)}, f32[128,4]{0,1:T(4,128)}, u32[]{:S(2)}) copy-start(f32[128,4]{0,1:T(4,128)} %param.11) | copy-start | bytes 6148
  121.6 42.2 %all-to-all-start.1 = ((bf16[64,40,256]{2,1,0:T(8,128)(2,1)}), bf16[64,40,256]{2,1,0:T(8,128)(2,1)S(1)}, u32[]{:S(2)}, u32[]{:S(2)}) async-start(bf16[64,40,256]{2,1,0:T(8,128)(2,1)} %reshape_reshape.14), calls=%async_computation.1 | async-start | bytes 2621440 | tf_op jit(solution)/shard_map/all_to_all | solution.py:60

commit v5 on v4

--- a/solution.py
+++ b/solution.py
@@ -98,17 +98,30 @@
     item_count = in_rows.shape[1]
     row_total = source_count * item_count
     flat_rows = in_rows.reshape(row_total, feature_local)
-    partial_value = jnp.dot(flat_rows, w_in[0], preferred_element_type=jnp.float32)
-    total = _reduce_scatter(partial_value.astype(jnp.bfloat16), 0)
+    t = lax.axis_index("tensor")
+    core = t % 2
+    high = t // 2
+    block = row_total // 4
+    away = jnp.concatenate(
+        [_slab(flat_rows, (1 - core) * block, block, 0), _slab(flat_rows, (3 - core) * block, block, 0)], 0
+    )
+    home = jnp.concatenate([_slab(flat_rows, core * block, block, 0), _slab(flat_rows, (2 + core) * block, block, 0)], 0)
+    sent = jnp.dot(away, w_in[0], preferred_element_type=jnp.float32).astype(jnp.bfloat16)
+    received = _exchange(sent, 1)
+    kept = jnp.dot(home, w_in[0], preferred_element_type=jnp.float32).astype(jnp.bfloat16)
+    half = kept.astype(jnp.float32) + received.astype(jnp.float32)
+    sent = _slab(half, (1 - high) * block, block, 0).astype(jnp.bfloat16)
+    total = _slab(half, high * block, block, 0) + _exchange(sent, 2).astype(jnp.float32)
     hidden = (jax.nn.silu(total[:, :hidden_width]) * total[:, hidden_width:]).astype(jnp.bfloat16)
     hidden = _all_gather(hidden, 0)
     produced = jnp.dot(hidden, w_down[0], preferred_element_type=jnp.float32).astype(jnp.bfloat16)
     results = produced.reshape(source_count, item_count, feature_local)
     returned = _exchange_rows(results)
-    routed = jnp.dot(
-        weights_table,
-        returned.reshape(expert_count * capacity, feature_local).astype(jnp.float32),
-        precision=lax.Precision.HIGHEST,
+    flat_returned = returned.reshape(expert_count * capacity, feature_local)
+    weights_high = weights_table.astype(jnp.bfloat16)
+    weights_low = (weights_table - weights_high.astype(jnp.float32)).astype(jnp.bfloat16)
+    routed = jnp.dot(weights_high, flat_returned, preferred_element_type=jnp.float32) + jnp.dot(
+        weights_low, flat_returned, preferred_element_type=jnp.float32
     )
     return (stream + routed).astype(jnp.bfloat16)
 

time: 169 us -> 171 us (1.012)
  other arithmetic: 9.48 us -> 6.57 us
  matrix products: 10.7 us -> 13.6 us
  local copies, waits for them, and re-layouts: 13.2 us -> 15.1 us
    dot_general x2 -> x4, matrix products: 8.54 us -> 11.5 us  [the longest x1 4.79 us: body(): jnp.dot(away, w_in[0], preferred_element_type=jnp.float32)]
    add x2 -> x1, other arithmetic: 3 us -> 1.23 us  [_reduce_scatter(): half = kept.astype(jnp.float32) + _exchange(sent, 1).astype(jnp.float32)]
where the time goes in v5:
time: 171 us
  waiting for transfers between devices  110 us (64%)
  starting transfers between devices  25.4 us (15%)
  local copies, waits for them, and re-layouts  15.1 us (9%)
  matrix products  13.6 us (8%)
  other arithmetic  6.57 us (4%)
    all_to_all x2, waiting for transfers between devices, _exchange_rows(): lax.all_to_all(packed, 'expert', split_axis=0, concat_axis=0, tiled=True)  69.9 us
    ppermute x8, waiting for transfers between devices, _exchange(): return lax.ppermute(value, 'tensor', [(j, j ^ flip) for j in range(size)])  39.7 us
    all_to_all x2, starting transfers between devices, _exchange_rows(): lax.all_to_all(packed, 'expert', split_axis=0, concat_axis=0, tiled=True)  20.6 us
    ppermute x8, starting transfers between devices, _exchange(): return lax.ppermute(value, 'tensor', [(j, j ^ flip) for j in range(size)])  4.8 us
    dot_general x1, matrix products, body(): jnp.dot(away, w_in[0], preferred_element_type=jnp.float32)  4.79 us
    dot_general x1, matrix products, body(): jnp.dot(home, w_in[0], preferred_element_type=jnp.float32)  4.1 us
    dynamic_slice x2, local copies, waits for them, and re-layouts, _slab(): return lax.dynamic_slice_in_dim(value, start, size, axis=axis)  3.48 us
  transfers between devices with their start and end apart: 10, of which 10 were waited for; matrix products, arithmetic and copies ran while one was open for 2% of the time, Pallas kernels for 0%

profile of v5, /device:TPU:32, one launch (start us, length us, event | category | flops | bytes accessed | tf_op | source)
XLA Modules:
  0.0 170.6 jit_solution(17548605711197065061)
XLA Ops:
  0.0 2.1 %dynamic-slice_bitcast_fusion.3 = (bf16[128,1024]{1,0:T(8,128)(2,1)S(1)}, bf16[128,1024]{1,0:T(8,128)(2,1)}, bf16[128,1024]{1,0:T(8,128)(2,1)S(1)}, bf16[128,1024]{1,0:T(8,128)(2,1)S(1)}) fusion(bf16[1,128,4096]{2,1,0:T(8,128)(2,1)} %param.7, s32[]{:T(128)S(6)} %select_n.64, s32[]{:T(128)S(6)} %select_n.65, s32[]{:T(128)S(6)} %select_n.67, s32[]{:T(128)S(6)} %select_n.66), kind=kLoop, calls=%fused_computation.46 | loop fusion | bytes 2097168 | tf_op jit(solution)/shard_map/dynamic_slice | solution.py:17
  2.5 1.6 collective-permute-done
  4.2 0.8 copy-done.5
  5.0 1.2 convert_add_fusion.2
  7.0 1.5 collective-permute-start.1
  8.6 1.2 reduce-window.6
  10.4 5.3 %collective-permute-done.1 = bf16[128,1024]{1,0:T(8,128)(2,1)} collective-permute-done((bf16[128,1024]{1,0:T(8,128)(2,1)}, bf16[128,1024]{1,0:T(8,128)(2,1)}, u32[]{:S(2)}, u32[]{:S(2)}) %collective-permute-start.1) | collective-permute-done | bytes 262176 | tf_op jit(solution)/shard_map/ppermute | solution.py:9
  15.6 1.2 multiply_reduce_fusion
  16.9 1.1 collective-permute-done.2
  18.1 1.5 collective-permute-start.3
  19.7 1.9 %collective-permute-done.3 = f32[128]{0:T(128)S(1)} collective-permute-done((f32[128]{0:T(128)S(1)}, f32[128]{0:T(128)S(1)}, u32[]{:S(2)}, u32[]{:S(2)}) %collective-permute-start.3) | collective-permute-done | bytes 544 | tf_op jit(solution)/shard_map/ppermute | solution.py:9
  22.3 1.6 reshape_reshape.12
  23.9 14.2 %all-to-all-start = ((bf16[64,40,256]{2,1,0:T(8,128)(2,1)}), bf16[64,40,256]{2,1,0:T(8,128)(2,1)S(1)}, u32[]{:S(2)}, u32[]{:S(2)}) async-start(bf16[64,40,256]{2,1,0:T(8,128)(2,1)} %reshape_reshape.12), calls=%async_computation | async-start | bytes 2621440 | tf_op jit(solution)/shard_map/all_to_all | solution.py:60
  38.2 34.9 %all-to-all-done = bf16[64,40,256]{2,1,0:T(8,128)(2,1)S(1)} async-done(((bf16[64,40,256]{2,1,0:T(8,128)(2,1)}), bf16[64,40,256]{2,1,0:T(8,128)(2,1)S(1)}, u32[]{:S(2)}, u32[]{:S(2)}) %all-to-all-start) | async-done | bytes 1310752 | tf_op jit(solution)/shard_map/all_to_all | solution.py:60
  73.1 1.6 reshape_reshape.13
  74.7 1.4 constant_dynamic-slice_fusion.3
  76.1 4.8 %fusion.10 = bf16[320,2048]{1,0:T(8,128)(2,1)} fusion(bf16[1,1024,2048]{2,1,0:T(8,128)(2,1)} %param.12, bf16[160,1024]{1,0:T(8,128)(2,1)S(1)} %get-tuple-element.10, bf16[160,1024]{1,0:T(8,128)(2,1)S(1)} %get-tuple-element.11), kind=kOutput, calls=%fused_computation.6 | convolution fusion | flops 1344143360 | bytes 6160384 | tf_op jit(solution)/shard_map/dot_general | solution.py:109
  80.9 3.4 %collective-permute-done.4 = bf16[320,2048]{1,0:T(8,128)(2,1)} collective-permute-done((bf16[320,2048]{1,0:T(8,128)(2,1)}, bf16[320,2048]{1,0:T(8,128)(2,1)}, u32[]{:S(2)}, u32[]{:S(2)}) %collective-permute-start.4) | collective-permute-done | bytes 1310752 | tf_op jit(solution)/shard_map/ppermute | solution.py:9
  84.2 4.1 %convert_add_fusion = f32[320,2048]{1,0:T(8,128)S(1)} fusion(bf16[320,2048]{1,0:T(8,128)(2,1)} %collective-permute-done.4, bf16[1,1024,2048]{2,1,0:T(8,128)(2,1)} %param.12, bf16[160,1024]{1,0:T(8,128)(2,1)S(1)} %get-tuple-element.12, bf16[160,1024]{1,0:T(8,128)(2,1)S(1)} %get-tuple-element.9), kind=kOutput, calls=%fused_computation.7 | convolution fusion | flops 1346109440 | bytes 8781824 | tf_op jit(solution)/shard_map/dot_general | solution.py:111
  88.4 1.5 copy-done.4
  90.6 16.2 %collective-permute-done.5 = bf16[160,2048]{1,0:T(8,128)(2,1)S(1)} collective-permute-done((bf16[160,2048]{1,0:T(8,128)(2,1)S(1)}, bf16[160,2048]{1,0:T(8,128)(2,1)S(1)}, u32[]{:S(2)}, u32[]{:S(2)}) %collective-permute-start.5) | collective-permute-done | bytes 655392 | tf_op jit(solution)/shard_map/ppermute | solution.py:9
  106.8 1.5 convert_add_fusion.1
  109.2 8.3 %collective-permute-done.6 = bf16[160,1024]{1,0:T(8,128)(2,1)S(1)} collective-permute-done((bf16[160,1024]{1,0:T(8,128)(2,1)S(1)}, bf16[160,1024]{1,0:T(8,128)(2,1)S(1)}, u32[]{:S(2)}, u32[]{:S(2)}) %collective-permute-start.6) | collective-permute-done | bytes 327712 | tf_op jit(solution)/shard_map/ppermute | solution.py:9
  118.1 1.8 %collective-permute-done.7 = bf16[320,1024]{1,0:T(8,128)(2,1)S(1)} collective-permute-done((bf16[320,1024]{1,0:T(8,128)(2,1)S(1)}, bf16[320,1024]{1,0:T(8,128)(2,1)S(1)}, u32[]{:S(2)}, u32[]{:S(2)}) %collective-permute-start.7) | collective-permute-done | bytes 655392 | tf_op jit(solution)/shard_map/ppermute | solution.py:9
  120.0 1.5 fusion.15
  121.6 1.6 reshape_reshape.14
  123.2 6.4 %all-to-all-start.1 = ((bf16[64,40,256]{2,1,0:T(8,128)(2,1)}), bf16[64,40,256]{2,1,0:T(8,128)(2,1)}, u32[]{:S(2)}, u32[]{:S(2)}) async-start(bf16[64,40,256]{2,1,0:T(8,128)(2,1)} %reshape_reshape.14), calls=%async_computation.1 | async-start | bytes 2621440 | tf_op jit(solution)/shard_map/all_to_all | solution.py:60
  129.6 0.9 select_reduce_fusion
  130.5 35.0 %all-to-all-done.1 = bf16[64,40,256]{2,1,0:T(8,128)(2,1)} async-done(((bf16[64,40,256]{2,1,0:T(8,128)(2,1)}), bf16[64,40,256]{2,1,0:T(8,128)(2,1)}, u32[]{:S(2)}, u32[]{:S(2)}) %all-to-all-start.1) | async-done | bytes 1310752 | tf_op jit(solution)/shard_map/all_to_all | solution.py:60
  165.5 2.5 %reshape_reshape.15 = bf16[640,1024]{1,0:T(8,128)(2,1)S(1)} reshape(bf16[64,40,256]{2,1,0:T(8,128)(2,1)} %all-to-all-done.1) | data formatting | bytes 2621440 | tf_op jit(solution)/shard_map/reshape;reshape | solution.py:120
  168.0 1.4 fusion.45
  169.5 1.1 fusion.20
  (48 shorter events, 4.9 us)
Async XLA Ops:
  0.0 120.0 %copy-start = (bf16[1,1024,1024]{2,1,0:T(8,128)(2,1)S(1)}, bf16[1,1024,1024]{2,1,0:T(8,128)(2,1)}, u32[]{:S(2)}) copy-start(bf16[1,1024,1024]{2,1,0:T(8,128)(2,1)} %param.13) | copy-start | bytes 6291460
  0.0 2.3 %copy-start.6 = (s32[128,4]{0,1:T(4,128)S(1)}, s32[128,4]{0,1:T(4,128)}, u32[]{:S(2)}) copy-start(s32[128,4]{0,1:T(4,128)} %param.10) | copy-start | bytes 6148
  2.2 2.0 %collective-permute-start = (bf16[128,2048]{1,0:T(8,128)(2,1)S(1)}, bf16[128,2048]{1,0:T(8,128)(2,1)S(1)}, u32[]{:S(2)}, u32[]{:S(2)}) collective-permute-start(bf16[128,2048]{1,0:T(8,128)(2,1)S(1)} %pad_maximum_fusion), channel_id=1, source_target_pairs={{0,1},{1,0},{2,3},{3,2},{4,5},{5,4},{6,7},{7,6},{8,9},{9,8},{10,11... | collective-permute-start | bytes 1572872 | tf_op jit(solution)/shard_map/ppermute | solution.py:9
  4.2 0.8 copy-start.5
  7.0 14.7 %copy-start.7 = (f32[1024]{0:T(1024)S(1)}, f32[1024]{0:T(1024)}, u32[]{:S(2)}) copy-start(f32[1024]{0:T(1024)} %param.9) | copy-start | bytes 12292
  7.0 8.7 %collective-permute-start.1 = (bf16[128,1024]{1,0:T(8,128)(2,1)}, bf16[128,1024]{1,0:T(8,128)(2,1)}, u32[]{:S(2)}, u32[]{:S(2)}) collective-permute-start(bf16[128,1024]{1,0:T(8,128)(2,1)} %dynamic-slice_convert_fusion.1), channel_id=1, source_target_pairs={{0,2},{1,3},{2,0},{3,1},{4,6},{5,7},{6,4},{7,5},{8,10},{9,11},{10,... | collective-permute-start | bytes 786440 | tf_op jit(solution)/shard_map/ppermute | solution.py:9
  16.8 4.8 %copy-start.1 = (f32[128,1024]{1,0:T(8,128)}, f32[128,1024]{1,0:T(8,128)S(1)}, u32[]{:S(2)}) copy-start(f32[128,1024]{1,0:T(8,128)S(1)} %get-tuple-element.8) | copy-start | bytes 1572868
  16.8 1.2 collective-permute-start.2
  18.1 3.6 %collective-permute-start.3 = (f32[128]{0:T(128)S(1)}, f32[128]{0:T(128)S(1)}, u32[]{:S(2)}, u32[]{:S(2)}) collective-permute-start(f32[128]{0:T(128)S(1)} %add.110), channel_id=1, source_target_pairs={{0,2},{1,3},{2,0},{3,1},{4,6},{5,7},{6,4},{7,5},{8,10},{9,11},{10,... | collective-permute-start | bytes 1544 | tf_op jit(solution)/shard_map/ppermute | solution.py:9
  23.9 49.2 %all-to-all-start = ((bf16[64,40,256]{2,1,0:T(8,128)(2,1)}), bf16[64,40,256]{2,1,0:T(8,128)(2,1)S(1)}, u32[]{:S(2)}, u32[]{:S(2)}) async-start(bf16[64,40,256]{2,1,0:T(8,128)(2,1)} %reshape_reshape.12), calls=%async_computation | async-start | bytes 2621440 | tf_op jit(solution)/shard_map/all_to_all | solution.py:60
  80.9 3.4 %collective-permute-start.4 = (bf16[320,2048]{1,0:T(8,128)(2,1)}, bf16[320,2048]{1,0:T(8,128)(2,1)}, u32[]{:S(2)}, u32[]{:S(2)}) collective-permute-start(bf16[320,2048]{1,0:T(8,128)(2,1)} %fusion.10), channel_id=1, source_target_pairs={{0,1},{1,0},{2,3},{3,2},{4,5},{5,4},{6,7},{7,6},{8,9},{9,8},{10,11... | collective-permute-start | bytes 3932168 | tf_op jit(solution)/shard_map/ppermute | solution.py:9
  88.3 1.5 copy-start.4
  89.9 16.9 %collective-permute-start.5 = (bf16[160,2048]{1,0:T(8,128)(2,1)S(1)}, bf16[160,2048]{1,0:T(8,128)(2,1)S(1)}, u32[]{:S(2)}, u32[]{:S(2)}) collective-permute-start(bf16[160,2048]{1,0:T(8,128)(2,1)S(1)} %dynamic-slice_convert_fusion), channel_id=1, source_target_pairs={{0,2},{1,3},{2,0},{3,1},{4,6},{5,7},{6,4},{7,5},{8,10},{9,11},{10,... | collective-permute-start | bytes 1966088 | tf_op jit(solution)/shard_map/ppermute | solution.py:9
  108.5 9.0 %collective-permute-start.6 = (bf16[160,1024]{1,0:T(8,128)(2,1)S(1)}, bf16[160,1024]{1,0:T(8,128)(2,1)S(1)}, u32[]{:S(2)}, u32[]{:S(2)}) collective-permute-start(bf16[160,1024]{1,0:T(8,128)(2,1)S(1)} %get-tuple-element.6), channel_id=1, source_target_pairs={{0,2},{1,3},{2,0},{3,1},{4,6},{5,7},{6,4},{7,5},{8,10},{9,11},{10,... | collective-permute-start | bytes 983048 | tf_op jit(solution)/shard_map/ppermute | solution.py:9
  117.6 2.4 %collective-permute-start.7 = (bf16[320,1024]{1,0:T(8,128)(2,1)S(1)}, bf16[320,1024]{1,0:T(8,128)(2,1)S(1)}, u32[]{:S(2)}, u32[]{:S(2)}) collective-permute-start(bf16[320,1024]{1,0:T(8,128)(2,1)S(1)} %constant_dynamic-update-slice_fusion), channel_id=1, source_target_pairs={{0,1},{1,0},{2,3},{3,2},{4,5},{5,4},{6,7},{7,6},{8,9},{9,8},{10,11... | collective-permute-start | bytes 1966088 | tf_op jit(solution)/shard_map/ppermute | solution.py:9
  123.2 6.4 %copy-start.8 = (f32[128,4]{0,1:T(4,128)S(1)}, f32[128,4]{0,1:T(4,128)}, u32[]{:S(2)}) copy-start(f32[128,4]{0,1:T(4,128)} %param.11) | copy-start | bytes 6148
  123.2 42.3 %all-to-all-start.1 = ((bf16[64,40,256]{2,1,0:T(8,128)(2,1)}), bf16[64,40,256]{2,1,0:T(8,128)(2,1)}, u32[]{:S(2)}, u32[]{:S(2)}) async-start(bf16[64,40,256]{2,1,0:T(8,128)(2,1)} %reshape_reshape.14), calls=%async_computation.1 | async-start | bytes 2621440 | tf_op jit(solution)/shard_map/all_to_all | solution.py:60
  168.0 1.5 copy-start.2
  168.0 1.5 copy-start.3

commit v6 on v4

--- a/solution.py
+++ b/solution.py
@@ -25,30 +25,38 @@
     sent = jnp.concatenate(
         [_slab(value, (1 - core) * n, n, axis), _slab(value, (3 - core) * n, n, axis)], axis
     ).astype(jnp.bfloat16)
-    kept = jnp.concatenate([_slab(value, core * n, n, axis), _slab(value, (2 + core) * n, n, axis)], axis)
-    half = kept.astype(jnp.float32) + _exchange(sent, 1).astype(jnp.float32)
-    sent = _slab(half, (1 - high) * n, n, axis).astype(jnp.bfloat16)
-    kept = _slab(half, high * n, n, axis)
-    return kept + _exchange(sent, 2).astype(jnp.float32)
+    received = _exchange(sent, 1)
+    away = _slab(value, (3 - 2 * high + core - 1) * n, n, axis).astype(jnp.float32)
+    away = away + _slab(received, (1 - high) * n, n, axis).astype(jnp.float32)
+    home = _slab(value, (2 * high + core) * n, n, axis).astype(jnp.float32)
+    home = home + _slab(received, high * n, n, axis).astype(jnp.float32)
+    return home + _exchange(away.astype(jnp.bfloat16), 2).astype(jnp.float32)
 
 
-def _all_gather(value, axis):
+def _reduce_scatter_rows(value):
     t = lax.axis_index("tensor")
     core = t % 2
     high = t // 2
-    n = value.shape[axis]
-    shape = list(value.shape)
-    shape[axis] = 2 * n
-    pair = jnp.zeros(shape, value.dtype)
-    pair = lax.dynamic_update_slice_in_dim(pair, value, high * n, axis)
-    pair = lax.dynamic_update_slice_in_dim(pair, _exchange(value, 2), (1 - high) * n, axis)
-    other = _exchange(pair, 1)
-    shape[axis] = 4 * n
-    full = jnp.zeros(shape, value.dtype)
-    for part, side in ((pair, core), (other, 1 - core)):
-        for a in range(2):
-            full = lax.dynamic_update_slice_in_dim(full, _slab(part, a * n, n, axis), (2 * a + side) * n, axis)
-    return full
+    n = value.shape[0] // 4
+    received = _exchange(_slab(value, 2 * (1 - core) * n, 2 * n, 0).astype(jnp.bfloat16), 1)
+    away = _slab(value, (2 * core + 1 - high) * n, n, 0).astype(jnp.float32)
+    away = away + _slab(received, (1 - high) * n, n, 0).astype(jnp.float32)
+    home = _slab(value, (2 * core + high) * n, n, 0).astype(jnp.float32)
+    home = home + _slab(received, high * n, n, 0).astype(jnp.float32)
+    return home + _exchange(away.astype(jnp.bfloat16), 2).astype(jnp.float32)
+
+
+def _all_gather_rows(value):
+    t = lax.axis_index("tensor")
+    core = t % 2
+    high = t // 2
+    n = value.shape[0]
+    pair = jnp.zeros((2 * n,) + value.shape[1:], value.dtype)
+    pair = lax.dynamic_update_slice_in_dim(pair, value, high * n, 0)
+    pair = lax.dynamic_update_slice_in_dim(pair, _exchange(value, 2), (1 - high) * n, 0)
+    full = jnp.zeros((4 * n,) + value.shape[1:], value.dtype)
+    full = lax.dynamic_update_slice_in_dim(full, pair, 2 * core * n, 0)
+    return lax.dynamic_update_slice_in_dim(full, _exchange(pair, 1), 2 * (1 - core) * n, 0)
 
 
 def _exchange_rows(value):
@@ -99,9 +107,9 @@
     row_total = source_count * item_count
     flat_rows = in_rows.reshape(row_total, feature_local)
     partial_value = jnp.dot(flat_rows, w_in[0], preferred_element_type=jnp.float32)
-    total = _reduce_scatter(partial_value.astype(jnp.bfloat16), 0)
+    total = _reduce_scatter_rows(partial_value.astype(jnp.bfloat16))
     hidden = (jax.nn.silu(total[:, :hidden_width]) * total[:, hidden_width:]).astype(jnp.bfloat16)
-    hidden = _all_gather(hidden, 0)
+    hidden = _all_gather_rows(hidden)
     produced = jnp.dot(hidden, w_down[0], preferred_element_type=jnp.float32).astype(jnp.bfloat16)
     results = produced.reshape(source_count, item_count, feature_local)
     returned = _exchange_rows(results)

time: 169 us -> 168 us (level)
  local copies, waits for them, and re-layouts: 13.2 us -> 10.8 us
    convert_element_type x0 -> x2, other arithmetic: none -> 3.84 us  [the longest x1 2.12 us: _reduce_scatter_rows(): return home + _exchange(away.astype(jnp.bfloat16), 2).astype(jnp.float32)]
    add x3 -> x1, other arithmetic: 4.45 us -> 1.58 us  [_reduce_scatter_rows(): return home + _exchange(away.astype(jnp.bfloat16), 2).astype(jnp.float32)]
    unnamed x15, local copies, waits for them, and re-layouts: 2.43 us -> 0.67 us
where the time goes in v6:
time: 168 us; the launch traced here: 167 us
  waiting for transfers between devices  110 us (65%)
  starting transfers between devices  25.1 us (15%)
  local copies, waits for them, and re-layouts  10.8 us (6%)
  matrix products  10.7 us (6%)
  other arithmetic  10.2 us (6%)
    all_to_all x2, waiting for transfers between devices, _exchange_rows(): lax.all_to_all(packed, 'expert', split_axis=0, concat_axis=0, tiled=True)  70 us
    ppermute x8, waiting for transfers between devices, _exchange(): return lax.ppermute(value, 'tensor', [(j, j ^ flip) for j in range(size)])  40.2 us
    all_to_all x2, starting transfers between devices, _exchange_rows(): lax.all_to_all(packed, 'expert', split_axis=0, concat_axis=0, tiled=True)  20.5 us
    dot_general x1, matrix products, body(): jnp.dot(flat_rows, w_in[0], preferred_element_type=jnp.float32)  5.46 us
    ppermute x8, starting transfers between devices, _exchange(): return lax.ppermute(value, 'tensor', [(j, j ^ flip) for j in range(size)])  4.62 us
  transfers between devices with their start and end apart: 10, of which 10 were waited for; matrix products, arithmetic and copies ran while one was open for 2% of the time, Pallas kernels for 0%

profile of v6, /device:TPU:32, one launch (start us, length us, event | category | flops | bytes accessed | tf_op | source)
XLA Modules:
  0.0 167.3 jit_solution(11847234771688508138)
XLA Ops:
  0.0 1.2 dynamic-slice_bitcast_fusion.1
  1.3 0.8 pad_maximum_fusion
  2.3 2.0 %collective-permute-done = bf16[128,2048]{1,0:T(8,128)(2,1)} collective-permute-done((bf16[128,2048]{1,0:T(8,128)(2,1)}, bf16[128,2048]{1,0:T(8,128)(2,1)}, u32[]{:S(2)}, u32[]{:S(2)}) %collective-permute-start) | collective-permute-done | bytes 524320 | tf_op jit(solution)/shard_map/ppermute | solution.py:9
  4.3 1.7 %fusion.13 = bf16[128,1024]{1,0:T(8,128)(2,1)} fusion(bf16[128,2048]{1,0:T(8,128)(2,1)} %collective-permute-done, s32[]{:T(128)S(6)} %select_n.67, bf16[1,128,4096]{2,1,0:T(8,128)(2,1)S(1)} %copy-done.3, s32[]{:T(128)S(6)} %select_n.66), kind=kLoop, calls=%fused_computation.18 | loop fusion | flops 524288 | bytes 786440 | tf_op jit(solution)/shard_map/convert_element_type | solution.py:33
  6.1 1.5 collective-permute-start.1
  7.7 1.2 reduce-window.6
  9.5 5.3 %collective-permute-done.1 = bf16[128,1024]{1,0:T(8,128)(2,1)} collective-permute-done((bf16[128,1024]{1,0:T(8,128)(2,1)}, bf16[128,1024]{1,0:T(8,128)(2,1)}, u32[]{:S(2)}, u32[]{:S(2)}) %collective-permute-start.1) | collective-permute-done | bytes 262176 | tf_op jit(solution)/shard_map/ppermute | solution.py:9
  14.7 1.3 multiply_reduce_fusion
  16.2 1.1 collective-permute-done.2
  17.3 1.5 collective-permute-start.3
  19.0 1.9 %collective-permute-done.3 = f32[128]{0:T(128)S(1)} collective-permute-done((f32[128]{0:T(128)S(1)}, f32[128]{0:T(128)S(1)}, u32[]{:S(2)}, u32[]{:S(2)}) %collective-permute-start.3) | collective-permute-done | bytes 544 | tf_op jit(solution)/shard_map/ppermute | solution.py:9
  21.5 1.7 reshape_reshape.12
  23.2 14.2 %all-to-all-start = ((bf16[64,40,256]{2,1,0:T(8,128)(2,1)}), bf16[64,40,256]{2,1,0:T(8,128)(2,1)S(1)}, u32[]{:S(2)}, u32[]{:S(2)}) async-start(bf16[64,40,256]{2,1,0:T(8,128)(2,1)} %reshape_reshape.12), calls=%async_computation | async-start | bytes 2621440 | tf_op jit(solution)/shard_map/all_to_all | solution.py:68
  37.4 34.9 %all-to-all-done = bf16[64,40,256]{2,1,0:T(8,128)(2,1)S(1)} async-done(((bf16[64,40,256]{2,1,0:T(8,128)(2,1)}), bf16[64,40,256]{2,1,0:T(8,128)(2,1)S(1)}, u32[]{:S(2)}, u32[]{:S(2)}) %all-to-all-start) | async-done | bytes 1310752 | tf_op jit(solution)/shard_map/all_to_all | solution.py:68
  72.3 1.6 reshape_reshape.13
  74.0 5.5 %fusion.2 = bf16[640,2048]{1,0:T(8,128)(2,1)S(1)} fusion(bf16[640,1024]{1,0:T(8,128)(2,1)} %reshape_reshape.13, bf16[1,1024,2048]{2,1,0:T(8,128)(2,1)} %param.12), kind=kOutput, calls=%fused_computation.2 | convolution fusion | flops 2685665280 | bytes 8126464 | tf_op jit(solution)/shard_map/dot_general | solution.py:109
  79.5 1.4 constant_dynamic-slice_fusion
  81.3 3.2 %collective-permute-done.4 = bf16[320,2048]{1,0:T(8,128)(2,1)S(1)} collective-permute-done((bf16[320,2048]{1,0:T(8,128)(2,1)}, bf16[320,2048]{1,0:T(8,128)(2,1)S(1)}, u32[]{:S(2)}, u32[]{:S(2)}) %collective-permute-start.4) | collective-permute-done | bytes 1310752 | tf_op jit(solution)/shard_map/ppermute | solution.py:9
  84.6 2.1 %add_convert_fusion = bf16[160,2048]{1,0:T(8,128)(2,1)} fusion(bf16[320,2048]{1,0:T(8,128)(2,1)S(1)} %collective-permute-done.4, s32[]{:T(128)S(6)} %select_n.73, bf16[640,2048]{1,0:T(8,128)(2,1)} %copy-done.2, s32[]{:T(128)S(6)} %select_n.72), kind=kLoop, calls=%fused_computation.8 | loop fusion | flops 1310720 | bytes 1966088 | tf_op jit(solution)/shard_map/convert_element_type | solution.py:46
  86.7 0.6 collective-permute-start.5
  87.3 16.5 %collective-permute-done.5 = bf16[160,2048]{1,0:T(8,128)(2,1)} collective-permute-done((bf16[160,2048]{1,0:T(8,128)(2,1)}, bf16[160,2048]{1,0:T(8,128)(2,1)}, u32[]{:S(2)}, u32[]{:S(2)}) %collective-permute-start.5) | collective-permute-done | bytes 655392 | tf_op jit(solution)/shard_map/ppermute | solution.py:9
  103.8 1.6 convert_add_fusion
  105.7 0.7 collective-permute-start.6
  106.4 8.3 %collective-permute-done.6 = bf16[160,1024]{1,0:T(8,128)(2,1)S(1)} collective-permute-done((bf16[160,1024]{1,0:T(8,128)(2,1)S(1)}, bf16[160,1024]{1,0:T(8,128)(2,1)S(1)}, u32[]{:S(2)}, u32[]{:S(2)}) %collective-permute-start.6) | collective-permute-done | bytes 327712 | tf_op jit(solution)/shard_map/ppermute | solution.py:9
  115.2 1.9 %collective-permute-done.7 = bf16[320,1024]{1,0:T(8,128)(2,1)S(1)} collective-permute-done((bf16[320,1024]{1,0:T(8,128)(2,1)S(1)}, bf16[320,1024]{1,0:T(8,128)(2,1)S(1)}, u32[]{:S(2)}, u32[]{:S(2)}) %collective-permute-start.7) | collective-permute-done | bytes 655392 | tf_op jit(solution)/shard_map/ppermute | solution.py:9
  117.1 1.5 fusion.7
  118.7 1.7 reshape_reshape.14
  120.3 6.2 %all-to-all-start.1 = ((bf16[64,40,256]{2,1,0:T(8,128)(2,1)}), bf16[64,40,256]{2,1,0:T(8,128)(2,1)S(1)}, u32[]{:S(2)}, u32[]{:S(2)}) async-start(bf16[64,40,256]{2,1,0:T(8,128)(2,1)} %reshape_reshape.14), calls=%async_computation.1 | async-start | bytes 2621440 | tf_op jit(solution)/shard_map/all_to_all | solution.py:68
  126.6 0.9 select_reduce_fusion
  127.5 35.1 %all-to-all-done.1 = bf16[64,40,256]{2,1,0:T(8,128)(2,1)S(1)} async-done(((bf16[64,40,256]{2,1,0:T(8,128)(2,1)}), bf16[64,40,256]{2,1,0:T(8,128)(2,1)S(1)}, u32[]{:S(2)}, u32[]{:S(2)}) %all-to-all-start.1) | async-done | bytes 1310752 | tf_op jit(solution)/shard_map/all_to_all | solution.py:68
  162.5 1.6 reshape_reshape.15
  164.2 3.1 %fusion.11 = bf16[128,1024]{1,0:T(8,128)(2,1)} fusion(f32[128,1024]{1,0:T(8,128)} %copy-done.1, f32[640,128]{1,0:T(8,128)} %select_reduce_fusion, bf16[640,1024]{1,0:T(8,128)(2,1)} %reshape_reshape.15), kind=kOutput, calls=%fused_computation.13 | convolution fusion | flops 1006895104 | bytes 2424832 | tf_op jit(solution)/shard_map/dot_general | solution.py:116
  (39 shorter events, 3.1 us)
Async XLA Ops:
  0.0 117.1 %copy-start = (bf16[1,1024,1024]{2,1,0:T(8,128)(2,1)S(1)}, bf16[1,1024,1024]{2,1,0:T(8,128)(2,1)}, u32[]{:S(2)}) copy-start(bf16[1,1024,1024]{2,1,0:T(8,128)(2,1)} %param.13) | copy-start | bytes 6291460
  0.0 4.3 %copy-start.3 = (bf16[1,128,4096]{2,1,0:T(8,128)(2,1)S(1)}, bf16[1,128,4096]{2,1,0:T(8,128)(2,1)}, u32[]{:S(2)}) copy-start(bf16[1,128,4096]{2,1,0:T(8,128)(2,1)} %param.7) | copy-start | bytes 3145732
  0.0 2.1 %copy-start.4 = (s32[128,4]{0,1:T(4,128)S(1)}, s32[128,4]{0,1:T(4,128)}, u32[]{:S(2)}) copy-start(s32[128,4]{0,1:T(4,128)} %param.10) | copy-start | bytes 6148
  2.1 2.3 %collective-permute-start = (bf16[128,2048]{1,0:T(8,128)(2,1)}, bf16[128,2048]{1,0:T(8,128)(2,1)}, u32[]{:S(2)}, u32[]{:S(2)}) collective-permute-start(bf16[128,2048]{1,0:T(8,128)(2,1)} %pad_maximum_fusion), channel_id=1, source_target_pairs={{0,1},{1,0},{2,3},{3,2},{4,5},{5,4},{6,7},{7,6},{8,9},{9,8},{10,11... | collective-permute-start | bytes 1572872 | tf_op jit(solution)/shard_map/ppermute | solution.py:9
  6.1 14.8 %copy-start.5 = (f32[1024]{0:T(1024)S(1)}, f32[1024]{0:T(1024)}, u32[]{:S(2)}) copy-start(f32[1024]{0:T(1024)} %param.9) | copy-start | bytes 12292
  6.1 8.7 %collective-permute-start.1 = (bf16[128,1024]{1,0:T(8,128)(2,1)}, bf16[128,1024]{1,0:T(8,128)(2,1)}, u32[]{:S(2)}, u32[]{:S(2)}) collective-permute-start(bf16[128,1024]{1,0:T(8,128)(2,1)} %fusion.13), channel_id=1, source_target_pairs={{0,2},{1,3},{2,0},{3,1},{4,6},{5,7},{6,4},{7,5},{8,10},{9,11},{10,... | collective-permute-start | bytes 786440 | tf_op jit(solution)/shard_map/ppermute | solution.py:9
  16.1 4.8 %copy-start.1 = (f32[128,1024]{1,0:T(8,128)}, f32[128,1024]{1,0:T(8,128)S(1)}, u32[]{:S(2)}) copy-start(f32[128,1024]{1,0:T(8,128)S(1)} %get-tuple-element.8) | copy-start | bytes 1572868
  16.1 1.2 collective-permute-start.2
  17.3 3.6 %collective-permute-start.3 = (f32[128]{0:T(128)S(1)}, f32[128]{0:T(128)S(1)}, u32[]{:S(2)}, u32[]{:S(2)}) collective-permute-start(f32[128]{0:T(128)S(1)} %add.118), channel_id=1, source_target_pairs={{0,2},{1,3},{2,0},{3,1},{4,6},{5,7},{6,4},{7,5},{8,10},{9,11},{10,... | collective-permute-start | bytes 1544 | tf_op jit(solution)/shard_map/ppermute | solution.py:9
  23.2 49.2 %all-to-all-start = ((bf16[64,40,256]{2,1,0:T(8,128)(2,1)}), bf16[64,40,256]{2,1,0:T(8,128)(2,1)S(1)}, u32[]{:S(2)}, u32[]{:S(2)}) async-start(bf16[64,40,256]{2,1,0:T(8,128)(2,1)} %reshape_reshape.12), calls=%async_computation | async-start | bytes 2621440 | tf_op jit(solution)/shard_map/all_to_all | solution.py:68
  79.4 1.9 %copy-start.2 = (bf16[640,2048]{1,0:T(8,128)(2,1)}, bf16[640,2048]{1,0:T(8,128)(2,1)S(1)}, u32[]{:S(2)}) copy-start(bf16[640,2048]{1,0:T(8,128)(2,1)S(1)} %fusion.2) | copy-start | bytes 7864324
  81.3 3.2 %collective-permute-start.4 = (bf16[320,2048]{1,0:T(8,128)(2,1)}, bf16[320,2048]{1,0:T(8,128)(2,1)S(1)}, u32[]{:S(2)}, u32[]{:S(2)}) collective-permute-start(bf16[320,2048]{1,0:T(8,128)(2,1)} %constant_dynamic-slice_fusion), channel_id=1, source_target_pairs={{0,1},{1,0},{2,3},{3,2},{4,5},{5,4},{6,7},{7,6},{8,9},{9,8},{10,11... | collective-permute-start | bytes 3932168 | tf_op jit(solution)/shard_map/ppermute | solution.py:9
  86.7 17.1 %collective-permute-start.5 = (bf16[160,2048]{1,0:T(8,128)(2,1)}, bf16[160,2048]{1,0:T(8,128)(2,1)}, u32[]{:S(2)}, u32[]{:S(2)}) collective-permute-start(bf16[160,2048]{1,0:T(8,128)(2,1)} %add_convert_fusion), channel_id=1, source_target_pairs={{0,2},{1,3},{2,0},{3,1},{4,6},{5,7},{6,4},{7,5},{8,10},{9,11},{10,... | collective-permute-start | bytes 1966088 | tf_op jit(solution)/shard_map/ppermute | solution.py:9
  105.7 9.0 %collective-permute-start.6 = (bf16[160,1024]{1,0:T(8,128)(2,1)S(1)}, bf16[160,1024]{1,0:T(8,128)(2,1)S(1)}, u32[]{:S(2)}, u32[]{:S(2)}) collective-permute-start(bf16[160,1024]{1,0:T(8,128)(2,1)S(1)} %get-tuple-element.6), channel_id=1, source_target_pairs={{0,2},{1,3},{2,0},{3,1},{4,6},{5,7},{6,4},{7,5},{8,10},{9,11},{10,... | collective-permute-start | bytes 983048 | tf_op jit(solution)/shard_map/ppermute | solution.py:9
  114.7 2.4 %collective-permute-start.7 = (bf16[320,1024]{1,0:T(8,128)(2,1)S(1)}, bf16[320,1024]{1,0:T(8,128)(2,1)S(1)}, u32[]{:S(2)}, u32[]{:S(2)}) collective-permute-start(bf16[320,1024]{1,0:T(8,128)(2,1)S(1)} %constant_dynamic-update-slice_fusion.2), channel_id=1, source_target_pairs={{0,1},{1,0},{2,3},{3,2},{4,5},{5,4},{6,7},{7,6},{8,9},{9,8},{10,11... | collective-permute-start | bytes 1966088 | tf_op jit(solution)/shard_map/ppermute | solution.py:9
  120.3 6.2 %copy-start.6 = (f32[128,4]{0,1:T(4,128)S(1)}, f32[128,4]{0,1:T(4,128)}, u32[]{:S(2)}) copy-start(f32[128,4]{0,1:T(4,128)} %param.11) | copy-start | bytes 6148
  120.3 42.2 %all-to-all-start.1 = ((bf16[64,40,256]{2,1,0:T(8,128)(2,1)}), bf16[64,40,256]{2,1,0:T(8,128)(2,1)S(1)}, u32[]{:S(2)}, u32[]{:S(2)}) async-start(bf16[64,40,256]{2,1,0:T(8,128)(2,1)} %reshape_reshape.14), calls=%async_computation.1 | async-start | bytes 2621440 | tf_op jit(solution)/shard_map/all_to_all | solution.py:68

commit v7 on v6

--- a/solution.py
+++ b/solution.py
@@ -7,10 +7,6 @@
 def _exchange(value, flip):
     size = lax.axis_size("tensor")
     return lax.ppermute(value, "tensor", [(j, j ^ flip) for j in range(size)])
-
-
-def _pick(value, axis, index):
-    return lax.dynamic_index_in_dim(value, index, axis=axis, keepdims=False)
 
 
 def _slab(value, start, size, axis):
@@ -30,19 +26,6 @@
     away = away + _slab(received, (1 - high) * n, n, axis).astype(jnp.float32)
     home = _slab(value, (2 * high + core) * n, n, axis).astype(jnp.float32)
     home = home + _slab(received, high * n, n, axis).astype(jnp.float32)
-    return home + _exchange(away.astype(jnp.bfloat16), 2).astype(jnp.float32)
-
-
-def _reduce_scatter_rows(value):
-    t = lax.axis_index("tensor")
-    core = t % 2
-    high = t // 2
-    n = value.shape[0] // 4
-    received = _exchange(_slab(value, 2 * (1 - core) * n, 2 * n, 0).astype(jnp.bfloat16), 1)
-    away = _slab(value, (2 * core + 1 - high) * n, n, 0).astype(jnp.float32)
-    away = away + _slab(received, (1 - high) * n, n, 0).astype(jnp.float32)
-    home = _slab(value, (2 * core + high) * n, n, 0).astype(jnp.float32)
-    home = home + _slab(received, high * n, n, 0).astype(jnp.float32)
     return home + _exchange(away.astype(jnp.bfloat16), 2).astype(jnp.float32)
 
 
@@ -74,7 +57,7 @@
     return value + _exchange(value, 2)
 
 
-def body(attn_partial, residual, norm_gain, expert_ids, route_weight, w_in, w_down):
+def _body(attn_partial, residual, norm_gain, expert_ids, route_weight, w_in, w_down):
     token_count = expert_ids.shape[0]
     topk_count = expert_ids.shape[1]
     feature_local = residual.shape[1]
@@ -106,8 +89,22 @@
     item_count = in_rows.shape[1]
     row_total = source_count * item_count
     flat_rows = in_rows.reshape(row_total, feature_local)
-    partial_value = jnp.dot(flat_rows, w_in[0], preferred_element_type=jnp.float32)
-    total = _reduce_scatter_rows(partial_value.astype(jnp.bfloat16))
+    t = lax.axis_index("tensor")
+    core = t % 2
+    high = t // 2
+    block = row_total // 4
+    away_rows = _slab(flat_rows, 2 * (1 - core) * block, 2 * block, 0)
+    home_rows = _slab(flat_rows, 2 * core * block, 2 * block, 0)
+    sent = jnp.dot(away_rows, w_in[0], preferred_element_type=jnp.float32).astype(jnp.bfloat16)
+    home_rows, sent = lax.optimization_barrier((home_rows, sent))
+    received = _exchange(sent, 1)
+    kept = jnp.dot(home_rows, w_in[0], preferred_element_type=jnp.float32).astype(jnp.bfloat16)
+    away = _slab(kept, (1 - high) * block, block, 0).astype(jnp.float32)
+    away = away + _slab(received, (1 - high) * block, block, 0).astype(jnp.float32)
+    far = _exchange(away.astype(jnp.bfloat16), 2)
+    home = _slab(kept, high * block, block, 0).astype(jnp.float32)
+    home = lax.optimization_barrier(home + _slab(received, high * block, block, 0).astype(jnp.float32))
+    total = home + far.astype(jnp.float32)
     hidden = (jax.nn.silu(total[:, :hidden_width]) * total[:, hidden_width:]).astype(jnp.bfloat16)
     hidden = _all_gather_rows(hidden)
     produced = jnp.dot(hidden, w_down[0], preferred_element_type=jnp.float32).astype(jnp.bfloat16)
@@ -132,4 +129,4 @@
         P("expert", None, "tensor"),
     )
     out_specs = P("expert", "tensor")
-    return jax.shard_map(body, mesh=mesh, in_specs=in_specs, out_specs=out_specs, check_vma=False)
+    return jax.shard_map(_body, mesh=mesh, in_specs=in_specs, out_specs=out_specs, check_vma=False)

time: 168 us -> 165 us (0.982)
  matrix products: 10.7 us -> 13.9 us
  other arithmetic: 10.2 us -> 7.1 us
  waiting for transfers between devices: 110 us -> 107 us
    dot_general x4 -> x5, matrix products: 10.7 us -> 13.9 us  [the longest x1 4.78 us: _body(): jnp.dot(away_rows, w_in[0], preferred_element_type=jnp.float32)]
    ppermute x8, waiting for transfers between devices: 40.2 us -> 37.4 us  [_exchange(): return lax.ppermute(value, 'tensor', [(j, j ^ flip) for j in range(size)])]
  transfers between devices with their start and end apart: 10 -> 10, of which waited for: 10 -> 9; matrix products, arithmetic and copies ran while one was open for 2% -> 4% of each run, Pallas kernels for 0% -> 0%
where the time goes in v7:
time: 165 us
  waiting for transfers between devices  107 us (65%)
  starting transfers between devices  25.2 us (15%)
  matrix products  13.9 us (8%)
  local copies, waits for them, and re-layouts  11 us (7%)
  other arithmetic  7.1 us (4%)
    all_to_all x2, waiting for transfers between devices, _exchange_rows(): lax.all_to_all(packed, 'expert', split_axis=0, concat_axis=0, tiled=True)  70 us
    ppermute x8, waiting for transfers between devices, _exchange(): return lax.ppermute(value, 'tensor', [(j, j ^ flip) for j in range(size)])  37.4 us
    all_to_all x2, starting transfers between devices, _exchange_rows(): lax.all_to_all(packed, 'expert', split_axis=0, concat_axis=0, tiled=True)  20.5 us
    dot_general x1, matrix products, _body(): jnp.dot(away_rows, w_in[0], preferred_element_type=jnp.float32)  4.78 us
    ppermute x8, starting transfers between devices, _exchange(): return lax.ppermute(value, 'tensor', [(j, j ^ flip) for j in range(size)])  4.71 us
    dot_general x1, matrix products, _body(): jnp.dot(home_rows, w_in[0], preferred_element_type=jnp.float32)  3.91 us
    dynamic_slice x2, local copies, waits for them, and re-layouts, _slab(): return lax.dynamic_slice_in_dim(value, start, size, axis=axis)  3.34 us
    another operation x2, local copies, waits for them, and re-layouts, _exchange_rows(): packed = value.reshape(experts, slots * features // lanes, lanes)  3.31 us
  transfers between devices with their start and end apart: 10, of which 9 were waited for; matrix products, arithmetic and copies ran while one was open for 4% of the time, Pallas kernels for 0%

profile of v7, /device:TPU:32, one launch (start us, length us, event | category | flops | bytes accessed | tf_op | source)
XLA Modules:
  0.0 164.9 jit_solution(13995259772517319191)
XLA Ops:
  0.0 1.2 dynamic-slice_bitcast_fusion.1
  1.3 0.8 pad_maximum_fusion
  2.3 2.0 %collective-permute-done = bf16[128,2048]{1,0:T(8,128)(2,1)} collective-permute-done((bf16[128,2048]{1,0:T(8,128)(2,1)}, bf16[128,2048]{1,0:T(8,128)(2,1)}, u32[]{:S(2)}, u32[]{:S(2)}) %collective-permute-start) | collective-permute-done | bytes 524320 | tf_op jit(solution)/shard_map/ppermute | solution.py:9
  4.3 1.7 %fusion.19 = bf16[128,1024]{1,0:T(8,128)(2,1)} fusion(bf16[128,2048]{1,0:T(8,128)(2,1)} %collective-permute-done, s32[]{:T(128)S(6)} %select_n.64, bf16[1,128,4096]{2,1,0:T(8,128)(2,1)S(1)} %copy-done.3, s32[]{:T(128)S(6)} %select_n.63), kind=kLoop, calls=%fused_computation.23 | loop fusion | flops 524288 | bytes 786440 | tf_op jit(solution)/shard_map/convert_element_type | solution.py:29
  6.1 1.5 collective-permute-start.1
  7.7 1.2 reduce-window.6
  9.5 5.3 %collective-permute-done.1 = bf16[128,1024]{1,0:T(8,128)(2,1)} collective-permute-done((bf16[128,1024]{1,0:T(8,128)(2,1)}, bf16[128,1024]{1,0:T(8,128)(2,1)}, u32[]{:S(2)}, u32[]{:S(2)}) %collective-permute-start.1) | collective-permute-done | bytes 262176 | tf_op jit(solution)/shard_map/ppermute | solution.py:9
  14.7 1.3 multiply_reduce_fusion
  16.2 1.1 collective-permute-done.2
  17.3 1.5 collective-permute-start.3
  19.0 1.9 %collective-permute-done.3 = f32[128]{0:T(128)S(1)} collective-permute-done((f32[128]{0:T(128)S(1)}, f32[128]{0:T(128)S(1)}, u32[]{:S(2)}, u32[]{:S(2)}) %collective-permute-start.3) | collective-permute-done | bytes 544 | tf_op jit(solution)/shard_map/ppermute | solution.py:9
  20.9 0.6 convolution_convert_fusion
  21.5 1.7 %reshape_reshape.12 = bf16[64,40,256]{2,1,0:T(8,128)(2,1)} reshape(bf16[640,1024]{1,0:T(8,128)(2,1)S(1)} %convolution_convert_fusion) | data formatting | bytes 2621440 | tf_op jit(solution)/shard_map/reshape;reshape | solution.py:50
  23.2 14.2 %all-to-all-start = ((bf16[64,40,256]{2,1,0:T(8,128)(2,1)}), bf16[64,40,256]{2,1,0:T(8,128)(2,1)S(1)}, u32[]{:S(2)}, u32[]{:S(2)}) async-start(bf16[64,40,256]{2,1,0:T(8,128)(2,1)} %reshape_reshape.12), calls=%async_computation | async-start | bytes 2621440 | tf_op jit(solution)/shard_map/all_to_all | solution.py:51
  37.4 34.9 %all-to-all-done = bf16[64,40,256]{2,1,0:T(8,128)(2,1)S(1)} async-done(((bf16[64,40,256]{2,1,0:T(8,128)(2,1)}), bf16[64,40,256]{2,1,0:T(8,128)(2,1)S(1)}, u32[]{:S(2)}, u32[]{:S(2)}) %all-to-all-start) | async-done | bytes 1310752 | tf_op jit(solution)/shard_map/all_to_all | solution.py:51
  72.3 1.6 reshape_reshape.13
  74.0 2.1 %constant_dynamic-slice_fusion = bf16[320,1024]{1,0:T(8,128)(2,1)} fusion(bf16[640,1024]{1,0:T(8,128)(2,1)} %reshape_reshape.13, s32[]{:T(128)S(6)} %select_n.66), kind=kLoop, calls=%fused_computation.44 | loop fusion | bytes 1310724 | tf_op jit(solution)/shard_map/dynamic_slice | solution.py:13
  76.1 4.8 %fusion.4 = bf16[320,2048]{1,0:T(8,128)(2,1)} fusion(bf16[1,1024,2048]{2,1,0:T(8,128)(2,1)} %param.12, bf16[640,1024]{1,0:T(8,128)(2,1)S(1)} %copy-done.2, s32[]{:T(128)S(6)} %select_n.67), kind=kOutput, calls=%fused_computation.4 | convolution fusion | flops 1342832640 | bytes 6160388 | tf_op jit(solution)/shard_map/dot_general | solution.py:98
  80.9 3.9 %fusion.7 = bf16[320,2048]{1,0:T(8,128)(2,1)S(1)} fusion(bf16[320,1024]{1,0:T(8,128)(2,1)} %constant_dynamic-slice_fusion, bf16[1,1024,2048]{2,1,0:T(8,128)(2,1)} %param.12), kind=kOutput, calls=%fused_computation.5 | convolution fusion | flops 1342832640 | bytes 6160384 | tf_op jit(solution)/shard_map/dot_general | solution.py:101
  84.8 0.4 add_convert_fusion
  85.3 0.7 collective-permute-start.5
  85.9 16.6 %collective-permute-done.5 = bf16[160,2048]{1,0:T(8,128)(2,1)S(1)} collective-permute-done((bf16[160,2048]{1,0:T(8,128)(2,1)S(1)}, bf16[160,2048]{1,0:T(8,128)(2,1)S(1)}, u32[]{:S(2)}, u32[]{:S(2)}) %collective-permute-start.5) | collective-permute-done | bytes 655392 | tf_op jit(solution)/shard_map/ppermute | solution.py:9
  102.9 0.7 collective-permute-start.6
  103.6 8.7 %collective-permute-done.6 = bf16[160,1024]{1,0:T(8,128)(2,1)S(1)} collective-permute-done((bf16[160,1024]{1,0:T(8,128)(2,1)S(1)}, bf16[160,1024]{1,0:T(8,128)(2,1)S(1)}, u32[]{:S(2)}, u32[]{:S(2)}) %collective-permute-start.6) | collective-permute-done | bytes 327712 | tf_op jit(solution)/shard_map/ppermute | solution.py:9
  112.8 1.9 %collective-permute-done.7 = bf16[320,1024]{1,0:T(8,128)(2,1)S(1)} collective-permute-done((bf16[320,1024]{1,0:T(8,128)(2,1)S(1)}, bf16[320,1024]{1,0:T(8,128)(2,1)S(1)}, u32[]{:S(2)}, u32[]{:S(2)}) %collective-permute-start.7) | collective-permute-done | bytes 655392 | tf_op jit(solution)/shard_map/ppermute | solution.py:9
  114.7 1.5 fusion.12
  116.3 1.7 %reshape_reshape.14 = bf16[64,40,256]{2,1,0:T(8,128)(2,1)} reshape(bf16[640,1024]{1,0:T(8,128)(2,1)S(1)} %fusion.12) | data formatting | bytes 2621440 | tf_op jit(solution)/shard_map/reshape;reshape | solution.py:50
  118.0 6.2 %all-to-all-start.1 = ((bf16[64,40,256]{2,1,0:T(8,128)(2,1)}), bf16[64,40,256]{2,1,0:T(8,128)(2,1)S(1)}, u32[]{:S(2)}, u32[]{:S(2)}) async-start(bf16[64,40,256]{2,1,0:T(8,128)(2,1)} %reshape_reshape.14), calls=%async_computation.1 | async-start | bytes 2621440 | tf_op jit(solution)/shard_map/all_to_all | solution.py:51
  124.2 0.9 select_reduce_fusion
  125.1 35.1 %all-to-all-done.1 = bf16[64,40,256]{2,1,0:T(8,128)(2,1)S(1)} async-done(((bf16[64,40,256]{2,1,0:T(8,128)(2,1)}), bf16[64,40,256]{2,1,0:T(8,128)(2,1)S(1)}, u32[]{:S(2)}, u32[]{:S(2)}) %all-to-all-start.1) | async-done | bytes 1310752 | tf_op jit(solution)/shard_map/all_to_all | solution.py:51
  160.2 1.6 reshape_reshape.15
  161.8 3.1 %fusion.16 = bf16[128,1024]{1,0:T(8,128)(2,1)} fusion(f32[128,1024]{1,0:T(8,128)} %copy-done.1, f32[640,128]{1,0:T(8,128)} %select_reduce_fusion, bf16[640,1024]{1,0:T(8,128)(2,1)} %reshape_reshape.15), kind=kOutput, calls=%fused_computation.17 | convolution fusion | flops 1006895104 | bytes 2424832 | tf_op jit(solution)/shard_map/dot_general | solution.py:113
  (40 shorter events, 2.2 us)
Async XLA Ops:
  0.0 114.7 %copy-start = (bf16[1,1024,1024]{2,1,0:T(8,128)(2,1)S(1)}, bf16[1,1024,1024]{2,1,0:T(8,128)(2,1)}, u32[]{:S(2)}) copy-start(bf16[1,1024,1024]{2,1,0:T(8,128)(2,1)} %param.13) | copy-start | bytes 6291460
  0.0 4.3 %copy-start.3 = (bf16[1,128,4096]{2,1,0:T(8,128)(2,1)S(1)}, bf16[1,128,4096]{2,1,0:T(8,128)(2,1)}, u32[]{:S(2)}) copy-start(bf16[1,128,4096]{2,1,0:T(8,128)(2,1)} %param.7) | copy-start | bytes 3145732
  0.0 2.1 %copy-start.4 = (s32[128,4]{0,1:T(4,128)S(1)}, s32[128,4]{0,1:T(4,128)}, u32[]{:S(2)}) copy-start(s32[128,4]{0,1:T(4,128)} %param.10) | copy-start | bytes 6148
  2.1 2.3 %collective-permute-start = (bf16[128,2048]{1,0:T(8,128)(2,1)}, bf16[128,2048]{1,0:T(8,128)(2,1)}, u32[]{:S(2)}, u32[]{:S(2)}) collective-permute-start(bf16[128,2048]{1,0:T(8,128)(2,1)} %pad_maximum_fusion), channel_id=1, source_target_pairs={{0,1},{1,0},{2,3},{3,2},{4,5},{5,4},{6,7},{7,6},{8,9},{9,8},{10,11... | collective-permute-start | bytes 1572872 | tf_op jit(solution)/shard_map/ppermute | solution.py:9
  6.1 14.8 %copy-start.5 = (f32[1024]{0:T(1024)S(1)}, f32[1024]{0:T(1024)}, u32[]{:S(2)}) copy-start(f32[1024]{0:T(1024)} %param.9) | copy-start | bytes 12292
  6.1 8.7 %collective-permute-start.1 = (bf16[128,1024]{1,0:T(8,128)(2,1)}, bf16[128,1024]{1,0:T(8,128)(2,1)}, u32[]{:S(2)}, u32[]{:S(2)}) collective-permute-start(bf16[128,1024]{1,0:T(8,128)(2,1)} %fusion.19), channel_id=1, source_target_pairs={{0,2},{1,3},{2,0},{3,1},{4,6},{5,7},{6,4},{7,5},{8,10},{9,11},{10,... | collective-permute-start | bytes 786440 | tf_op jit(solution)/shard_map/ppermute | solution.py:9
  16.1 4.8 %copy-start.1 = (f32[128,1024]{1,0:T(8,128)}, f32[128,1024]{1,0:T(8,128)S(1)}, u32[]{:S(2)}) copy-start(f32[128,1024]{1,0:T(8,128)S(1)} %get-tuple-element.12) | copy-start | bytes 1572868
  16.1 1.2 collective-permute-start.2
  17.3 3.6 %collective-permute-start.3 = (f32[128]{0:T(128)S(1)}, f32[128]{0:T(128)S(1)}, u32[]{:S(2)}, u32[]{:S(2)}) collective-permute-start(f32[128]{0:T(128)S(1)} %add.109), channel_id=1, source_target_pairs={{0,2},{1,3},{2,0},{3,1},{4,6},{5,7},{6,4},{7,5},{8,10},{9,11},{10,... | collective-permute-start | bytes 1544 | tf_op jit(solution)/shard_map/ppermute | solution.py:9
  23.2 49.2 %all-to-all-start = ((bf16[64,40,256]{2,1,0:T(8,128)(2,1)}), bf16[64,40,256]{2,1,0:T(8,128)(2,1)S(1)}, u32[]{:S(2)}, u32[]{:S(2)}) async-start(bf16[64,40,256]{2,1,0:T(8,128)(2,1)} %reshape_reshape.12), calls=%async_computation | async-start | bytes 2621440 | tf_op jit(solution)/shard_map/all_to_all | solution.py:51
  74.0 2.1 %copy-start.2 = (bf16[640,1024]{1,0:T(8,128)(2,1)S(1)}, bf16[640,1024]{1,0:T(8,128)(2,1)}, u32[]{:S(2)}) copy-start(bf16[640,1024]{1,0:T(8,128)(2,1)} %reshape_reshape.13) | copy-start | bytes 3932164
  80.9 3.9 %collective-permute-start.4 = (bf16[320,2048]{1,0:T(8,128)(2,1)}, bf16[320,2048]{1,0:T(8,128)(2,1)S(1)}, u32[]{:S(2)}, u32[]{:S(2)}) collective-permute-start(bf16[320,2048]{1,0:T(8,128)(2,1)} %fusion.4), channel_id=1, source_target_pairs={{0,1},{1,0},{2,3},{3,2},{4,5},{5,4},{6,7},{7,6},{8,9},{9,8},{10,11... | collective-permute-start | bytes 3932168 | tf_op jit(solution)/shard_map/ppermute | solution.py:9
  85.3 17.2 %collective-permute-start.5 = (bf16[160,2048]{1,0:T(8,128)(2,1)S(1)}, bf16[160,2048]{1,0:T(8,128)(2,1)S(1)}, u32[]{:S(2)}, u32[]{:S(2)}) collective-permute-start(bf16[160,2048]{1,0:T(8,128)(2,1)S(1)} %get-tuple-element.13), channel_id=1, source_target_pairs={{0,2},{1,3},{2,0},{3,1},{4,6},{5,7},{6,4},{7,5},{8,10},{9,11},{10,... | collective-permute-start | bytes 1966088 | tf_op jit(solution)/shard_map/ppermute | solution.py:9
  102.9 9.4 %collective-permute-start.6 = (bf16[160,1024]{1,0:T(8,128)(2,1)S(1)}, bf16[160,1024]{1,0:T(8,128)(2,1)S(1)}, u32[]{:S(2)}, u32[]{:S(2)}) collective-permute-start(bf16[160,1024]{1,0:T(8,128)(2,1)S(1)} %get-tuple-element.10), channel_id=1, source_target_pairs={{0,2},{1,3},{2,0},{3,1},{4,6},{5,7},{6,4},{7,5},{8,10},{9,11},{10,... | collective-permute-start | bytes 983048 | tf_op jit(solution)/shard_map/ppermute | solution.py:9
  112.3 2.4 %collective-permute-start.7 = (bf16[320,1024]{1,0:T(8,128)(2,1)S(1)}, bf16[320,1024]{1,0:T(8,128)(2,1)S(1)}, u32[]{:S(2)}, u32[]{:S(2)}) collective-permute-start(bf16[320,1024]{1,0:T(8,128)(2,1)S(1)} %constant_dynamic-update-slice_fusion.3), channel_id=1, source_target_pairs={{0,1},{1,0},{2,3},{3,2},{4,5},{5,4},{6,7},{7,6},{8,9},{9,8},{10,11... | collective-permute-start | bytes 1966088 | tf_op jit(solution)/shard_map/ppermute | solution.py:9
  118.0 6.2 %copy-start.6 = (f32[128,4]{0,1:T(4,128)S(1)}, f32[128,4]{0,1:T(4,128)}, u32[]{:S(2)}) copy-start(f32[128,4]{0,1:T(4,128)} %param.11) | copy-start | bytes 6148
  118.0 42.2 %all-to-all-start.1 = ((bf16[64,40,256]{2,1,0:T(8,128)(2,1)}), bf16[64,40,256]{2,1,0:T(8,128)(2,1)S(1)}, u32[]{:S(2)}, u32[]{:S(2)}) async-start(bf16[64,40,256]{2,1,0:T(8,128)(2,1)} %reshape_reshape.14), calls=%async_computation.1 | async-start | bytes 2621440 | tf_op jit(solution)/shard_map/all_to_all | solution.py:51

commit v8 on v7

--- a/solution.py
+++ b/solution.py
@@ -24,9 +24,10 @@
     received = _exchange(sent, 1)
     away = _slab(value, (3 - 2 * high + core - 1) * n, n, axis).astype(jnp.float32)
     away = away + _slab(received, (1 - high) * n, n, axis).astype(jnp.float32)
+    far = _exchange(away.astype(jnp.bfloat16), 2)
     home = _slab(value, (2 * high + core) * n, n, axis).astype(jnp.float32)
-    home = home + _slab(received, high * n, n, axis).astype(jnp.float32)
-    return home + _exchange(away.astype(jnp.bfloat16), 2).astype(jnp.float32)
+    home = lax.optimization_barrier(home + _slab(received, high * n, n, axis).astype(jnp.float32))
+    return home + far.astype(jnp.float32)
 
 
 def _all_gather_rows(value):
@@ -110,11 +111,13 @@
     produced = jnp.dot(hidden, w_down[0], preferred_element_type=jnp.float32).astype(jnp.bfloat16)
     results = produced.reshape(source_count, item_count, feature_local)
     returned = _exchange_rows(results)
-    routed = jnp.dot(
-        weights_table,
-        returned.reshape(expert_count * capacity, feature_local).astype(jnp.float32),
-        precision=lax.Precision.HIGHEST,
+    flat_returned = returned.reshape(expert_count * capacity, feature_local)
+    weights_high = weights_table.astype(jnp.bfloat16)
+    weights_low = (weights_table - weights_high.astype(jnp.float32)).astype(jnp.bfloat16)
+    both = jnp.dot(
+        jnp.concatenate([weights_high, weights_low], 0), flat_returned, preferred_element_type=jnp.float32
     )
+    routed = both[:token_count] + both[token_count:]
     return (stream + routed).astype(jnp.bfloat16)
 
 

time: 165 us -> 174 us (1.055)
  local copies, waits for them, and re-layouts: 11 us -> 18 us
    another operation x2, local copies, waits for them, and re-layouts: 3.31 us -> 6.78 us  [_exchange_rows(): packed = value.reshape(experts, slots * features // lanes, lanes)]
    another operation x2, local copies, waits for them, and re-layouts: 1.64 us -> 3.39 us  [the longest x1 3.39 us: _body(): flat_returned = returned.reshape(expert_count * capacity, feature_local)]
    another operation x1, local copies, waits for them, and re-layouts: 1.64 us -> 3.39 us  [_body(): flat_rows = in_rows.reshape(row_total, feature_local)]
where the time goes in v8:
time: 174 us; the launch traced here: 173 us
  waiting for transfers between devices  108 us (62%)
  starting transfers between devices  25.6 us (15%)
  local copies, waits for them, and re-layouts  18 us (10%)
  matrix products  14.9 us (9%)
  other arithmetic  6.98 us (4%)
    all_to_all x2, waiting for transfers between devices, _exchange_rows(): lax.all_to_all(packed, 'expert', split_axis=0, concat_axis=0, tiled=True)  70.6 us
    ppermute x8, waiting for transfers between devices, _exchange(): return lax.ppermute(value, 'tensor', [(j, j ^ flip) for j in range(size)])  37 us
    all_to_all x2, starting transfers between devices, _exchange_rows(): lax.all_to_all(packed, 'expert', split_axis=0, concat_axis=0, tiled=True)  20.8 us
    another operation x2, local copies, waits for them, and re-layouts, _exchange_rows(): packed = value.reshape(experts, slots * features // lanes, lanes)  6.78 us
    ppermute x8, starting transfers between devices, _exchange(): return lax.ppermute(value, 'tensor', [(j, j ^ flip) for j in range(size)])  4.8 us
    dot_general x1, matrix products, _body(): jnp.dot(away_rows, w_in[0], preferred_element_type=jnp.float32)  4.78 us
    dot_general x1, matrix products, _body(): jnp.dot(home_rows, w_in[0], preferred_element_type=jnp.float32)  3.91 us
  transfers between devices with their start and end apart: 10, of which 9 were waited for; matrix products, arithmetic and copies ran while one was open for 4% of the time, Pallas kernels for 0%

profile of v8, /device:TPU:32, one launch (start us, length us, event | category | flops | bytes accessed | tf_op | source)
XLA Modules:
  0.0 173.3 jit_solution(17385308653876168394)
XLA Ops:
  0.0 1.2 dynamic-slice_bitcast_fusion.1
  1.7 1.7 collective-permute-done
  3.4 2.1 %fusion.20 = (bf16[128,1024]{1,0:T(8,128)(2,1)}, f32[128,1024]{1,0:T(8,128)S(1)}) fusion(bf16[128,2048]{1,0:T(8,128)(2,1)} %collective-permute-done, s32[]{:T(128)S(6)} %select_n.64, bf16[1,128,4096]{2,1,0:T(8,128)(2,1)} %param.7, s32[]{:T(128)S(6)} %select_n.63, s32[]{:T(128)S(6)} %select_n.62, s32[]{:T(128)S(6)} %select_n.59), kind=kLoop, calls=%fused_computation.24 | loop fusion | flops 917504 | bytes 1835024 | tf_op jit(solution)/shard_map/convert_element_type | solution.py:27
  5.5 1.5 collective-permute-start.1
  7.1 1.2 reduce-window.6
  8.3 0.2 slice_reduce_fusion
  8.9 5.2 %collective-permute-done.1 = bf16[128,1024]{1,0:T(8,128)(2,1)S(1)} collective-permute-done((bf16[128,1024]{1,0:T(8,128)(2,1)}, bf16[128,1024]{1,0:T(8,128)(2,1)S(1)}, u32[]{:S(2)}, u32[]{:S(2)}) %collective-permute-start.1) | collective-permute-done | bytes 262176 | tf_op jit(solution)/shard_map/ppermute | solution.py:9
  14.3 1.1 collective-permute-done.2
  15.5 1.5 collective-permute-start.3
  17.1 1.9 %collective-permute-done.3 = f32[128]{0:T(128)S(1)} collective-permute-done((f32[128]{0:T(128)S(1)}, f32[128]{0:T(128)S(1)}, u32[]{:S(2)}, u32[]{:S(2)}) %collective-permute-start.3) | collective-permute-done | bytes 544 | tf_op jit(solution)/shard_map/ppermute | solution.py:9
  19.0 1.6 convolution_convert_fusion
  20.7 3.4 %reshape_reshape.12 = bf16[64,40,256]{2,1,0:T(8,128)(2,1)} reshape(bf16[640,1024]{1,0:T(8,128)(2,1)} %convolution_convert_fusion) | data formatting | bytes 2621440 | tf_op jit(solution)/shard_map/reshape;reshape | solution.py:51
  24.1 14.4 %all-to-all-start = ((bf16[64,40,256]{2,1,0:T(8,128)(2,1)}), bf16[64,40,256]{2,1,0:T(8,128)(2,1)}, u32[]{:S(2)}, u32[]{:S(2)}) async-start(bf16[64,40,256]{2,1,0:T(8,128)(2,1)} %reshape_reshape.12), calls=%async_computation | async-start | bytes 2621440 | tf_op jit(solution)/shard_map/all_to_all | solution.py:52
  38.5 34.9 %all-to-all-done = bf16[64,40,256]{2,1,0:T(8,128)(2,1)} async-done(((bf16[64,40,256]{2,1,0:T(8,128)(2,1)}), bf16[64,40,256]{2,1,0:T(8,128)(2,1)}, u32[]{:S(2)}, u32[]{:S(2)}) %all-to-all-start) | async-done | bytes 1310752 | tf_op jit(solution)/shard_map/all_to_all | solution.py:52
  73.4 3.4 %reshape_reshape.13 = bf16[640,1024]{1,0:T(8,128)(2,1)} reshape(bf16[64,40,256]{2,1,0:T(8,128)(2,1)} %all-to-all-done) | data formatting | bytes 2621440 | tf_op jit(solution)/shard_map/reshape;reshape | solution.py:92
  76.7 2.1 %constant_dynamic-slice_fusion = bf16[320,1024]{1,0:T(8,128)(2,1)} fusion(bf16[640,1024]{1,0:T(8,128)(2,1)} %reshape_reshape.13, s32[]{:T(128)S(6)} %select_n.66), kind=kLoop, calls=%fused_computation.51 | loop fusion | bytes 1310724 | tf_op jit(solution)/shard_map/dynamic_slice | solution.py:13
  78.8 4.8 %fusion.4 = bf16[320,2048]{1,0:T(8,128)(2,1)} fusion(bf16[1,1024,2048]{2,1,0:T(8,128)(2,1)} %param.12, bf16[640,1024]{1,0:T(8,128)(2,1)S(1)} %copy-done.1, s32[]{:T(128)S(6)} %select_n.67), kind=kOutput, calls=%fused_computation.4 | convolution fusion | flops 1342832640 | bytes 6160388 | tf_op jit(solution)/shard_map/dot_general | solution.py:99
  83.6 3.9 %fusion.7 = bf16[320,2048]{1,0:T(8,128)(2,1)S(1)} fusion(bf16[320,1024]{1,0:T(8,128)(2,1)} %constant_dynamic-slice_fusion, bf16[1,1024,2048]{2,1,0:T(8,128)(2,1)} %param.12), kind=kOutput, calls=%fused_computation.5 | convolution fusion | flops 1342832640 | bytes 6160384 | tf_op jit(solution)/shard_map/dot_general | solution.py:102
  87.5 1.7 add_convert_fusion
  89.3 0.7 collective-permute-start.5
  90.0 16.6 %collective-permute-done.5 = bf16[160,2048]{1,0:T(8,128)(2,1)S(1)} collective-permute-done((bf16[160,2048]{1,0:T(8,128)(2,1)S(1)}, bf16[160,2048]{1,0:T(8,128)(2,1)S(1)}, u32[]{:S(2)}, u32[]{:S(2)}) %collective-permute-start.5) | collective-permute-done | bytes 655392 | tf_op jit(solution)/shard_map/ppermute | solution.py:9
  106.9 0.7 collective-permute-start.6
  107.6 8.7 %collective-permute-done.6 = bf16[160,1024]{1,0:T(8,128)(2,1)S(1)} collective-permute-done((bf16[160,1024]{1,0:T(8,128)(2,1)S(1)}, bf16[160,1024]{1,0:T(8,128)(2,1)S(1)}, u32[]{:S(2)}, u32[]{:S(2)}) %collective-permute-start.6) | collective-permute-done | bytes 327712 | tf_op jit(solution)/shard_map/ppermute | solution.py:9
  116.3 0.3 collective-permute-start.7
  116.8 1.9 %collective-permute-done.7 = bf16[320,1024]{1,0:T(8,128)(2,1)S(1)} collective-permute-done((bf16[320,1024]{1,0:T(8,128)(2,1)S(1)}, bf16[320,1024]{1,0:T(8,128)(2,1)S(1)}, u32[]{:S(2)}, u32[]{:S(2)}) %collective-permute-start.7) | collective-permute-done | bytes 655392 | tf_op jit(solution)/shard_map/ppermute | solution.py:9
  118.8 2.6 %fusion.12 = bf16[640,1024]{1,0:T(8,128)(2,1)} fusion(bf16[640,1024]{1,0:T(8,128)(2,1)S(1)} %constant_dynamic-update-slice_fusion, bf16[1,1024,1024]{2,1,0:T(8,128)(2,1)S(1)} %copy-done), kind=kOutput, calls=%fused_computation.8 | convolution fusion | flops 1342832640 | bytes 4718592 | tf_op jit(solution)/shard_map/dot_general | solution.py:111
  121.4 3.4 %reshape_reshape.14 = bf16[64,40,256]{2,1,0:T(8,128)(2,1)} reshape(bf16[640,1024]{1,0:T(8,128)(2,1)} %fusion.12) | data formatting | bytes 2621440 | tf_op jit(solution)/shard_map/reshape;reshape | solution.py:51
  124.8 6.4 %all-to-all-start.1 = ((bf16[64,40,256]{2,1,0:T(8,128)(2,1)}), bf16[64,40,256]{2,1,0:T(8,128)(2,1)}, u32[]{:S(2)}, u32[]{:S(2)}) async-start(bf16[64,40,256]{2,1,0:T(8,128)(2,1)} %reshape_reshape.14), calls=%async_computation.1 | async-start | bytes 2621440 | tf_op jit(solution)/shard_map/all_to_all | solution.py:52
  131.4 35.7 %all-to-all-done.1 = bf16[64,40,256]{2,1,0:T(8,128)(2,1)} async-done(((bf16[64,40,256]{2,1,0:T(8,128)(2,1)}), bf16[64,40,256]{2,1,0:T(8,128)(2,1)}, u32[]{:S(2)}, u32[]{:S(2)}) %all-to-all-start.1) | async-done | bytes 1310752 | tf_op jit(solution)/shard_map/all_to_all | solution.py:52
  167.1 3.4 %reshape_reshape.15 = bf16[640,1024]{1,0:T(8,128)(2,1)} reshape(bf16[64,40,256]{2,1,0:T(8,128)(2,1)} %all-to-all-done.1) | data formatting | bytes 2621440 | tf_op jit(solution)/shard_map/reshape;reshape | solution.py:114
  170.5 1.9 %fusion.21 = f32[256,1024]{1,0:T(8,128)S(1)} fusion(bf16[640,1024]{1,0:T(8,128)(2,1)} %reshape_reshape.15, bf16[128,640]{0,1:T(8,128)(2,1)S(1)} %get-tuple-element.9, bf16[128,640]{0,1:T(8,128)(2,1)S(1)} %get-tuple-element.10), kind=kOutput, calls=%fused_computation.29 | convolution fusion | flops 336199680 | bytes 2686976 | tf_op jit(solution)/shard_map/dot_general | solution.py:117
  172.4 0.9 fusion.19
  (40 shorter events, 2.2 us)
Async XLA Ops:
  0.0 118.8 %copy-start = (bf16[1,1024,1024]{2,1,0:T(8,128)(2,1)S(1)}, bf16[1,1024,1024]{2,1,0:T(8,128)(2,1)}, u32[]{:S(2)}) copy-start(bf16[1,1024,1024]{2,1,0:T(8,128)(2,1)} %param.13) | copy-start | bytes 6291460
  0.0 1.4 copy-start.3
  1.3 2.1 %collective-permute-start = (bf16[128,2048]{1,0:T(8,128)(2,1)S(1)}, bf16[128,2048]{1,0:T(8,128)(2,1)}, u32[]{:S(2)}, u32[]{:S(2)}) collective-permute-start(bf16[128,2048]{1,0:T(8,128)(2,1)S(1)} %pad_maximum_fusion), channel_id=1, source_target_pairs={{0,1},{1,0},{2,3},{3,2},{4,5},{5,4},{6,7},{7,6},{8,9},{9,8},{10,11... | collective-permute-start | bytes 1572872 | tf_op jit(solution)/shard_map/ppermute | solution.py:9
  1.7 12.4 %copy-start.2 = (bf16[128,1024]{1,0:T(8,128)(2,1)S(1)}, bf16[128,1024]{1,0:T(8,128)(2,1)}, u32[]{:S(2)}) copy-start(bf16[128,1024]{1,0:T(8,128)(2,1)} %param.8) | copy-start | bytes 786436
  5.5 13.6 %copy-start.4 = (f32[1024]{0:T(1024)S(1)}, f32[1024]{0:T(1024)}, u32[]{:S(2)}) copy-start(f32[1024]{0:T(1024)} %param.9) | copy-start | bytes 12292
  5.5 8.6 %collective-permute-start.1 = (bf16[128,1024]{1,0:T(8,128)(2,1)}, bf16[128,1024]{1,0:T(8,128)(2,1)S(1)}, u32[]{:S(2)}, u32[]{:S(2)}) collective-permute-start(bf16[128,1024]{1,0:T(8,128)(2,1)} %get-tuple-element.15), channel_id=1, source_target_pairs={{0,2},{1,3},{2,0},{3,1},{4,6},{5,7},{6,4},{7,5},{8,10},{9,11},{10,... | collective-permute-start | bytes 786440 | tf_op jit(solution)/shard_map/ppermute | solution.py:9
  14.2 1.2 collective-permute-start.2
  15.5 3.6 %collective-permute-start.3 = (f32[128]{0:T(128)S(1)}, f32[128]{0:T(128)S(1)}, u32[]{:S(2)}, u32[]{:S(2)}) collective-permute-start(f32[128]{0:T(128)S(1)} %add.112), channel_id=1, source_target_pairs={{0,2},{1,3},{2,0},{3,1},{4,6},{5,7},{6,4},{7,5},{8,10},{9,11},{10,... | collective-permute-start | bytes 1544 | tf_op jit(solution)/shard_map/ppermute | solution.py:9
  24.1 49.3 %all-to-all-start = ((bf16[64,40,256]{2,1,0:T(8,128)(2,1)}), bf16[64,40,256]{2,1,0:T(8,128)(2,1)}, u32[]{:S(2)}, u32[]{:S(2)}) async-start(bf16[64,40,256]{2,1,0:T(8,128)(2,1)} %reshape_reshape.12), calls=%async_computation | async-start | bytes 2621440 | tf_op jit(solution)/shard_map/all_to_all | solution.py:52
  76.7 2.1 %copy-start.1 = (bf16[640,1024]{1,0:T(8,128)(2,1)S(1)}, bf16[640,1024]{1,0:T(8,128)(2,1)}, u32[]{:S(2)}) copy-start(bf16[640,1024]{1,0:T(8,128)(2,1)} %reshape_reshape.13) | copy-start | bytes 3932164
  83.6 3.9 %collective-permute-start.4 = (bf16[320,2048]{1,0:T(8,128)(2,1)}, bf16[320,2048]{1,0:T(8,128)(2,1)}, u32[]{:S(2)}, u32[]{:S(2)}) collective-permute-start(bf16[320,2048]{1,0:T(8,128)(2,1)} %fusion.4), channel_id=1, source_target_pairs={{0,1},{1,0},{2,3},{3,2},{4,5},{5,4},{6,7},{7,6},{8,9},{9,8},{10,11... | collective-permute-start | bytes 3932168 | tf_op jit(solution)/shard_map/ppermute | solution.py:9
  89.3 17.2 %collective-permute-start.5 = (bf16[160,2048]{1,0:T(8,128)(2,1)S(1)}, bf16[160,2048]{1,0:T(8,128)(2,1)S(1)}, u32[]{:S(2)}, u32[]{:S(2)}) collective-permute-start(bf16[160,2048]{1,0:T(8,128)(2,1)S(1)} %get-tuple-element.13), channel_id=1, source_target_pairs={{0,2},{1,3},{2,0},{3,1},{4,6},{5,7},{6,4},{7,5},{8,10},{9,11},{10,... | collective-permute-start | bytes 1966088 | tf_op jit(solution)/shard_map/ppermute | solution.py:9
  106.9 9.4 %collective-permute-start.6 = (bf16[160,1024]{1,0:T(8,128)(2,1)S(1)}, bf16[160,1024]{1,0:T(8,128)(2,1)S(1)}, u32[]{:S(2)}, u32[]{:S(2)}) collective-permute-start(bf16[160,1024]{1,0:T(8,128)(2,1)S(1)} %get-tuple-element.12), channel_id=1, source_target_pairs={{0,2},{1,3},{2,0},{3,1},{4,6},{5,7},{6,4},{7,5},{8,10},{9,11},{10,... | collective-permute-start | bytes 983048 | tf_op jit(solution)/shard_map/ppermute | solution.py:9
  116.3 2.4 %collective-permute-start.7 = (bf16[320,1024]{1,0:T(8,128)(2,1)S(1)}, bf16[320,1024]{1,0:T(8,128)(2,1)S(1)}, u32[]{:S(2)}, u32[]{:S(2)}) collective-permute-start(bf16[320,1024]{1,0:T(8,128)(2,1)S(1)} %constant_dynamic-update-slice_fusion.3), channel_id=1, source_target_pairs={{0,1},{1,0},{2,3},{3,2},{4,5},{5,4},{6,7},{7,6},{8,9},{9,8},{10,11... | collective-permute-start | bytes 1966088 | tf_op jit(solution)/shard_map/ppermute | solution.py:9
  124.8 6.4 %copy-start.5 = (f32[128,4]{0,1:T(4,128)S(1)}, f32[128,4]{0,1:T(4,128)}, u32[]{:S(2)}) copy-start(f32[128,4]{0,1:T(4,128)} %param.11) | copy-start | bytes 6148
  124.8 42.3 %all-to-all-start.1 = ((bf16[64,40,256]{2,1,0:T(8,128)(2,1)}), bf16[64,40,256]{2,1,0:T(8,128)(2,1)}, u32[]{:S(2)}, u32[]{:S(2)}) async-start(bf16[64,40,256]{2,1,0:T(8,128)(2,1)} %reshape_reshape.14), calls=%async_computation.1 | async-start | bytes 2621440 | tf_op jit(solution)/shard_map/all_to_all | solution.py:52

commit v9 on v7

--- a/solution.py
+++ b/solution.py
@@ -24,9 +24,10 @@
     received = _exchange(sent, 1)
     away = _slab(value, (3 - 2 * high + core - 1) * n, n, axis).astype(jnp.float32)
     away = away + _slab(received, (1 - high) * n, n, axis).astype(jnp.float32)
+    far = _exchange(away.astype(jnp.bfloat16), 2)
     home = _slab(value, (2 * high + core) * n, n, axis).astype(jnp.float32)
-    home = home + _slab(received, high * n, n, axis).astype(jnp.float32)
-    return home + _exchange(away.astype(jnp.bfloat16), 2).astype(jnp.float32)
+    home = lax.optimization_barrier(home + _slab(received, high * n, n, axis).astype(jnp.float32))
+    return home + far.astype(jnp.float32)
 
 
 def _all_gather_rows(value):

time: 165 us -> 174 us (1.055)
  local copies, waits for them, and re-layouts: 11 us -> 18 us
  matrix products: 13.9 us -> 15.8 us
    another operation x2, local copies, waits for them, and re-layouts: 3.31 us -> 6.78 us  [_exchange_rows(): packed = value.reshape(experts, slots * features // lanes, lanes)]
    another operation x1, local copies, waits for them, and re-layouts: 1.64 us -> 3.39 us  [_body(): flat_rows = in_rows.reshape(row_total, feature_local)]
    another operation x1, local copies, waits for them, and re-layouts: 1.64 us -> 3.39 us  [_body(): returned.reshape(expert_count * capacity, feature_local).astype(jnp.float32)]
where the time goes in v9:
time: 174 us; the launch traced here: 173 us
  waiting for transfers between devices  108 us (62%)
  starting transfers between devices  25.6 us (15%)
  local copies, waits for them, and re-layouts  18 us (10%)
  matrix products  15.8 us (9%)
  other arithmetic  6.05 us (3%)
    all_to_all x2, waiting for transfers between devices, _exchange_rows(): lax.all_to_all(packed, 'expert', split_axis=0, concat_axis=0, tiled=True)  70.6 us
    ppermute x8, waiting for transfers between devices, _exchange(): return lax.ppermute(value, 'tensor', [(j, j ^ flip) for j in range(size)])  37 us
    all_to_all x2, starting transfers between devices, _exchange_rows(): lax.all_to_all(packed, 'expert', split_axis=0, concat_axis=0, tiled=True)  20.8 us
    another operation x2, local copies, waits for them, and re-layouts, _exchange_rows(): packed = value.reshape(experts, slots * features // lanes, lanes)  6.78 us
    ppermute x8, starting transfers between devices, _exchange(): return lax.ppermute(value, 'tensor', [(j, j ^ flip) for j in range(size)])  4.8 us
    dot_general x1, matrix products, _body(): jnp.dot(away_rows, w_in[0], preferred_element_type=jnp.float32)  4.78 us
    dot_general x1, matrix products, _body(): jnp.dot(home_rows, w_in[0], preferred_element_type=jnp.float32)  3.91 us
  transfers between devices with their start and end apart: 10, of which 9 were waited for; matrix products, arithmetic and copies ran while one was open for 4% of the time, Pallas kernels for 0%

profile of v9, /device:TPU:32, one launch (start us, length us, event | category | flops | bytes accessed | tf_op | source)
XLA Modules:
  0.0 173.3 jit_solution(7512816446823827686)
XLA Ops:
  0.0 1.2 dynamic-slice_bitcast_fusion.1
  1.7 1.7 collective-permute-done
  3.4 2.1 %fusion.19 = (bf16[128,1024]{1,0:T(8,128)(2,1)}, f32[128,1024]{1,0:T(8,128)S(1)}) fusion(bf16[128,2048]{1,0:T(8,128)(2,1)} %collective-permute-done, s32[]{:T(128)S(6)} %select_n.64, bf16[1,128,4096]{2,1,0:T(8,128)(2,1)} %param.7, s32[]{:T(128)S(6)} %select_n.63, s32[]{:T(128)S(6)} %select_n.62, s32[]{:T(128)S(6)} %select_n.59), kind=kLoop, calls=%fused_computation.23 | loop fusion | flops 917504 | bytes 1835024 | tf_op jit(solution)/shard_map/convert_element_type | solution.py:27
  5.5 1.5 collective-permute-start.1
  7.1 1.2 reduce-window.6
  8.3 0.2 slice_reduce_fusion
  8.9 5.2 %collective-permute-done.1 = bf16[128,1024]{1,0:T(8,128)(2,1)S(1)} collective-permute-done((bf16[128,1024]{1,0:T(8,128)(2,1)}, bf16[128,1024]{1,0:T(8,128)(2,1)S(1)}, u32[]{:S(2)}, u32[]{:S(2)}) %collective-permute-start.1) | collective-permute-done | bytes 262176 | tf_op jit(solution)/shard_map/ppermute | solution.py:9
  14.3 1.1 collective-permute-done.2
  15.5 1.5 collective-permute-start.3
  17.1 1.9 %collective-permute-done.3 = f32[128]{0:T(128)S(1)} collective-permute-done((f32[128]{0:T(128)S(1)}, f32[128]{0:T(128)S(1)}, u32[]{:S(2)}, u32[]{:S(2)}) %collective-permute-start.3) | collective-permute-done | bytes 544 | tf_op jit(solution)/shard_map/ppermute | solution.py:9
  19.0 1.6 convolution_convert_fusion
  20.7 3.4 %reshape_reshape.12 = bf16[64,40,256]{2,1,0:T(8,128)(2,1)} reshape(bf16[640,1024]{1,0:T(8,128)(2,1)} %convolution_convert_fusion) | data formatting | bytes 2621440 | tf_op jit(solution)/shard_map/reshape;reshape | solution.py:51
  24.1 14.4 %all-to-all-start = ((bf16[64,40,256]{2,1,0:T(8,128)(2,1)}), bf16[64,40,256]{2,1,0:T(8,128)(2,1)}, u32[]{:S(2)}, u32[]{:S(2)}) async-start(bf16[64,40,256]{2,1,0:T(8,128)(2,1)} %reshape_reshape.12), calls=%async_computation | async-start | bytes 2621440 | tf_op jit(solution)/shard_map/all_to_all | solution.py:52
  38.5 34.9 %all-to-all-done = bf16[64,40,256]{2,1,0:T(8,128)(2,1)} async-done(((bf16[64,40,256]{2,1,0:T(8,128)(2,1)}), bf16[64,40,256]{2,1,0:T(8,128)(2,1)}, u32[]{:S(2)}, u32[]{:S(2)}) %all-to-all-start) | async-done | bytes 1310752 | tf_op jit(solution)/shard_map/all_to_all | solution.py:52
  73.4 3.4 %reshape_reshape.13 = bf16[640,1024]{1,0:T(8,128)(2,1)} reshape(bf16[64,40,256]{2,1,0:T(8,128)(2,1)} %all-to-all-done) | data formatting | bytes 2621440 | tf_op jit(solution)/shard_map/reshape;reshape | solution.py:92
  76.8 2.1 %constant_dynamic-slice_fusion = bf16[320,1024]{1,0:T(8,128)(2,1)} fusion(bf16[640,1024]{1,0:T(8,128)(2,1)} %reshape_reshape.13, s32[]{:T(128)S(6)} %select_n.66), kind=kLoop, calls=%fused_computation.43 | loop fusion | bytes 1310724 | tf_op jit(solution)/shard_map/dynamic_slice | solution.py:13
  78.8 4.8 %fusion.4 = bf16[320,2048]{1,0:T(8,128)(2,1)} fusion(bf16[1,1024,2048]{2,1,0:T(8,128)(2,1)} %param.12, bf16[640,1024]{1,0:T(8,128)(2,1)S(1)} %copy-done.1, s32[]{:T(128)S(6)} %select_n.67), kind=kOutput, calls=%fused_computation.4 | convolution fusion | flops 1342832640 | bytes 6160388 | tf_op jit(solution)/shard_map/dot_general | solution.py:99
  83.6 3.9 %fusion.7 = bf16[320,2048]{1,0:T(8,128)(2,1)S(1)} fusion(bf16[320,1024]{1,0:T(8,128)(2,1)} %constant_dynamic-slice_fusion, bf16[1,1024,2048]{2,1,0:T(8,128)(2,1)} %param.12), kind=kOutput, calls=%fused_computation.5 | convolution fusion | flops 1342832640 | bytes 6160384 | tf_op jit(solution)/shard_map/dot_general | solution.py:102
  87.5 1.7 add_convert_fusion
  89.3 0.7 collective-permute-start.5
  90.0 16.6 %collective-permute-done.5 = bf16[160,2048]{1,0:T(8,128)(2,1)S(1)} collective-permute-done((bf16[160,2048]{1,0:T(8,128)(2,1)S(1)}, bf16[160,2048]{1,0:T(8,128)(2,1)S(1)}, u32[]{:S(2)}, u32[]{:S(2)}) %collective-permute-start.5) | collective-permute-done | bytes 655392 | tf_op jit(solution)/shard_map/ppermute | solution.py:9
  106.7 0.2 constant_dynamic-update-slice_fusion.1
  106.9 0.7 collective-permute-start.6
  107.6 8.7 %collective-permute-done.6 = bf16[160,1024]{1,0:T(8,128)(2,1)S(1)} collective-permute-done((bf16[160,1024]{1,0:T(8,128)(2,1)S(1)}, bf16[160,1024]{1,0:T(8,128)(2,1)S(1)}, u32[]{:S(2)}, u32[]{:S(2)}) %collective-permute-start.6) | collective-permute-done | bytes 327712 | tf_op jit(solution)/shard_map/ppermute | solution.py:9
  116.3 0.3 collective-permute-start.7
  116.8 1.9 %collective-permute-done.7 = bf16[320,1024]{1,0:T(8,128)(2,1)S(1)} collective-permute-done((bf16[320,1024]{1,0:T(8,128)(2,1)S(1)}, bf16[320,1024]{1,0:T(8,128)(2,1)S(1)}, u32[]{:S(2)}, u32[]{:S(2)}) %collective-permute-start.7) | collective-permute-done | bytes 655392 | tf_op jit(solution)/shard_map/ppermute | solution.py:9
  118.8 2.6 %fusion.12 = bf16[640,1024]{1,0:T(8,128)(2,1)} fusion(bf16[640,1024]{1,0:T(8,128)(2,1)S(1)} %constant_dynamic-update-slice_fusion, bf16[1,1024,1024]{2,1,0:T(8,128)(2,1)S(1)} %copy-done), kind=kOutput, calls=%fused_computation.8 | convolution fusion | flops 1342832640 | bytes 4718592 | tf_op jit(solution)/shard_map/dot_general | solution.py:111
  121.4 3.4 %reshape_reshape.14 = bf16[64,40,256]{2,1,0:T(8,128)(2,1)} reshape(bf16[640,1024]{1,0:T(8,128)(2,1)} %fusion.12) | data formatting | bytes 2621440 | tf_op jit(solution)/shard_map/reshape;reshape | solution.py:51
  124.8 6.4 %all-to-all-start.1 = ((bf16[64,40,256]{2,1,0:T(8,128)(2,1)}), bf16[64,40,256]{2,1,0:T(8,128)(2,1)}, u32[]{:S(2)}, u32[]{:S(2)}) async-start(bf16[64,40,256]{2,1,0:T(8,128)(2,1)} %reshape_reshape.14), calls=%async_computation.1 | async-start | bytes 2621440 | tf_op jit(solution)/shard_map/all_to_all | solution.py:52
  131.3 35.7 %all-to-all-done.1 = bf16[64,40,256]{2,1,0:T(8,128)(2,1)} async-done(((bf16[64,40,256]{2,1,0:T(8,128)(2,1)}), bf16[64,40,256]{2,1,0:T(8,128)(2,1)}, u32[]{:S(2)}, u32[]{:S(2)}) %all-to-all-start.1) | async-done | bytes 1310752 | tf_op jit(solution)/shard_map/all_to_all | solution.py:52
  167.1 3.4 %reshape_reshape.15 = bf16[640,1024]{1,0:T(8,128)(2,1)} reshape(bf16[64,40,256]{2,1,0:T(8,128)(2,1)} %all-to-all-done.1) | data formatting | bytes 2621440 | tf_op jit(solution)/shard_map/reshape;reshape | solution.py:116
  170.5 2.9 %fusion.16 = bf16[128,1024]{1,0:T(8,128)(2,1)} fusion(f32[640,128]{1,0:T(8,128)S(1)} %select_reduce_fusion, bf16[640,1024]{1,0:T(8,128)(2,1)} %reshape_reshape.15, f32[128,1024]{1,0:T(8,128)S(1)} %get-tuple-element.14, bf16[128,1024]{1,0:T(8,128)(2,1)S(1)} %collective-permute-done.1, bf16[128,1024]{1,0:T(8,128)(2,1)S(1)} %copy-done.2), kind=kOutput, calls=%fused_computation.17 | convolution fusion | flops 1007419392 | bytes 2949120 | tf_op jit(solution)/shard_map/dot_general | solution.py:114
  (38 shorter events, 1.9 us)
Async XLA Ops:
  0.0 118.8 %copy-start = (bf16[1,1024,1024]{2,1,0:T(8,128)(2,1)S(1)}, bf16[1,1024,1024]{2,1,0:T(8,128)(2,1)}, u32[]{:S(2)}) copy-start(bf16[1,1024,1024]{2,1,0:T(8,128)(2,1)} %param.13) | copy-start | bytes 6291460
  0.0 1.4 copy-start.3
  1.3 2.1 %collective-permute-start = (bf16[128,2048]{1,0:T(8,128)(2,1)S(1)}, bf16[128,2048]{1,0:T(8,128)(2,1)}, u32[]{:S(2)}, u32[]{:S(2)}) collective-permute-start(bf16[128,2048]{1,0:T(8,128)(2,1)S(1)} %pad_maximum_fusion), channel_id=1, source_target_pairs={{0,1},{1,0},{2,3},{3,2},{4,5},{5,4},{6,7},{7,6},{8,9},{9,8},{10,11... | collective-permute-start | bytes 1572872 | tf_op jit(solution)/shard_map/ppermute | solution.py:9
  1.7 12.4 %copy-start.2 = (bf16[128,1024]{1,0:T(8,128)(2,1)S(1)}, bf16[128,1024]{1,0:T(8,128)(2,1)}, u32[]{:S(2)}) copy-start(bf16[128,1024]{1,0:T(8,128)(2,1)} %param.8) | copy-start | bytes 786436
  5.5 13.6 %copy-start.4 = (f32[1024]{0:T(1024)S(1)}, f32[1024]{0:T(1024)}, u32[]{:S(2)}) copy-start(f32[1024]{0:T(1024)} %param.9) | copy-start | bytes 12292
  5.5 8.6 %collective-permute-start.1 = (bf16[128,1024]{1,0:T(8,128)(2,1)}, bf16[128,1024]{1,0:T(8,128)(2,1)S(1)}, u32[]{:S(2)}, u32[]{:S(2)}) collective-permute-start(bf16[128,1024]{1,0:T(8,128)(2,1)} %get-tuple-element.13), channel_id=1, source_target_pairs={{0,2},{1,3},{2,0},{3,1},{4,6},{5,7},{6,4},{7,5},{8,10},{9,11},{10,... | collective-permute-start | bytes 786440 | tf_op jit(solution)/shard_map/ppermute | solution.py:9
  14.2 1.2 collective-permute-start.2
  15.5 3.6 %collective-permute-start.3 = (f32[128]{0:T(128)S(1)}, f32[128]{0:T(128)S(1)}, u32[]{:S(2)}, u32[]{:S(2)}) collective-permute-start(f32[128]{0:T(128)S(1)} %add.109), channel_id=1, source_target_pairs={{0,2},{1,3},{2,0},{3,1},{4,6},{5,7},{6,4},{7,5},{8,10},{9,11},{10,... | collective-permute-start | bytes 1544 | tf_op jit(solution)/shard_map/ppermute | solution.py:9
  24.1 49.3 %all-to-all-start = ((bf16[64,40,256]{2,1,0:T(8,128)(2,1)}), bf16[64,40,256]{2,1,0:T(8,128)(2,1)}, u32[]{:S(2)}, u32[]{:S(2)}) async-start(bf16[64,40,256]{2,1,0:T(8,128)(2,1)} %reshape_reshape.12), calls=%async_computation | async-start | bytes 2621440 | tf_op jit(solution)/shard_map/all_to_all | solution.py:52
  76.7 2.1 %copy-start.1 = (bf16[640,1024]{1,0:T(8,128)(2,1)S(1)}, bf16[640,1024]{1,0:T(8,128)(2,1)}, u32[]{:S(2)}) copy-start(bf16[640,1024]{1,0:T(8,128)(2,1)} %reshape_reshape.13) | copy-start | bytes 3932164
  83.6 3.9 %collective-permute-start.4 = (bf16[320,2048]{1,0:T(8,128)(2,1)}, bf16[320,2048]{1,0:T(8,128)(2,1)}, u32[]{:S(2)}, u32[]{:S(2)}) collective-permute-start(bf16[320,2048]{1,0:T(8,128)(2,1)} %fusion.4), channel_id=1, source_target_pairs={{0,1},{1,0},{2,3},{3,2},{4,5},{5,4},{6,7},{7,6},{8,9},{9,8},{10,11... | collective-permute-start | bytes 3932168 | tf_op jit(solution)/shard_map/ppermute | solution.py:9
  89.3 17.2 %collective-permute-start.5 = (bf16[160,2048]{1,0:T(8,128)(2,1)S(1)}, bf16[160,2048]{1,0:T(8,128)(2,1)S(1)}, u32[]{:S(2)}, u32[]{:S(2)}) collective-permute-start(bf16[160,2048]{1,0:T(8,128)(2,1)S(1)} %get-tuple-element.11), channel_id=1, source_target_pairs={{0,2},{1,3},{2,0},{3,1},{4,6},{5,7},{6,4},{7,5},{8,10},{9,11},{10,... | collective-permute-start | bytes 1966088 | tf_op jit(solution)/shard_map/ppermute | solution.py:9
  106.9 9.4 %collective-permute-start.6 = (bf16[160,1024]{1,0:T(8,128)(2,1)S(1)}, bf16[160,1024]{1,0:T(8,128)(2,1)S(1)}, u32[]{:S(2)}, u32[]{:S(2)}) collective-permute-start(bf16[160,1024]{1,0:T(8,128)(2,1)S(1)} %get-tuple-element.10), channel_id=1, source_target_pairs={{0,2},{1,3},{2,0},{3,1},{4,6},{5,7},{6,4},{7,5},{8,10},{9,11},{10,... | collective-permute-start | bytes 983048 | tf_op jit(solution)/shard_map/ppermute | solution.py:9
  116.3 2.4 %collective-permute-start.7 = (bf16[320,1024]{1,0:T(8,128)(2,1)S(1)}, bf16[320,1024]{1,0:T(8,128)(2,1)S(1)}, u32[]{:S(2)}, u32[]{:S(2)}) collective-permute-start(bf16[320,1024]{1,0:T(8,128)(2,1)S(1)} %constant_dynamic-update-slice_fusion.3), channel_id=1, source_target_pairs={{0,1},{1,0},{2,3},{3,2},{4,5},{5,4},{6,7},{7,6},{8,9},{9,8},{10,11... | collective-permute-start | bytes 1966088 | tf_op jit(solution)/shard_map/ppermute | solution.py:9
  124.8 6.4 %copy-start.5 = (f32[128,4]{0,1:T(4,128)S(1)}, f32[128,4]{0,1:T(4,128)}, u32[]{:S(2)}) copy-start(f32[128,4]{0,1:T(4,128)} %param.11) | copy-start | bytes 6148
  124.8 42.3 %all-to-all-start.1 = ((bf16[64,40,256]{2,1,0:T(8,128)(2,1)}), bf16[64,40,256]{2,1,0:T(8,128)(2,1)}, u32[]{:S(2)}, u32[]{:S(2)}) async-start(bf16[64,40,256]{2,1,0:T(8,128)(2,1)} %reshape_reshape.14), calls=%async_computation.1 | async-start | bytes 2621440 | tf_op jit(solution)/shard_map/all_to_all | solution.py:52

commit v10 on v7

--- a/solution.py
+++ b/solution.py
@@ -44,12 +44,9 @@
 
 def _exchange_rows(value):
     experts, slots, features = value.shape
-    lanes = features
-    while lanes > 128 and (slots * features // lanes) % 8 != 0:
-        lanes //= 2
+    lanes = 128
     packed = value.reshape(experts, slots * features // lanes, lanes)
-    moved = lax.all_to_all(packed, "expert", split_axis=0, concat_axis=0, tiled=True)
-    return moved.reshape(experts, slots, features)
+    return lax.all_to_all(packed, "expert", split_axis=0, concat_axis=0, tiled=True)
 
 
 def _psum(value):
@@ -85,19 +82,19 @@
     sent_rows = sent_rows.astype(jnp.bfloat16).reshape(expert_count, capacity, feature_local)
     weights_table = jnp.sum(jnp.where(matches, route_weight[None, :, :], 0.0), axis=2).T
     in_rows = _exchange_rows(sent_rows)
-    source_count = in_rows.shape[0]
-    item_count = in_rows.shape[1]
+    source_count = sent_rows.shape[0]
+    item_count = sent_rows.shape[1]
     row_total = source_count * item_count
-    flat_rows = in_rows.reshape(row_total, feature_local)
     t = lax.axis_index("tensor")
     core = t % 2
     high = t // 2
     block = row_total // 4
-    away_rows = _slab(flat_rows, 2 * (1 - core) * block, 2 * block, 0)
-    home_rows = _slab(flat_rows, 2 * core * block, 2 * block, 0)
+    sources = source_count // 2
+    away_rows = _slab(in_rows, (1 - core) * sources, sources, 0).reshape(2 * block, feature_local)
     sent = jnp.dot(away_rows, w_in[0], preferred_element_type=jnp.float32).astype(jnp.bfloat16)
-    home_rows, sent = lax.optimization_barrier((home_rows, sent))
+    in_rows, sent = lax.optimization_barrier((in_rows, sent))
     received = _exchange(sent, 1)
+    home_rows = _slab(in_rows, core * sources, sources, 0).reshape(2 * block, feature_local)
     kept = jnp.dot(home_rows, w_in[0], preferred_element_type=jnp.float32).astype(jnp.bfloat16)
     away = _slab(kept, (1 - high) * block, block, 0).astype(jnp.float32)
     away = away + _slab(received, (1 - high) * block, block, 0).astype(jnp.float32)
@@ -109,7 +106,7 @@
     hidden = _all_gather_rows(hidden)
     produced = jnp.dot(hidden, w_down[0], preferred_element_type=jnp.float32).astype(jnp.bfloat16)
     results = produced.reshape(source_count, item_count, feature_local)
-    returned = _exchange_rows(results)
+    returned = _exchange_rows(results).reshape(expert_count, capacity, feature_local)
     routed = jnp.dot(
         weights_table,
         returned.reshape(expert_count * capacity, feature_local).astype(jnp.float32),

time: 165 us -> 168 us (1.018)
    reshape x0 -> x2, local copies, waits for them, and re-layouts: none -> 3.51 us  [the longest x1 2.14 us: _body(): _slab(in_rows, (1 - core) * sources, sources, 0)]
  transfers between devices with their start and end apart: 10 -> 10, of which waited for: 9 -> 9; matrix products, arithmetic and copies ran while one was open for 4% -> 6% of each run, Pallas kernels for 0% -> 0%
where the time goes in v10:
time: 168 us; the launch traced here: 167 us
  waiting for transfers between devices  107 us (64%)
  starting transfers between devices  25.2 us (15%)
  matrix products  13.9 us (8%)
  local copies, waits for them, and re-layouts  11.9 us (7%)
  other arithmetic  8.39 us (5%)
    all_to_all x2, waiting for transfers between devices, _exchange_rows(): lax.all_to_all(packed, 'expert', split_axis=0, concat_axis=0, tiled=True)  70 us
    ppermute x8, waiting for transfers between devices, _exchange(): return lax.ppermute(value, 'tensor', [(j, j ^ flip) for j in range(size)])  37.4 us
    all_to_all x2, starting transfers between devices, _exchange_rows(): lax.all_to_all(packed, 'expert', split_axis=0, concat_axis=0, tiled=True)  20.5 us
    dot_general x1, matrix products, _body(): jnp.dot(away_rows, w_in[0], preferred_element_type=jnp.float32)  4.98 us
    ppermute x8, starting transfers between devices, _exchange(): return lax.ppermute(value, 'tensor', [(j, j ^ flip) for j in range(size)])  4.71 us
    dot_general x1, matrix products, _body(): jnp.dot(home_rows, w_in[0], preferred_element_type=jnp.float32)  3.71 us
  transfers between devices with their start and end apart: 10, of which 9 were waited for; matrix products, arithmetic and copies ran while one was open for 6% of the time, Pallas kernels for 0%

profile of v10, /device:TPU:32, one launch (start us, length us, event | category | flops | bytes accessed | tf_op | source)
XLA Modules:
  0.0 167.0 jit_solution(4656733389000737688)
XLA Ops:
  0.0 1.2 dynamic-slice_bitcast_fusion.1
  1.3 0.8 pad_maximum_fusion
  2.3 2.0 %collective-permute-done = bf16[128,2048]{1,0:T(8,128)(2,1)} collective-permute-done((bf16[128,2048]{1,0:T(8,128)(2,1)}, bf16[128,2048]{1,0:T(8,128)(2,1)}, u32[]{:S(2)}, u32[]{:S(2)}) %collective-permute-start) | collective-permute-done | bytes 524320 | tf_op jit(solution)/shard_map/ppermute | solution.py:9
  4.3 1.7 %fusion.18 = bf16[128,1024]{1,0:T(8,128)(2,1)} fusion(bf16[128,2048]{1,0:T(8,128)(2,1)} %collective-permute-done, s32[]{:T(128)S(6)} %select_n.68, bf16[1,128,4096]{2,1,0:T(8,128)(2,1)S(1)} %copy-done.2, s32[]{:T(128)S(6)} %select_n.67), kind=kLoop, calls=%fused_computation.22 | loop fusion | flops 524288 | bytes 786440 | tf_op jit(solution)/shard_map/convert_element_type | solution.py:29
  6.1 1.5 collective-permute-start.1
  7.7 1.2 reduce-window.6
  9.5 5.3 %collective-permute-done.1 = bf16[128,1024]{1,0:T(8,128)(2,1)} collective-permute-done((bf16[128,1024]{1,0:T(8,128)(2,1)}, bf16[128,1024]{1,0:T(8,128)(2,1)}, u32[]{:S(2)}, u32[]{:S(2)}) %collective-permute-start.1) | collective-permute-done | bytes 262176 | tf_op jit(solution)/shard_map/ppermute | solution.py:9
  14.7 1.3 multiply_reduce_fusion
  16.2 1.1 collective-permute-done.2
  17.3 1.5 collective-permute-start.3
  19.0 1.9 %collective-permute-done.3 = f32[128]{0:T(128)S(1)} collective-permute-done((f32[128]{0:T(128)S(1)}, f32[128]{0:T(128)S(1)}, u32[]{:S(2)}, u32[]{:S(2)}) %collective-permute-start.3) | collective-permute-done | bytes 544 | tf_op jit(solution)/shard_map/ppermute | solution.py:9
  21.5 1.4 reshape_reshape.9
  22.9 14.2 %all-to-all-start = ((bf16[64,80,128]{2,1,0:T(8,128)(2,1)}), bf16[64,80,128]{2,1,0:T(8,128)(2,1)S(1)}, u32[]{:S(2)}, u32[]{:S(2)}) async-start(bf16[64,80,128]{2,1,0:T(8,128)(2,1)} %reshape_reshape.9), calls=%async_computation | async-start | bytes 2621440 | tf_op jit(solution)/shard_map/all_to_all | solution.py:49
  37.2 34.9 %all-to-all-done = bf16[64,80,128]{2,1,0:T(8,128)(2,1)S(1)} async-done(((bf16[64,80,128]{2,1,0:T(8,128)(2,1)}), bf16[64,80,128]{2,1,0:T(8,128)(2,1)S(1)}, u32[]{:S(2)}, u32[]{:S(2)}) %all-to-all-start) | async-done | bytes 1310752 | tf_op jit(solution)/shard_map/all_to_all | solution.py:49
  72.1 0.9 constant_dynamic-slice_fusion.1
  73.0 2.1 %reshape.42 = bf16[320,1024]{1,0:T(8,128)(2,1)} reshape(bf16[32,80,128]{2,1,0:T(8,128)(2,1)} %constant_dynamic-slice_fusion.1) | data formatting | bytes 1310720 | tf_op jit(solution)/shard_map/reshape | solution.py:93
  75.1 5.0 %fusion.4 = bf16[320,2048]{1,0:T(8,128)(2,1)} fusion(bf16[320,1024]{1,0:T(8,128)(2,1)} %reshape.42, bf16[1,1024,2048]{2,1,0:T(8,128)(2,1)} %param.12), kind=kOutput, calls=%fused_computation.4 | convolution fusion | flops 1342832640 | bytes 6160384 | tf_op jit(solution)/shard_map/dot_general | solution.py:94
  80.1 0.9 constant_dynamic-slice_fusion
  81.0 1.4 reshape.43
  82.4 3.7 %fusion.7 = bf16[320,2048]{1,0:T(8,128)(2,1)S(1)} fusion(bf16[320,1024]{1,0:T(8,128)(2,1)S(1)} %reshape.43, bf16[1,1024,2048]{2,1,0:T(8,128)(2,1)} %param.12), kind=kOutput, calls=%fused_computation.5 | convolution fusion | flops 1342832640 | bytes 6160384 | tf_op jit(solution)/shard_map/dot_general | solution.py:98
  86.1 1.7 %add_convert_fusion = (bf16[160,2048]{1,0:T(8,128)(2,1)S(1)}, f32[160,2048]{1,0:T(8,128)S(1)}) fusion(bf16[320,2048]{1,0:T(8,128)(2,1)} %collective-permute-done.4, s32[]{:T(128)S(6)} %select_n.73, bf16[320,2048]{1,0:T(8,128)(2,1)S(1)} %fusion.7, s32[]{:T(128)S(6)} %select_n.72), kind=kLoop, calls=%fused_computation.11 | loop fusion | flops 2293760 | bytes 4587528 | tf_op jit(solution)/shard_map/convert_element_type | solution.py:101
  87.9 0.7 collective-permute-start.5
  88.5 16.6 %collective-permute-done.5 = bf16[160,2048]{1,0:T(8,128)(2,1)S(1)} collective-permute-done((bf16[160,2048]{1,0:T(8,128)(2,1)S(1)}, bf16[160,2048]{1,0:T(8,128)(2,1)S(1)}, u32[]{:S(2)}, u32[]{:S(2)}) %collective-permute-start.5) | collective-permute-done | bytes 655392 | tf_op jit(solution)/shard_map/ppermute | solution.py:9
  106.2 8.7 %collective-permute-done.6 = bf16[160,1024]{1,0:T(8,128)(2,1)S(1)} collective-permute-done((bf16[160,1024]{1,0:T(8,128)(2,1)S(1)}, bf16[160,1024]{1,0:T(8,128)(2,1)S(1)}, u32[]{:S(2)}, u32[]{:S(2)}) %collective-permute-start.6) | collective-permute-done | bytes 327712 | tf_op jit(solution)/shard_map/ppermute | solution.py:9
  115.4 1.8 %collective-permute-done.7 = bf16[320,1024]{1,0:T(8,128)(2,1)S(1)} collective-permute-done((bf16[320,1024]{1,0:T(8,128)(2,1)S(1)}, bf16[320,1024]{1,0:T(8,128)(2,1)S(1)}, u32[]{:S(2)}, u32[]{:S(2)}) %collective-permute-start.7) | collective-permute-done | bytes 655392 | tf_op jit(solution)/shard_map/ppermute | solution.py:9
  117.3 1.5 fusion.12
  118.9 1.4 reshape_reshape.10
  120.3 6.2 %all-to-all-start.1 = ((bf16[64,80,128]{2,1,0:T(8,128)(2,1)}), bf16[64,80,128]{2,1,0:T(8,128)(2,1)S(1)}, u32[]{:S(2)}, u32[]{:S(2)}) async-start(bf16[64,80,128]{2,1,0:T(8,128)(2,1)} %reshape_reshape.10), calls=%async_computation.1 | async-start | bytes 2621440 | tf_op jit(solution)/shard_map/all_to_all | solution.py:49
  126.6 0.9 select_reduce_fusion
  127.5 35.1 %all-to-all-done.1 = bf16[64,80,128]{2,1,0:T(8,128)(2,1)S(1)} async-done(((bf16[64,80,128]{2,1,0:T(8,128)(2,1)}), bf16[64,80,128]{2,1,0:T(8,128)(2,1)S(1)}, u32[]{:S(2)}, u32[]{:S(2)}) %all-to-all-start.1) | async-done | bytes 1310752 | tf_op jit(solution)/shard_map/all_to_all | solution.py:49
  162.5 1.4 reshape_reshape.11
  163.9 3.1 %fusion.16 = bf16[128,1024]{1,0:T(8,128)(2,1)} fusion(f32[128,1024]{1,0:T(8,128)} %copy-done.1, f32[640,128]{1,0:T(8,128)} %select_reduce_fusion, bf16[640,1024]{1,0:T(8,128)(2,1)} %reshape_reshape.11), kind=kOutput, calls=%fused_computation.17 | convolution fusion | flops 1006895104 | bytes 2424832 | tf_op jit(solution)/shard_map/dot_general | solution.py:110
  (40 shorter events, 3.4 us)
Async XLA Ops:
  0.0 117.3 %copy-start = (bf16[1,1024,1024]{2,1,0:T(8,128)(2,1)S(1)}, bf16[1,1024,1024]{2,1,0:T(8,128)(2,1)}, u32[]{:S(2)}) copy-start(bf16[1,1024,1024]{2,1,0:T(8,128)(2,1)} %param.13) | copy-start | bytes 6291460
  0.0 4.3 %copy-start.2 = (bf16[1,128,4096]{2,1,0:T(8,128)(2,1)S(1)}, bf16[1,128,4096]{2,1,0:T(8,128)(2,1)}, u32[]{:S(2)}) copy-start(bf16[1,128,4096]{2,1,0:T(8,128)(2,1)} %param.7) | copy-start | bytes 3145732
  0.0 2.1 %copy-start.3 = (s32[128,4]{0,1:T(4,128)S(1)}, s32[128,4]{0,1:T(4,128)}, u32[]{:S(2)}) copy-start(s32[128,4]{0,1:T(4,128)} %param.10) | copy-start | bytes 6148
  2.1 2.3 %collective-permute-start = (bf16[128,2048]{1,0:T(8,128)(2,1)}, bf16[128,2048]{1,0:T(8,128)(2,1)}, u32[]{:S(2)}, u32[]{:S(2)}) collective-permute-start(bf16[128,2048]{1,0:T(8,128)(2,1)} %pad_maximum_fusion), channel_id=1, source_target_pairs={{0,1},{1,0},{2,3},{3,2},{4,5},{5,4},{6,7},{7,6},{8,9},{9,8},{10,11... | collective-permute-start | bytes 1572872 | tf_op jit(solution)/shard_map/ppermute | solution.py:9
  6.1 14.8 %copy-start.4 = (f32[1024]{0:T(1024)S(1)}, f32[1024]{0:T(1024)}, u32[]{:S(2)}) copy-start(f32[1024]{0:T(1024)} %param.9) | copy-start | bytes 12292
  6.1 8.7 %collective-permute-start.1 = (bf16[128,1024]{1,0:T(8,128)(2,1)}, bf16[128,1024]{1,0:T(8,128)(2,1)}, u32[]{:S(2)}, u32[]{:S(2)}) collective-permute-start(bf16[128,1024]{1,0:T(8,128)(2,1)} %fusion.18), channel_id=1, source_target_pairs={{0,2},{1,3},{2,0},{3,1},{4,6},{5,7},{6,4},{7,5},{8,10},{9,11},{10,... | collective-permute-start | bytes 786440 | tf_op jit(solution)/shard_map/ppermute | solution.py:9
  16.1 4.8 %copy-start.1 = (f32[128,1024]{1,0:T(8,128)}, f32[128,1024]{1,0:T(8,128)S(1)}, u32[]{:S(2)}) copy-start(f32[128,1024]{1,0:T(8,128)S(1)} %get-tuple-element.12) | copy-start | bytes 1572868
  16.1 1.2 collective-permute-start.2
  17.3 3.6 %collective-permute-start.3 = (f32[128]{0:T(128)S(1)}, f32[128]{0:T(128)S(1)}, u32[]{:S(2)}, u32[]{:S(2)}) collective-permute-start(f32[128]{0:T(128)S(1)} %add.113), channel_id=1, source_target_pairs={{0,2},{1,3},{2,0},{3,1},{4,6},{5,7},{6,4},{7,5},{8,10},{9,11},{10,... | collective-permute-start | bytes 1544 | tf_op jit(solution)/shard_map/ppermute | solution.py:9
  22.9 49.2 %all-to-all-start = ((bf16[64,80,128]{2,1,0:T(8,128)(2,1)}), bf16[64,80,128]{2,1,0:T(8,128)(2,1)S(1)}, u32[]{:S(2)}, u32[]{:S(2)}) async-start(bf16[64,80,128]{2,1,0:T(8,128)(2,1)} %reshape_reshape.9), calls=%async_computation | async-start | bytes 2621440 | tf_op jit(solution)/shard_map/all_to_all | solution.py:49
  80.1 6.0 %collective-permute-start.4 = (bf16[320,2048]{1,0:T(8,128)(2,1)}, bf16[320,2048]{1,0:T(8,128)(2,1)}, u32[]{:S(2)}, u32[]{:S(2)}) collective-permute-start(bf16[320,2048]{1,0:T(8,128)(2,1)} %fusion.4), channel_id=1, source_target_pairs={{0,1},{1,0},{2,3},{3,2},{4,5},{5,4},{6,7},{7,6},{8,9},{9,8},{10,11... | collective-permute-start | bytes 3932168 | tf_op jit(solution)/shard_map/ppermute | solution.py:9
  87.9 17.2 %collective-permute-start.5 = (bf16[160,2048]{1,0:T(8,128)(2,1)S(1)}, bf16[160,2048]{1,0:T(8,128)(2,1)S(1)}, u32[]{:S(2)}, u32[]{:S(2)}) collective-permute-start(bf16[160,2048]{1,0:T(8,128)(2,1)S(1)} %get-tuple-element.13), channel_id=1, source_target_pairs={{0,2},{1,3},{2,0},{3,1},{4,6},{5,7},{6,4},{7,5},{8,10},{9,11},{10,... | collective-permute-start | bytes 1966088 | tf_op jit(solution)/shard_map/ppermute | solution.py:9
  105.5 9.4 %collective-permute-start.6 = (bf16[160,1024]{1,0:T(8,128)(2,1)S(1)}, bf16[160,1024]{1,0:T(8,128)(2,1)S(1)}, u32[]{:S(2)}, u32[]{:S(2)}) collective-permute-start(bf16[160,1024]{1,0:T(8,128)(2,1)S(1)} %get-tuple-element.10), channel_id=1, source_target_pairs={{0,2},{1,3},{2,0},{3,1},{4,6},{5,7},{6,4},{7,5},{8,10},{9,11},{10,... | collective-permute-start | bytes 983048 | tf_op jit(solution)/shard_map/ppermute | solution.py:9
  114.9 2.4 %collective-permute-start.7 = (bf16[320,1024]{1,0:T(8,128)(2,1)S(1)}, bf16[320,1024]{1,0:T(8,128)(2,1)S(1)}, u32[]{:S(2)}, u32[]{:S(2)}) collective-permute-start(bf16[320,1024]{1,0:T(8,128)(2,1)S(1)} %constant_dynamic-update-slice_fusion), channel_id=1, source_target_pairs={{0,1},{1,0},{2,3},{3,2},{4,5},{5,4},{6,7},{7,6},{8,9},{9,8},{10,11... | collective-permute-start | bytes 1966088 | tf_op jit(solution)/shard_map/ppermute | solution.py:9
  120.3 6.2 %copy-start.5 = (f32[128,4]{0,1:T(4,128)S(1)}, f32[128,4]{0,1:T(4,128)}, u32[]{:S(2)}) copy-start(f32[128,4]{0,1:T(4,128)} %param.11) | copy-start | bytes 6148
  120.3 42.2 %all-to-all-start.1 = ((bf16[64,80,128]{2,1,0:T(8,128)(2,1)}), bf16[64,80,128]{2,1,0:T(8,128)(2,1)S(1)}, u32[]{:S(2)}, u32[]{:S(2)}) async-start(bf16[64,80,128]{2,1,0:T(8,128)(2,1)} %reshape_reshape.10), calls=%async_computation.1 | async-start | bytes 2621440 | tf_op jit(solution)/shard_map/all_to_all | solution.py:49

commit v11 on v7

--- a/solution.py
+++ b/solution.py
@@ -18,14 +18,11 @@
     core = t % 2
     high = t // 2
     n = value.shape[axis] // 4
-    sent = jnp.concatenate(
-        [_slab(value, (1 - core) * n, n, axis), _slab(value, (3 - core) * n, n, axis)], axis
-    ).astype(jnp.bfloat16)
-    received = _exchange(sent, 1)
-    away = _slab(value, (3 - 2 * high + core - 1) * n, n, axis).astype(jnp.float32)
-    away = away + _slab(received, (1 - high) * n, n, axis).astype(jnp.float32)
-    home = _slab(value, (2 * high + core) * n, n, axis).astype(jnp.float32)
-    home = home + _slab(received, high * n, n, axis).astype(jnp.float32)
+    first = _exchange(_slab(value, (1 - core) * n, n, axis).astype(jnp.bfloat16), 1)
+    second = _exchange(_slab(value, (3 - core) * n, n, axis).astype(jnp.bfloat16), 1)
+    away_in, home_in = jnp.where(high == 0, second, first), jnp.where(high == 0, first, second)
+    away = _slab(value, (3 - 2 * high + core - 1) * n, n, axis).astype(jnp.float32) + away_in.astype(jnp.float32)
+    home = _slab(value, (2 * high + core) * n, n, axis).astype(jnp.float32) + home_in.astype(jnp.float32)
     return home + _exchange(away.astype(jnp.bfloat16), 2).astype(jnp.float32)
 
 
@@ -44,9 +41,7 @@
 
 def _exchange_rows(value):
     experts, slots, features = value.shape
-    lanes = features
-    while lanes > 128 and (slots * features // lanes) % 8 != 0:
-        lanes //= 2
+    lanes = 128
     packed = value.reshape(experts, slots * features // lanes, lanes)
     moved = lax.all_to_all(packed, "expert", split_axis=0, concat_axis=0, tiled=True)
     return moved.reshape(experts, slots, features)

time: 165 us -> 165 us (level)
  starting transfers between devices: 25.2 us -> 23 us
    ppermute x8 -> x9, starting transfers between devices: 4.71 us -> 2.51 us  [_exchange(): return lax.ppermute(value, 'tensor', [(j, j ^ flip) for j in range(size)])]
    ppermute x8 -> x9, waiting for transfers between devices: 37.4 us -> 37.1 us  [_exchange(): return lax.ppermute(value, 'tensor', [(j, j ^ flip) for j in range(size)])]
  transfers between devices with their start and end apart: 10 -> 11, of which waited for: 9 -> 10; matrix products, arithmetic and copies ran while one was open for 4% -> 6% of each run, Pallas kernels for 0% -> 0%
where the time goes in v11:
time: 165 us
  waiting for transfers between devices  107 us (65%)
  starting transfers between devices  23 us (14%)
  matrix products  14.6 us (9%)
  local copies, waits for them, and re-layouts  11.6 us (7%)
  other arithmetic  8.12 us (5%)
    all_to_all x2, waiting for transfers between devices, _exchange_rows(): lax.all_to_all(packed, 'expert', split_axis=0, concat_axis=0, tiled=True)  70 us
    ppermute x9, waiting for transfers between devices, _exchange(): return lax.ppermute(value, 'tensor', [(j, j ^ flip) for j in range(size)])  37.1 us
    all_to_all x2, starting transfers between devices, _exchange_rows(): lax.all_to_all(packed, 'expert', split_axis=0, concat_axis=0, tiled=True)  20.5 us
    dot_general x1, matrix products, _body(): jnp.dot(away_rows, w_in[0], preferred_element_type=jnp.float32)  4.78 us
    dynamic_slice x2, local copies, waits for them, and re-layouts, _slab(): return lax.dynamic_slice_in_dim(value, start, size, axis=axis)  4.13 us
    dot_general x1, matrix products, _body(): jnp.dot(home_rows, w_in[0], preferred_element_type=jnp.float32)  3.91 us
  transfers between devices with their start and end apart: 11, of which 10 were waited for; matrix products, arithmetic and copies ran while one was open for 6% of the time, Pallas kernels for 0%

profile of v11, /device:TPU:32, one launch (start us, length us, event | category | flops | bytes accessed | tf_op | source)
XLA Modules:
  0.0 164.6 jit_solution(14598873191390788621)
XLA Ops:
  0.0 2.0 %dynamic-slice_bitcast_fusion.1 = (bf16[128,1024]{1,0:T(8,128)(2,1)}, bf16[128,1024]{1,0:T(8,128)(2,1)}) fusion(bf16[1,128,4096]{2,1,0:T(8,128)(2,1)} %param.7, s32[]{:T(128)S(6)} %select_n.67, s32[]{:T(128)S(6)} %select_n.68), kind=kLoop, calls=%fused_computation.31 | loop fusion | bytes 1048584 | tf_op jit(solution)/shard_map/dynamic_slice | solution.py:13
  2.0 0.5 collective-permute-start.1
  2.5 0.8 copy.22
  3.8 0.5 collective-permute-done.1
  4.3 1.8 %fusion.19 = bf16[128,1024]{1,0:T(8,128)(2,1)} fusion(bf16[128,1024]{1,0:T(8,128)(2,1)} %collective-permute-done.1, bf16[128,1024]{1,0:T(8,128)(2,1)S(1)} %collective-permute-done, bf16[1,128,4096]{2,1,0:T(8,128)(2,1)S(1)} %copy-done.3, s32[]{:T(128)S(6)} %select_n.70, pred[]{:T(512)S(6)} %eq.46), kind=kLoop, calls=%fused_computation.22 | loop fusion | flops 655360 | bytes 1048581 | tf_op jit(solution)/shard_map/convert_element_type | solution.py:26
  6.1 0.5 collective-permute-start.2
  6.6 0.7 fusion.27
  7.4 2.4 %reduce-window.6 = s32[64,4,128]{2,0,1:T(8,128)S(1)} reduce-window(s32[64,4,128]{2,0,1:T(8,128)} %fusion.27, s32[]{:T(128)} %constant.60.clone.1), window={size=1x1x128 pad=0_0x0_0x127_0}, to_apply=%region_0.1 | reduce-window | flops 4161536 | bytes 262148 | tf_op jit(solution)/shard_map/reduce-window
  10.3 4.4 %collective-permute-done.2 = bf16[128,1024]{1,0:T(8,128)(2,1)} collective-permute-done((bf16[128,1024]{1,0:T(8,128)(2,1)}, bf16[128,1024]{1,0:T(8,128)(2,1)}, u32[]{:S(2)}, u32[]{:S(2)}) %collective-permute-start.2) | collective-permute-done | bytes 262176 | tf_op jit(solution)/shard_map/ppermute | solution.py:9
  14.7 1.3 multiply_reduce_fusion
  16.1 1.1 collective-permute-done.3
  17.3 0.6 collective-permute-start.4
  18.1 2.8 %collective-permute-done.4 = f32[128]{0:T(128)S(1)} collective-permute-done((f32[128]{0:T(128)S(1)}, f32[128]{0:T(128)S(1)}, u32[]{:S(2)}, u32[]{:S(2)}) %collective-permute-start.4) | collective-permute-done | bytes 544 | tf_op jit(solution)/shard_map/ppermute | solution.py:9
  20.9 1.3 convolution_convert_fusion
  22.1 1.4 reshape_reshape.12
  23.6 14.2 %all-to-all-start = ((bf16[64,80,128]{2,1,0:T(8,128)(2,1)}), bf16[64,80,128]{2,1,0:T(8,128)(2,1)S(1)}, u32[]{:S(2)}, u32[]{:S(2)}) async-start(bf16[64,80,128]{2,1,0:T(8,128)(2,1)} %reshape_reshape.12), calls=%async_computation | async-start | bytes 2621440 | tf_op jit(solution)/shard_map/all_to_all | solution.py:46
  37.8 34.9 %all-to-all-done = bf16[64,80,128]{2,1,0:T(8,128)(2,1)S(1)} async-done(((bf16[64,80,128]{2,1,0:T(8,128)(2,1)}), bf16[64,80,128]{2,1,0:T(8,128)(2,1)S(1)}, u32[]{:S(2)}, u32[]{:S(2)}) %all-to-all-start) | async-done | bytes 1310752 | tf_op jit(solution)/shard_map/all_to_all | solution.py:46
  72.7 1.4 reshape_reshape.13
  74.2 2.1 %constant_dynamic-slice_fusion = bf16[320,1024]{1,0:T(8,128)(2,1)} fusion(bf16[640,1024]{1,0:T(8,128)(2,1)} %reshape_reshape.13, s32[]{:T(128)S(6)} %select_n.73), kind=kLoop, calls=%fused_computation.45 | loop fusion | bytes 1310724 | tf_op jit(solution)/shard_map/dynamic_slice | solution.py:13
  76.3 4.8 %fusion.4 = bf16[320,2048]{1,0:T(8,128)(2,1)} fusion(bf16[1,1024,2048]{2,1,0:T(8,128)(2,1)} %param.12, bf16[640,1024]{1,0:T(8,128)(2,1)S(1)} %copy-done.2, s32[]{:T(128)S(6)} %select_n.74), kind=kOutput, calls=%fused_computation.4 | convolution fusion | flops 1342832640 | bytes 6160388 | tf_op jit(solution)/shard_map/dot_general | solution.py:93
  81.1 3.9 %fusion.7 = bf16[320,2048]{1,0:T(8,128)(2,1)S(1)} fusion(bf16[320,1024]{1,0:T(8,128)(2,1)} %constant_dynamic-slice_fusion, bf16[1,1024,2048]{2,1,0:T(8,128)(2,1)} %param.12), kind=kOutput, calls=%fused_computation.5 | convolution fusion | flops 1342832640 | bytes 6160384 | tf_op jit(solution)/shard_map/dot_general | solution.py:96
  85.0 0.4 add_convert_fusion
  85.6 17.1 %collective-permute-done.6 = bf16[160,2048]{1,0:T(8,128)(2,1)S(1)} collective-permute-done((bf16[160,2048]{1,0:T(8,128)(2,1)S(1)}, bf16[160,2048]{1,0:T(8,128)(2,1)S(1)}, u32[]{:S(2)}, u32[]{:S(2)}) %collective-permute-start.6) | collective-permute-done | bytes 655392 | tf_op jit(solution)/shard_map/ppermute | solution.py:9
  103.5 9.0 %collective-permute-done.7 = bf16[160,1024]{1,0:T(8,128)(2,1)S(1)} collective-permute-done((bf16[160,1024]{1,0:T(8,128)(2,1)S(1)}, bf16[160,1024]{1,0:T(8,128)(2,1)S(1)}, u32[]{:S(2)}, u32[]{:S(2)}) %collective-permute-start.7) | collective-permute-done | bytes 327712 | tf_op jit(solution)/shard_map/ppermute | solution.py:9
  113.0 1.9 %collective-permute-done.8 = bf16[320,1024]{1,0:T(8,128)(2,1)S(1)} collective-permute-done((bf16[320,1024]{1,0:T(8,128)(2,1)S(1)}, bf16[320,1024]{1,0:T(8,128)(2,1)S(1)}, u32[]{:S(2)}, u32[]{:S(2)}) %collective-permute-start.8) | collective-permute-done | bytes 655392 | tf_op jit(solution)/shard_map/ppermute | solution.py:9
  114.9 1.5 fusion.12
  116.5 1.4 reshape_reshape.14
  117.9 6.2 %all-to-all-start.1 = ((bf16[64,80,128]{2,1,0:T(8,128)(2,1)}), bf16[64,80,128]{2,1,0:T(8,128)(2,1)S(1)}, u32[]{:S(2)}, u32[]{:S(2)}) async-start(bf16[64,80,128]{2,1,0:T(8,128)(2,1)} %reshape_reshape.14), calls=%async_computation.1 | async-start | bytes 2621440 | tf_op jit(solution)/shard_map/all_to_all | solution.py:46
  124.2 0.9 select_reduce_fusion
  125.1 35.1 %all-to-all-done.1 = bf16[64,80,128]{2,1,0:T(8,128)(2,1)S(1)} async-done(((bf16[64,80,128]{2,1,0:T(8,128)(2,1)}), bf16[64,80,128]{2,1,0:T(8,128)(2,1)S(1)}, u32[]{:S(2)}, u32[]{:S(2)}) %all-to-all-start.1) | async-done | bytes 1310752 | tf_op jit(solution)/shard_map/all_to_all | solution.py:46
  160.1 1.4 reshape_reshape.15
  161.6 3.1 %fusion.16 = bf16[128,1024]{1,0:T(8,128)(2,1)} fusion(f32[128,1024]{1,0:T(8,128)} %copy-done.1, f32[640,128]{1,0:T(8,128)} %select_reduce_fusion, bf16[640,1024]{1,0:T(8,128)(2,1)} %reshape_reshape.15), kind=kOutput, calls=%fused_computation.17 | convolution fusion | flops 1006895104 | bytes 2424832 | tf_op jit(solution)/shard_map/dot_general | solution.py:108
  (39 shorter events, 2.8 us)
Async XLA Ops:
  0.0 114.9 %copy-start = (bf16[1,1024,1024]{2,1,0:T(8,128)(2,1)S(1)}, bf16[1,1024,1024]{2,1,0:T(8,128)(2,1)}, u32[]{:S(2)}) copy-start(bf16[1,1024,1024]{2,1,0:T(8,128)(2,1)} %param.13) | copy-start | bytes 6291460
  0.0 4.3 %copy-start.3 = (bf16[1,128,4096]{2,1,0:T(8,128)(2,1)S(1)}, bf16[1,128,4096]{2,1,0:T(8,128)(2,1)}, u32[]{:S(2)}) copy-start(bf16[1,128,4096]{2,1,0:T(8,128)(2,1)} %param.7) | copy-start | bytes 3145732
  2.0 1.7 %collective-permute-start = (bf16[128,1024]{1,0:T(8,128)(2,1)}, bf16[128,1024]{1,0:T(8,128)(2,1)S(1)}, u32[]{:S(2)}, u32[]{:S(2)}) collective-permute-start(bf16[128,1024]{1,0:T(8,128)(2,1)} %get-tuple-element.15), channel_id=1, source_target_pairs={{0,1},{1,0},{2,3},{3,2},{4,5},{5,4},{6,7},{7,6},{8,9},{9,8},{10,11... | collective-permute-start | bytes 786440 | tf_op jit(solution)/shard_map/ppermute | solution.py:9
  2.0 2.2 %collective-permute-start.1 = (bf16[128,1024]{1,0:T(8,128)(2,1)}, bf16[128,1024]{1,0:T(8,128)(2,1)}, u32[]{:S(2)}, u32[]{:S(2)}) collective-permute-start(bf16[128,1024]{1,0:T(8,128)(2,1)} %get-tuple-element.16), channel_id=1, source_target_pairs={{0,1},{1,0},{2,3},{3,2},{4,5},{5,4},{6,7},{7,6},{8,9},{9,8},{10,11... | collective-permute-start | bytes 786440 | tf_op jit(solution)/shard_map/ppermute | solution.py:9
  6.1 8.7 %collective-permute-start.2 = (bf16[128,1024]{1,0:T(8,128)(2,1)}, bf16[128,1024]{1,0:T(8,128)(2,1)}, u32[]{:S(2)}, u32[]{:S(2)}) collective-permute-start(bf16[128,1024]{1,0:T(8,128)(2,1)} %fusion.19), channel_id=1, source_target_pairs={{0,2},{1,3},{2,0},{3,1},{4,6},{5,7},{6,4},{7,5},{8,10},{9,11},{10,... | collective-permute-start | bytes 786440 | tf_op jit(solution)/shard_map/ppermute | solution.py:9
  7.3 8.9 %copy-start.4 = (s32[128,4]{0,1:T(4,128)S(1)}, s32[128,4]{0,1:T(4,128)}, u32[]{:S(2)}) copy-start(s32[128,4]{0,1:T(4,128)} %param.10) | copy-start | bytes 6148
  16.0 4.8 %copy-start.1 = (f32[128,1024]{1,0:T(8,128)}, f32[128,1024]{1,0:T(8,128)S(1)}, u32[]{:S(2)}) copy-start(f32[128,1024]{1,0:T(8,128)S(1)} %get-tuple-element.12) | copy-start | bytes 1572868
  16.0 1.2 collective-permute-start.3
  17.3 3.6 %collective-permute-start.4 = (f32[128]{0:T(128)S(1)}, f32[128]{0:T(128)S(1)}, u32[]{:S(2)}, u32[]{:S(2)}) collective-permute-start(f32[128]{0:T(128)S(1)} %add.101), channel_id=1, source_target_pairs={{0,2},{1,3},{2,0},{3,1},{4,6},{5,7},{6,4},{7,5},{8,10},{9,11},{10,... | collective-permute-start | bytes 1544 | tf_op jit(solution)/shard_map/ppermute | solution.py:9
  23.6 49.2 %all-to-all-start = ((bf16[64,80,128]{2,1,0:T(8,128)(2,1)}), bf16[64,80,128]{2,1,0:T(8,128)(2,1)S(1)}, u32[]{:S(2)}, u32[]{:S(2)}) async-start(bf16[64,80,128]{2,1,0:T(8,128)(2,1)} %reshape_reshape.12), calls=%async_computation | async-start | bytes 2621440 | tf_op jit(solution)/shard_map/all_to_all | solution.py:46
  74.2 2.1 %copy-start.2 = (bf16[640,1024]{1,0:T(8,128)(2,1)S(1)}, bf16[640,1024]{1,0:T(8,128)(2,1)}, u32[]{:S(2)}) copy-start(bf16[640,1024]{1,0:T(8,128)(2,1)} %reshape_reshape.13) | copy-start | bytes 3932164
  81.1 3.9 %collective-permute-start.5 = (bf16[320,2048]{1,0:T(8,128)(2,1)}, bf16[320,2048]{1,0:T(8,128)(2,1)S(1)}, u32[]{:S(2)}, u32[]{:S(2)}) collective-permute-start(bf16[320,2048]{1,0:T(8,128)(2,1)} %fusion.4), channel_id=1, source_target_pairs={{0,1},{1,0},{2,3},{3,2},{4,5},{5,4},{6,7},{7,6},{8,9},{9,8},{10,11... | collective-permute-start | bytes 3932168 | tf_op jit(solution)/shard_map/ppermute | solution.py:9
  85.5 17.2 %collective-permute-start.6 = (bf16[160,2048]{1,0:T(8,128)(2,1)S(1)}, bf16[160,2048]{1,0:T(8,128)(2,1)S(1)}, u32[]{:S(2)}, u32[]{:S(2)}) collective-permute-start(bf16[160,2048]{1,0:T(8,128)(2,1)S(1)} %get-tuple-element.13), channel_id=1, source_target_pairs={{0,2},{1,3},{2,0},{3,1},{4,6},{5,7},{6,4},{7,5},{8,10},{9,11},{10,... | collective-permute-start | bytes 1966088 | tf_op jit(solution)/shard_map/ppermute | solution.py:9
  103.1 9.4 %collective-permute-start.7 = (bf16[160,1024]{1,0:T(8,128)(2,1)S(1)}, bf16[160,1024]{1,0:T(8,128)(2,1)S(1)}, u32[]{:S(2)}, u32[]{:S(2)}) collective-permute-start(bf16[160,1024]{1,0:T(8,128)(2,1)S(1)} %get-tuple-element.10), channel_id=1, source_target_pairs={{0,2},{1,3},{2,0},{3,1},{4,6},{5,7},{6,4},{7,5},{8,10},{9,11},{10,... | collective-permute-start | bytes 983048 | tf_op jit(solution)/shard_map/ppermute | solution.py:9
  112.5 2.4 %collective-permute-start.8 = (bf16[320,1024]{1,0:T(8,128)(2,1)S(1)}, bf16[320,1024]{1,0:T(8,128)(2,1)S(1)}, u32[]{:S(2)}, u32[]{:S(2)}) collective-permute-start(bf16[320,1024]{1,0:T(8,128)(2,1)S(1)} %constant_dynamic-update-slice_fusion), channel_id=1, source_target_pairs={{0,1},{1,0},{2,3},{3,2},{4,5},{5,4},{6,7},{7,6},{8,9},{9,8},{10,11... | collective-permute-start | bytes 1966088 | tf_op jit(solution)/shard_map/ppermute | solution.py:9
  117.9 6.2 %copy-start.5 = (f32[128,4]{0,1:T(4,128)S(1)}, f32[128,4]{0,1:T(4,128)}, u32[]{:S(2)}) copy-start(f32[128,4]{0,1:T(4,128)} %param.11) | copy-start | bytes 6148
  117.9 42.2 %all-to-all-start.1 = ((bf16[64,80,128]{2,1,0:T(8,128)(2,1)}), bf16[64,80,128]{2,1,0:T(8,128)(2,1)S(1)}, u32[]{:S(2)}, u32[]{:S(2)}) async-start(bf16[64,80,128]{2,1,0:T(8,128)(2,1)} %reshape_reshape.14), calls=%async_computation.1 | async-start | bytes 2621440 | tf_op jit(solution)/shard_map/all_to_all | solution.py:46

commit v12 on v7

--- a/solution.py
+++ b/solution.py
@@ -44,9 +44,7 @@
 
 def _exchange_rows(value):
     experts, slots, features = value.shape
-    lanes = features
-    while lanes > 128 and (slots * features // lanes) % 8 != 0:
-        lanes //= 2
+    lanes = 128
     packed = value.reshape(experts, slots * features // lanes, lanes)
     moved = lax.all_to_all(packed, "expert", split_axis=0, concat_axis=0, tiled=True)
     return moved.reshape(experts, slots, features)
@@ -113,7 +111,7 @@
     routed = jnp.dot(
         weights_table,
         returned.reshape(expert_count * capacity, feature_local).astype(jnp.float32),
-        precision=lax.Precision.HIGHEST,
+        precision=lax.Precision.HIGH,
     )
     return (stream + routed).astype(jnp.bfloat16)
 

time: 165 us -> 164 us (level)
  no operation moved by 1% of the time
where the time goes in v12:
time: 164 us
  waiting for transfers between devices  107 us (65%)
  starting transfers between devices  25.2 us (15%)
  matrix products  13.7 us (8%)
  local copies, waits for them, and re-layouts  10.2 us (6%)
  other arithmetic  7.1 us (4%)
    all_to_all x2, waiting for transfers between devices, _exchange_rows(): lax.all_to_all(packed, 'expert', split_axis=0, concat_axis=0, tiled=True)  70 us
    ppermute x8, waiting for transfers between devices, _exchange(): return lax.ppermute(value, 'tensor', [(j, j ^ flip) for j in range(size)])  37.4 us
    all_to_all x2, starting transfers between devices, _exchange_rows(): lax.all_to_all(packed, 'expert', split_axis=0, concat_axis=0, tiled=True)  20.5 us
    dot_general x1, matrix products, _body(): jnp.dot(away_rows, w_in[0], preferred_element_type=jnp.float32)  4.78 us
    ppermute x8, starting transfers between devices, _exchange(): return lax.ppermute(value, 'tensor', [(j, j ^ flip) for j in range(size)])  4.71 us
    dot_general x1, matrix products, _body(): jnp.dot(home_rows, w_in[0], preferred_element_type=jnp.float32)  3.91 us
    dynamic_slice x2, local copies, waits for them, and re-layouts, _slab(): return lax.dynamic_slice_in_dim(value, start, size, axis=axis)  3.34 us
  transfers between devices with their start and end apart: 10, of which 9 were waited for; matrix products, arithmetic and copies ran while one was open for 4% of the time, Pallas kernels for 0%

profile of v12, /device:TPU:32, one launch (start us, length us, event | category | flops | bytes accessed | tf_op | source)
XLA Modules:
  0.0 163.8 jit_solution(8566364621303780791)
XLA Ops:
  0.0 1.2 dynamic-slice_bitcast_fusion.1
  1.3 0.8 pad_maximum_fusion
  2.3 2.0 %collective-permute-done = bf16[128,2048]{1,0:T(8,128)(2,1)} collective-permute-done((bf16[128,2048]{1,0:T(8,128)(2,1)}, bf16[128,2048]{1,0:T(8,128)(2,1)}, u32[]{:S(2)}, u32[]{:S(2)}) %collective-permute-start) | collective-permute-done | bytes 524320 | tf_op jit(solution)/shard_map/ppermute | solution.py:9
  4.3 1.7 %fusion.19 = bf16[128,1024]{1,0:T(8,128)(2,1)} fusion(bf16[128,2048]{1,0:T(8,128)(2,1)} %collective-permute-done, s32[]{:T(128)S(6)} %select_n.64, bf16[1,128,4096]{2,1,0:T(8,128)(2,1)S(1)} %copy-done.3, s32[]{:T(128)S(6)} %select_n.63), kind=kLoop, calls=%fused_computation.23 | loop fusion | flops 524288 | bytes 786440 | tf_op jit(solution)/shard_map/convert_element_type | solution.py:29
  6.1 1.5 collective-permute-start.1
  7.7 1.2 reduce-window.6
  9.5 5.3 %collective-permute-done.1 = bf16[128,1024]{1,0:T(8,128)(2,1)} collective-permute-done((bf16[128,1024]{1,0:T(8,128)(2,1)}, bf16[128,1024]{1,0:T(8,128)(2,1)}, u32[]{:S(2)}, u32[]{:S(2)}) %collective-permute-start.1) | collective-permute-done | bytes 262176 | tf_op jit(solution)/shard_map/ppermute | solution.py:9
  14.7 1.3 multiply_reduce_fusion
  16.2 1.1 collective-permute-done.2
  17.3 1.5 collective-permute-start.3
  19.0 1.9 %collective-permute-done.3 = f32[128]{0:T(128)S(1)} collective-permute-done((f32[128]{0:T(128)S(1)}, f32[128]{0:T(128)S(1)}, u32[]{:S(2)}, u32[]{:S(2)}) %collective-permute-start.3) | collective-permute-done | bytes 544 | tf_op jit(solution)/shard_map/ppermute | solution.py:9
  20.9 0.6 convolution_convert_fusion
  21.5 1.4 reshape_reshape.12
  22.9 14.2 %all-to-all-start = ((bf16[64,80,128]{2,1,0:T(8,128)(2,1)}), bf16[64,80,128]{2,1,0:T(8,128)(2,1)S(1)}, u32[]{:S(2)}, u32[]{:S(2)}) async-start(bf16[64,80,128]{2,1,0:T(8,128)(2,1)} %reshape_reshape.12), calls=%async_computation | async-start | bytes 2621440 | tf_op jit(solution)/shard_map/all_to_all | solution.py:49
  37.2 34.9 %all-to-all-done = bf16[64,80,128]{2,1,0:T(8,128)(2,1)S(1)} async-done(((bf16[64,80,128]{2,1,0:T(8,128)(2,1)}), bf16[64,80,128]{2,1,0:T(8,128)(2,1)S(1)}, u32[]{:S(2)}, u32[]{:S(2)}) %all-to-all-start) | async-done | bytes 1310752 | tf_op jit(solution)/shard_map/all_to_all | solution.py:49
  72.1 1.4 reshape_reshape.13
  73.5 2.1 %constant_dynamic-slice_fusion = bf16[320,1024]{1,0:T(8,128)(2,1)} fusion(bf16[640,1024]{1,0:T(8,128)(2,1)} %reshape_reshape.13, s32[]{:T(128)S(6)} %select_n.66), kind=kLoop, calls=%fused_computation.44 | loop fusion | bytes 1310724 | tf_op jit(solution)/shard_map/dynamic_slice | solution.py:13
  75.7 4.8 %fusion.4 = bf16[320,2048]{1,0:T(8,128)(2,1)} fusion(bf16[1,1024,2048]{2,1,0:T(8,128)(2,1)} %param.12, bf16[640,1024]{1,0:T(8,128)(2,1)S(1)} %copy-done.2, s32[]{:T(128)S(6)} %select_n.67), kind=kOutput, calls=%fused_computation.4 | convolution fusion | flops 1342832640 | bytes 6160388 | tf_op jit(solution)/shard_map/dot_general | solution.py:96
  80.4 3.9 %fusion.7 = bf16[320,2048]{1,0:T(8,128)(2,1)S(1)} fusion(bf16[320,1024]{1,0:T(8,128)(2,1)} %constant_dynamic-slice_fusion, bf16[1,1024,2048]{2,1,0:T(8,128)(2,1)} %param.12), kind=kOutput, calls=%fused_computation.5 | convolution fusion | flops 1342832640 | bytes 6160384 | tf_op jit(solution)/shard_map/dot_general | solution.py:99
  84.4 0.4 add_convert_fusion
  84.8 0.7 collective-permute-start.5
  85.5 16.6 %collective-permute-done.5 = bf16[160,2048]{1,0:T(8,128)(2,1)S(1)} collective-permute-done((bf16[160,2048]{1,0:T(8,128)(2,1)S(1)}, bf16[160,2048]{1,0:T(8,128)(2,1)S(1)}, u32[]{:S(2)}, u32[]{:S(2)}) %collective-permute-start.5) | collective-permute-done | bytes 655392 | tf_op jit(solution)/shard_map/ppermute | solution.py:9
  102.5 0.7 collective-permute-start.6
  103.2 8.7 %collective-permute-done.6 = bf16[160,1024]{1,0:T(8,128)(2,1)S(1)} collective-permute-done((bf16[160,1024]{1,0:T(8,128)(2,1)S(1)}, bf16[160,1024]{1,0:T(8,128)(2,1)S(1)}, u32[]{:S(2)}, u32[]{:S(2)}) %collective-permute-start.6) | collective-permute-done | bytes 327712 | tf_op jit(solution)/shard_map/ppermute | solution.py:9
  112.4 1.9 %collective-permute-done.7 = bf16[320,1024]{1,0:T(8,128)(2,1)S(1)} collective-permute-done((bf16[320,1024]{1,0:T(8,128)(2,1)S(1)}, bf16[320,1024]{1,0:T(8,128)(2,1)S(1)}, u32[]{:S(2)}, u32[]{:S(2)}) %collective-permute-start.7) | collective-permute-done | bytes 655392 | tf_op jit(solution)/shard_map/ppermute | solution.py:9
  114.3 1.5 fusion.12
  115.9 1.4 reshape_reshape.14
  117.3 6.2 %all-to-all-start.1 = ((bf16[64,80,128]{2,1,0:T(8,128)(2,1)}), bf16[64,80,128]{2,1,0:T(8,128)(2,1)S(1)}, u32[]{:S(2)}, u32[]{:S(2)}) async-start(bf16[64,80,128]{2,1,0:T(8,128)(2,1)} %reshape_reshape.14), calls=%async_computation.1 | async-start | bytes 2621440 | tf_op jit(solution)/shard_map/all_to_all | solution.py:49
  123.6 0.9 select_reduce_fusion
  124.4 35.1 %all-to-all-done.1 = bf16[64,80,128]{2,1,0:T(8,128)(2,1)S(1)} async-done(((bf16[64,80,128]{2,1,0:T(8,128)(2,1)}), bf16[64,80,128]{2,1,0:T(8,128)(2,1)S(1)}, u32[]{:S(2)}, u32[]{:S(2)}) %all-to-all-start.1) | async-done | bytes 1310752 | tf_op jit(solution)/shard_map/all_to_all | solution.py:49
  159.5 1.4 reshape_reshape.15
  160.9 2.9 %fusion.16 = bf16[128,1024]{1,0:T(8,128)(2,1)} fusion(f32[128,1024]{1,0:T(8,128)} %copy-done.1, f32[640,128]{1,0:T(8,128)} %select_reduce_fusion, bf16[640,1024]{1,0:T(8,128)(2,1)} %reshape_reshape.15), kind=kOutput, calls=%fused_computation.17 | convolution fusion | flops 503578624 | bytes 2424832 | tf_op jit(solution)/shard_map/dot_general | solution.py:111
  (40 shorter events, 2.2 us)
Async XLA Ops:
  0.0 114.3 %copy-start = (bf16[1,1024,1024]{2,1,0:T(8,128)(2,1)S(1)}, bf16[1,1024,1024]{2,1,0:T(8,128)(2,1)}, u32[]{:S(2)}) copy-start(bf16[1,1024,1024]{2,1,0:T(8,128)(2,1)} %param.13) | copy-start | bytes 6291460
  0.0 4.3 %copy-start.3 = (bf16[1,128,4096]{2,1,0:T(8,128)(2,1)S(1)}, bf16[1,128,4096]{2,1,0:T(8,128)(2,1)}, u32[]{:S(2)}) copy-start(bf16[1,128,4096]{2,1,0:T(8,128)(2,1)} %param.7) | copy-start | bytes 3145732
  0.0 2.1 %copy-start.4 = (s32[128,4]{0,1:T(4,128)S(1)}, s32[128,4]{0,1:T(4,128)}, u32[]{:S(2)}) copy-start(s32[128,4]{0,1:T(4,128)} %param.10) | copy-start | bytes 6148
  2.1 2.3 %collective-permute-start = (bf16[128,2048]{1,0:T(8,128)(2,1)}, bf16[128,2048]{1,0:T(8,128)(2,1)}, u32[]{:S(2)}, u32[]{:S(2)}) collective-permute-start(bf16[128,2048]{1,0:T(8,128)(2,1)} %pad_maximum_fusion), channel_id=1, source_target_pairs={{0,1},{1,0},{2,3},{3,2},{4,5},{5,4},{6,7},{7,6},{8,9},{9,8},{10,11... | collective-permute-start | bytes 1572872 | tf_op jit(solution)/shard_map/ppermute | solution.py:9
  6.1 14.8 %copy-start.5 = (f32[1024]{0:T(1024)S(1)}, f32[1024]{0:T(1024)}, u32[]{:S(2)}) copy-start(f32[1024]{0:T(1024)} %param.9) | copy-start | bytes 12292
  6.1 8.7 %collective-permute-start.1 = (bf16[128,1024]{1,0:T(8,128)(2,1)}, bf16[128,1024]{1,0:T(8,128)(2,1)}, u32[]{:S(2)}, u32[]{:S(2)}) collective-permute-start(bf16[128,1024]{1,0:T(8,128)(2,1)} %fusion.19), channel_id=1, source_target_pairs={{0,2},{1,3},{2,0},{3,1},{4,6},{5,7},{6,4},{7,5},{8,10},{9,11},{10,... | collective-permute-start | bytes 786440 | tf_op jit(solution)/shard_map/ppermute | solution.py:9
  16.1 4.8 %copy-start.1 = (f32[128,1024]{1,0:T(8,128)}, f32[128,1024]{1,0:T(8,128)S(1)}, u32[]{:S(2)}) copy-start(f32[128,1024]{1,0:T(8,128)S(1)} %get-tuple-element.12) | copy-start | bytes 1572868
  16.1 1.2 collective-permute-start.2
  17.3 3.6 %collective-permute-start.3 = (f32[128]{0:T(128)S(1)}, f32[128]{0:T(128)S(1)}, u32[]{:S(2)}, u32[]{:S(2)}) collective-permute-start(f32[128]{0:T(128)S(1)} %add.109), channel_id=1, source_target_pairs={{0,2},{1,3},{2,0},{3,1},{4,6},{5,7},{6,4},{7,5},{8,10},{9,11},{10,... | collective-permute-start | bytes 1544 | tf_op jit(solution)/shard_map/ppermute | solution.py:9
  22.9 49.2 %all-to-all-start = ((bf16[64,80,128]{2,1,0:T(8,128)(2,1)}), bf16[64,80,128]{2,1,0:T(8,128)(2,1)S(1)}, u32[]{:S(2)}, u32[]{:S(2)}) async-start(bf16[64,80,128]{2,1,0:T(8,128)(2,1)} %reshape_reshape.12), calls=%async_computation | async-start | bytes 2621440 | tf_op jit(solution)/shard_map/all_to_all | solution.py:49
  73.5 2.1 %copy-start.2 = (bf16[640,1024]{1,0:T(8,128)(2,1)S(1)}, bf16[640,1024]{1,0:T(8,128)(2,1)}, u32[]{:S(2)}) copy-start(bf16[640,1024]{1,0:T(8,128)(2,1)} %reshape_reshape.13) | copy-start | bytes 3932164
  80.4 3.9 %collective-permute-start.4 = (bf16[320,2048]{1,0:T(8,128)(2,1)}, bf16[320,2048]{1,0:T(8,128)(2,1)S(1)}, u32[]{:S(2)}, u32[]{:S(2)}) collective-permute-start(bf16[320,2048]{1,0:T(8,128)(2,1)} %fusion.4), channel_id=1, source_target_pairs={{0,1},{1,0},{2,3},{3,2},{4,5},{5,4},{6,7},{7,6},{8,9},{9,8},{10,11... | collective-permute-start | bytes 3932168 | tf_op jit(solution)/shard_map/ppermute | solution.py:9
  84.8 17.2 %collective-permute-start.5 = (bf16[160,2048]{1,0:T(8,128)(2,1)S(1)}, bf16[160,2048]{1,0:T(8,128)(2,1)S(1)}, u32[]{:S(2)}, u32[]{:S(2)}) collective-permute-start(bf16[160,2048]{1,0:T(8,128)(2,1)S(1)} %get-tuple-element.13), channel_id=1, source_target_pairs={{0,2},{1,3},{2,0},{3,1},{4,6},{5,7},{6,4},{7,5},{8,10},{9,11},{10,... | collective-permute-start | bytes 1966088 | tf_op jit(solution)/shard_map/ppermute | solution.py:9
  102.5 9.4 %collective-permute-start.6 = (bf16[160,1024]{1,0:T(8,128)(2,1)S(1)}, bf16[160,1024]{1,0:T(8,128)(2,1)S(1)}, u32[]{:S(2)}, u32[]{:S(2)}) collective-permute-start(bf16[160,1024]{1,0:T(8,128)(2,1)S(1)} %get-tuple-element.10), channel_id=1, source_target_pairs={{0,2},{1,3},{2,0},{3,1},{4,6},{5,7},{6,4},{7,5},{8,10},{9,11},{10,... | collective-permute-start | bytes 983048 | tf_op jit(solution)/shard_map/ppermute | solution.py:9
  111.9 2.4 %collective-permute-start.7 = (bf16[320,1024]{1,0:T(8,128)(2,1)S(1)}, bf16[320,1024]{1,0:T(8,128)(2,1)S(1)}, u32[]{:S(2)}, u32[]{:S(2)}) collective-permute-start(bf16[320,1024]{1,0:T(8,128)(2,1)S(1)} %constant_dynamic-update-slice_fusion.3), channel_id=1, source_target_pairs={{0,1},{1,0},{2,3},{3,2},{4,5},{5,4},{6,7},{7,6},{8,9},{9,8},{10,11... | collective-permute-start | bytes 1966088 | tf_op jit(solution)/shard_map/ppermute | solution.py:9
  117.3 6.2 %copy-start.6 = (f32[128,4]{0,1:T(4,128)S(1)}, f32[128,4]{0,1:T(4,128)}, u32[]{:S(2)}) copy-start(f32[128,4]{0,1:T(4,128)} %param.11) | copy-start | bytes 6148
  117.3 42.2 %all-to-all-start.1 = ((bf16[64,80,128]{2,1,0:T(8,128)(2,1)}), bf16[64,80,128]{2,1,0:T(8,128)(2,1)S(1)}, u32[]{:S(2)}, u32[]{:S(2)}) async-start(bf16[64,80,128]{2,1,0:T(8,128)(2,1)} %reshape_reshape.14), calls=%async_computation.1 | async-start | bytes 2621440 | tf_op jit(solution)/shard_map/all_to_all | solution.py:49

commit v13 on v12

--- a/solution.py
+++ b/solution.py
@@ -27,19 +27,6 @@
     home = _slab(value, (2 * high + core) * n, n, axis).astype(jnp.float32)
     home = home + _slab(received, high * n, n, axis).astype(jnp.float32)
     return home + _exchange(away.astype(jnp.bfloat16), 2).astype(jnp.float32)
-
-
-def _all_gather_rows(value):
-    t = lax.axis_index("tensor")
-    core = t % 2
-    high = t // 2
-    n = value.shape[0]
-    pair = jnp.zeros((2 * n,) + value.shape[1:], value.dtype)
-    pair = lax.dynamic_update_slice_in_dim(pair, value, high * n, 0)
-    pair = lax.dynamic_update_slice_in_dim(pair, _exchange(value, 2), (1 - high) * n, 0)
-    full = jnp.zeros((4 * n,) + value.shape[1:], value.dtype)
-    full = lax.dynamic_update_slice_in_dim(full, pair, 2 * core * n, 0)
-    return lax.dynamic_update_slice_in_dim(full, _exchange(pair, 1), 2 * (1 - core) * n, 0)
 
 
 def _exchange_rows(value):
@@ -104,14 +91,23 @@
     home = lax.optimization_barrier(home + _slab(received, high * block, block, 0).astype(jnp.float32))
     total = home + far.astype(jnp.float32)
     hidden = (jax.nn.silu(total[:, :hidden_width]) * total[:, hidden_width:]).astype(jnp.bfloat16)
-    hidden = _all_gather_rows(hidden)
-    produced = jnp.dot(hidden, w_down[0], preferred_element_type=jnp.float32).astype(jnp.bfloat16)
+    n = hidden.shape[0]
+    pair = jnp.zeros((2 * n,) + hidden.shape[1:], hidden.dtype)
+    pair = lax.dynamic_update_slice_in_dim(pair, hidden, high * n, 0)
+    pair = lax.dynamic_update_slice_in_dim(pair, _exchange(hidden, 2), (1 - high) * n, 0)
+    pair = lax.optimization_barrier(pair)
+    other = _exchange(pair, 1)
+    near = jnp.dot(pair, w_down[0], preferred_element_type=jnp.float32).astype(jnp.bfloat16)
+    far_out = jnp.dot(other, w_down[0], preferred_element_type=jnp.float32).astype(jnp.bfloat16)
+    produced = jnp.zeros((4 * n, near.shape[1]), near.dtype)
+    produced = lax.dynamic_update_slice_in_dim(produced, near, 2 * core * n, 0)
+    produced = lax.dynamic_update_slice_in_dim(produced, far_out, 2 * (1 - core) * n, 0)
     results = produced.reshape(source_count, item_count, feature_local)
     returned = _exchange_rows(results)
     routed = jnp.dot(
         weights_table,
         returned.reshape(expert_count * capacity, feature_local).astype(jnp.float32),
-        precision=lax.Precision.HIGH,
+        precision=lax.Precision.HIGHEST,
     )
     return (stream + routed).astype(jnp.bfloat16)
 

time: 164 us -> 164 us (level)
  transfers between devices with their start and end apart: 10 -> 10, of which waited for: 9 -> 9; matrix products, arithmetic and copies ran while one was open for 4% -> 5% of each run, Pallas kernels for 0% -> 0%
where the time goes in v13:
time: 164 us; the launch traced here: 163 us
  waiting for transfers between devices  107 us (65%)
  starting transfers between devices  25.2 us (15%)
  matrix products  14 us (9%)
  local copies, waits for them, and re-layouts  10.1 us (6%)
  other arithmetic  7.1 us (4%)
    all_to_all x2, waiting for transfers between devices, _exchange_rows(): lax.all_to_all(packed, 'expert', split_axis=0, concat_axis=0, tiled=True)  70 us
    ppermute x8, waiting for transfers between devices, _exchange(): return lax.ppermute(value, 'tensor', [(j, j ^ flip) for j in range(size)])  36.6 us
    all_to_all x2, starting transfers between devices, _exchange_rows(): lax.all_to_all(packed, 'expert', split_axis=0, concat_axis=0, tiled=True)  20.5 us
    dot_general x1, matrix products, _body(): jnp.dot(away_rows, w_in[0], preferred_element_type=jnp.float32)  4.78 us
    ppermute x8, starting transfers between devices, _exchange(): return lax.ppermute(value, 'tensor', [(j, j ^ flip) for j in range(size)])  4.71 us
    dot_general x1, matrix products, _body(): jnp.dot(home_rows, w_in[0], preferred_element_type=jnp.float32)  3.91 us
    dynamic_slice x2, local copies, waits for them, and re-layouts, _slab(): return lax.dynamic_slice_in_dim(value, start, size, axis=axis)  3.34 us
  transfers between devices with their start and end apart: 10, of which 9 were waited for; matrix products, arithmetic and copies ran while one was open for 5% of the time, Pallas kernels for 0%

profile of v13, /device:TPU:32, one launch (start us, length us, event | category | flops | bytes accessed | tf_op | source)
XLA Modules:
  0.0 163.2 jit_solution(2471639447482021968)
XLA Ops:
  0.0 1.2 dynamic-slice_bitcast_fusion.1
  1.3 0.8 pad_maximum_fusion
  2.3 2.0 %collective-permute-done = bf16[128,2048]{1,0:T(8,128)(2,1)} collective-permute-done((bf16[128,2048]{1,0:T(8,128)(2,1)}, bf16[128,2048]{1,0:T(8,128)(2,1)}, u32[]{:S(2)}, u32[]{:S(2)}) %collective-permute-start) | collective-permute-done | bytes 524320 | tf_op jit(solution)/shard_map/ppermute | solution.py:9
  4.3 1.7 %fusion.30 = bf16[128,1024]{1,0:T(8,128)(2,1)} fusion(bf16[128,2048]{1,0:T(8,128)(2,1)} %collective-permute-done, s32[]{:T(128)S(6)} %select_n.61, bf16[1,128,4096]{2,1,0:T(8,128)(2,1)S(1)} %copy-done.3, s32[]{:T(128)S(6)} %select_n.60), kind=kLoop, calls=%fused_computation.28 | loop fusion | flops 524288 | bytes 786440 | tf_op jit(solution)/shard_map/convert_element_type | solution.py:29
  6.1 1.5 collective-permute-start.1
  7.7 1.2 reduce-window.6
  9.5 5.3 %collective-permute-done.1 = bf16[128,1024]{1,0:T(8,128)(2,1)} collective-permute-done((bf16[128,1024]{1,0:T(8,128)(2,1)}, bf16[128,1024]{1,0:T(8,128)(2,1)}, u32[]{:S(2)}, u32[]{:S(2)}) %collective-permute-start.1) | collective-permute-done | bytes 262176 | tf_op jit(solution)/shard_map/ppermute | solution.py:9
  14.7 1.3 multiply_reduce_fusion
  16.2 1.1 collective-permute-done.2
  17.3 1.5 collective-permute-start.3
  19.0 1.9 %collective-permute-done.3 = f32[128]{0:T(128)S(1)} collective-permute-done((f32[128]{0:T(128)S(1)}, f32[128]{0:T(128)S(1)}, u32[]{:S(2)}, u32[]{:S(2)}) %collective-permute-start.3) | collective-permute-done | bytes 544 | tf_op jit(solution)/shard_map/ppermute | solution.py:9
  20.9 0.6 convolution_convert_fusion
  21.5 1.4 reshape_reshape.12
  22.9 14.2 %all-to-all-start = ((bf16[64,80,128]{2,1,0:T(8,128)(2,1)}), bf16[64,80,128]{2,1,0:T(8,128)(2,1)S(1)}, u32[]{:S(2)}, u32[]{:S(2)}) async-start(bf16[64,80,128]{2,1,0:T(8,128)(2,1)} %reshape_reshape.12), calls=%async_computation | async-start | bytes 2621440 | tf_op jit(solution)/shard_map/all_to_all | solution.py:36
  37.2 34.9 %all-to-all-done = bf16[64,80,128]{2,1,0:T(8,128)(2,1)S(1)} async-done(((bf16[64,80,128]{2,1,0:T(8,128)(2,1)}), bf16[64,80,128]{2,1,0:T(8,128)(2,1)S(1)}, u32[]{:S(2)}, u32[]{:S(2)}) %all-to-all-start) | async-done | bytes 1310752 | tf_op jit(solution)/shard_map/all_to_all | solution.py:36
  72.1 1.4 reshape_reshape.13
  73.5 2.1 %constant_dynamic-slice_fusion = bf16[320,1024]{1,0:T(8,128)(2,1)} fusion(bf16[640,1024]{1,0:T(8,128)(2,1)} %reshape_reshape.13, s32[]{:T(128)S(6)} %select_n.63), kind=kLoop, calls=%fused_computation.48 | loop fusion | bytes 1310724 | tf_op jit(solution)/shard_map/dynamic_slice | solution.py:13
  75.7 4.8 %fusion.4 = bf16[320,2048]{1,0:T(8,128)(2,1)} fusion(bf16[1,1024,2048]{2,1,0:T(8,128)(2,1)} %param.12, bf16[640,1024]{1,0:T(8,128)(2,1)S(1)} %copy-done.2, s32[]{:T(128)S(6)} %select_n.64), kind=kOutput, calls=%fused_computation.4 | convolution fusion | flops 1342832640 | bytes 6160388 | tf_op jit(solution)/shard_map/dot_general | solution.py:83
  80.4 3.9 %fusion.7 = bf16[320,2048]{1,0:T(8,128)(2,1)S(1)} fusion(bf16[320,1024]{1,0:T(8,128)(2,1)} %constant_dynamic-slice_fusion, bf16[1,1024,2048]{2,1,0:T(8,128)(2,1)} %param.12), kind=kOutput, calls=%fused_computation.5 | convolution fusion | flops 1342832640 | bytes 6160384 | tf_op jit(solution)/shard_map/dot_general | solution.py:86
  84.8 0.7 collective-permute-start.5
  85.5 16.6 %collective-permute-done.5 = bf16[160,2048]{1,0:T(8,128)(2,1)S(1)} collective-permute-done((bf16[160,2048]{1,0:T(8,128)(2,1)S(1)}, bf16[160,2048]{1,0:T(8,128)(2,1)S(1)}, u32[]{:S(2)}, u32[]{:S(2)}) %collective-permute-start.5) | collective-permute-done | bytes 655392 | tf_op jit(solution)/shard_map/ppermute | solution.py:9
  102.5 0.7 collective-permute-start.6
  103.2 8.7 %collective-permute-done.6 = bf16[160,1024]{1,0:T(8,128)(2,1)S(1)} collective-permute-done((bf16[160,1024]{1,0:T(8,128)(2,1)S(1)}, bf16[160,1024]{1,0:T(8,128)(2,1)S(1)}, u32[]{:S(2)}, u32[]{:S(2)}) %collective-permute-start.6) | collective-permute-done | bytes 327712 | tf_op jit(solution)/shard_map/ppermute | solution.py:9
  112.3 0.8 fusion.17
  113.2 1.1 collective-permute-done.7
  114.2 0.8 fusion.23
  115.1 1.4 reshape_reshape.14
  116.5 6.2 %all-to-all-start.1 = ((bf16[64,80,128]{2,1,0:T(8,128)(2,1)}), bf16[64,80,128]{2,1,0:T(8,128)(2,1)S(1)}, u32[]{:S(2)}, u32[]{:S(2)}) async-start(bf16[64,80,128]{2,1,0:T(8,128)(2,1)} %reshape_reshape.14), calls=%async_computation.1 | async-start | bytes 2621440 | tf_op jit(solution)/shard_map/all_to_all | solution.py:36
  122.8 0.9 select_reduce_fusion
  123.7 35.1 %all-to-all-done.1 = bf16[64,80,128]{2,1,0:T(8,128)(2,1)S(1)} async-done(((bf16[64,80,128]{2,1,0:T(8,128)(2,1)}), bf16[64,80,128]{2,1,0:T(8,128)(2,1)S(1)}, u32[]{:S(2)}, u32[]{:S(2)}) %all-to-all-start.1) | async-done | bytes 1310752 | tf_op jit(solution)/shard_map/all_to_all | solution.py:36
  158.7 1.4 reshape_reshape.15
  160.1 3.1 %fusion.27 = bf16[128,1024]{1,0:T(8,128)(2,1)} fusion(f32[128,1024]{1,0:T(8,128)} %copy-done.1, f32[640,128]{1,0:T(8,128)} %select_reduce_fusion, bf16[640,1024]{1,0:T(8,128)(2,1)} %reshape_reshape.15), kind=kOutput, calls=%fused_computation.22 | convolution fusion | flops 1006895104 | bytes 2424832 | tf_op jit(solution)/shard_map/dot_general | solution.py:107
  (39 shorter events, 2.5 us)
Async XLA Ops:
  0.0 112.3 %copy-start = (bf16[1,1024,1024]{2,1,0:T(8,128)(2,1)S(1)}, bf16[1,1024,1024]{2,1,0:T(8,128)(2,1)}, u32[]{:S(2)}) copy-start(bf16[1,1024,1024]{2,1,0:T(8,128)(2,1)} %param.13) | copy-start | bytes 6291460
  0.0 4.3 %copy-start.3 = (bf16[1,128,4096]{2,1,0:T(8,128)(2,1)S(1)}, bf16[1,128,4096]{2,1,0:T(8,128)(2,1)}, u32[]{:S(2)}) copy-start(bf16[1,128,4096]{2,1,0:T(8,128)(2,1)} %param.7) | copy-start | bytes 3145732
  0.0 2.1 %copy-start.4 = (s32[128,4]{0,1:T(4,128)S(1)}, s32[128,4]{0,1:T(4,128)}, u32[]{:S(2)}) copy-start(s32[128,4]{0,1:T(4,128)} %param.10) | copy-start | bytes 6148
  2.1 2.3 %collective-permute-start = (bf16[128,2048]{1,0:T(8,128)(2,1)}, bf16[128,2048]{1,0:T(8,128)(2,1)}, u32[]{:S(2)}, u32[]{:S(2)}) collective-permute-start(bf16[128,2048]{1,0:T(8,128)(2,1)} %pad_maximum_fusion), channel_id=1, source_target_pairs={{0,1},{1,0},{2,3},{3,2},{4,5},{5,4},{6,7},{7,6},{8,9},{9,8},{10,11... | collective-permute-start | bytes 1572872 | tf_op jit(solution)/shard_map/ppermute | solution.py:9
  6.1 14.8 %copy-start.5 = (f32[1024]{0:T(1024)S(1)}, f32[1024]{0:T(1024)}, u32[]{:S(2)}) copy-start(f32[1024]{0:T(1024)} %param.9) | copy-start | bytes 12292
  6.1 8.7 %collective-permute-start.1 = (bf16[128,1024]{1,0:T(8,128)(2,1)}, bf16[128,1024]{1,0:T(8,128)(2,1)}, u32[]{:S(2)}, u32[]{:S(2)}) collective-permute-start(bf16[128,1024]{1,0:T(8,128)(2,1)} %fusion.30), channel_id=1, source_target_pairs={{0,2},{1,3},{2,0},{3,1},{4,6},{5,7},{6,4},{7,5},{8,10},{9,11},{10,... | collective-permute-start | bytes 786440 | tf_op jit(solution)/shard_map/ppermute | solution.py:9
  16.1 4.8 %copy-start.1 = (f32[128,1024]{1,0:T(8,128)}, f32[128,1024]{1,0:T(8,128)S(1)}, u32[]{:S(2)}) copy-start(f32[128,1024]{1,0:T(8,128)S(1)} %get-tuple-element.12) | copy-start | bytes 1572868
  16.1 1.2 collective-permute-start.2
  17.3 3.6 %collective-permute-start.3 = (f32[128]{0:T(128)S(1)}, f32[128]{0:T(128)S(1)}, u32[]{:S(2)}, u32[]{:S(2)}) collective-permute-start(f32[128]{0:T(128)S(1)} %add.108), channel_id=1, source_target_pairs={{0,2},{1,3},{2,0},{3,1},{4,6},{5,7},{6,4},{7,5},{8,10},{9,11},{10,... | collective-permute-start | bytes 1544 | tf_op jit(solution)/shard_map/ppermute | solution.py:9
  22.9 49.2 %all-to-all-start = ((bf16[64,80,128]{2,1,0:T(8,128)(2,1)}), bf16[64,80,128]{2,1,0:T(8,128)(2,1)S(1)}, u32[]{:S(2)}, u32[]{:S(2)}) async-start(bf16[64,80,128]{2,1,0:T(8,128)(2,1)} %reshape_reshape.12), calls=%async_computation | async-start | bytes 2621440 | tf_op jit(solution)/shard_map/all_to_all | solution.py:36
  73.5 2.1 %copy-start.2 = (bf16[640,1024]{1,0:T(8,128)(2,1)S(1)}, bf16[640,1024]{1,0:T(8,128)(2,1)}, u32[]{:S(2)}) copy-start(bf16[640,1024]{1,0:T(8,128)(2,1)} %reshape_reshape.13) | copy-start | bytes 3932164
  80.4 3.9 %collective-permute-start.4 = (bf16[320,2048]{1,0:T(8,128)(2,1)}, bf16[320,2048]{1,0:T(8,128)(2,1)S(1)}, u32[]{:S(2)}, u32[]{:S(2)}) collective-permute-start(bf16[320,2048]{1,0:T(8,128)(2,1)} %fusion.4), channel_id=1, source_target_pairs={{0,1},{1,0},{2,3},{3,2},{4,5},{5,4},{6,7},{7,6},{8,9},{9,8},{10,11... | collective-permute-start | bytes 3932168 | tf_op jit(solution)/shard_map/ppermute | solution.py:9
  84.8 17.2 %collective-permute-start.5 = (bf16[160,2048]{1,0:T(8,128)(2,1)S(1)}, bf16[160,2048]{1,0:T(8,128)(2,1)S(1)}, u32[]{:S(2)}, u32[]{:S(2)}) collective-permute-start(bf16[160,2048]{1,0:T(8,128)(2,1)S(1)} %get-tuple-element.13), channel_id=1, source_target_pairs={{0,2},{1,3},{2,0},{3,1},{4,6},{5,7},{6,4},{7,5},{8,10},{9,11},{10,... | collective-permute-start | bytes 1966088 | tf_op jit(solution)/shard_map/ppermute | solution.py:9
  102.5 9.4 %collective-permute-start.6 = (bf16[160,1024]{1,0:T(8,128)(2,1)S(1)}, bf16[160,1024]{1,0:T(8,128)(2,1)S(1)}, u32[]{:S(2)}, u32[]{:S(2)}) collective-permute-start(bf16[160,1024]{1,0:T(8,128)(2,1)S(1)} %get-tuple-element.10), channel_id=1, source_target_pairs={{0,2},{1,3},{2,0},{3,1},{4,6},{5,7},{6,4},{7,5},{8,10},{9,11},{10,... | collective-permute-start | bytes 983048 | tf_op jit(solution)/shard_map/ppermute | solution.py:9
  111.9 2.4 %collective-permute-start.7 = (bf16[320,1024]{1,0:T(8,128)(2,1)S(1)}, bf16[320,1024]{1,0:T(8,128)(2,1)S(1)}, u32[]{:S(2)}, u32[]{:S(2)}) collective-permute-start(bf16[320,1024]{1,0:T(8,128)(2,1)S(1)} %constant_dynamic-update-slice_fusion.1), channel_id=1, source_target_pairs={{0,1},{1,0},{2,3},{3,2},{4,5},{5,4},{6,7},{7,6},{8,9},{9,8},{10,11... | collective-permute-start | bytes 1966088 | tf_op jit(solution)/shard_map/ppermute | solution.py:9
  116.5 6.2 %copy-start.6 = (f32[128,4]{0,1:T(4,128)S(1)}, f32[128,4]{0,1:T(4,128)}, u32[]{:S(2)}) copy-start(f32[128,4]{0,1:T(4,128)} %param.11) | copy-start | bytes 6148
  116.5 42.2 %all-to-all-start.1 = ((bf16[64,80,128]{2,1,0:T(8,128)(2,1)}), bf16[64,80,128]{2,1,0:T(8,128)(2,1)S(1)}, u32[]{:S(2)}, u32[]{:S(2)}) async-start(bf16[64,80,128]{2,1,0:T(8,128)(2,1)} %reshape_reshape.14), calls=%async_computation.1 | async-start | bytes 2621440 | tf_op jit(solution)/shard_map/all_to_all | solution.py:36

commit v14 on v13

--- a/solution.py
+++ b/solution.py
@@ -94,13 +94,16 @@
     n = hidden.shape[0]
     pair = jnp.zeros((2 * n,) + hidden.shape[1:], hidden.dtype)
     pair = lax.dynamic_update_slice_in_dim(pair, hidden, high * n, 0)
-    pair = lax.dynamic_update_slice_in_dim(pair, _exchange(hidden, 2), (1 - high) * n, 0)
+    beside = _exchange(hidden, 2)
+    own_out = jnp.dot(hidden, w_down[0], preferred_element_type=jnp.float32).astype(jnp.bfloat16)
+    pair = lax.dynamic_update_slice_in_dim(pair, beside, (1 - high) * n, 0)
     pair = lax.optimization_barrier(pair)
     other = _exchange(pair, 1)
-    near = jnp.dot(pair, w_down[0], preferred_element_type=jnp.float32).astype(jnp.bfloat16)
+    beside_out = jnp.dot(beside, w_down[0], preferred_element_type=jnp.float32).astype(jnp.bfloat16)
     far_out = jnp.dot(other, w_down[0], preferred_element_type=jnp.float32).astype(jnp.bfloat16)
-    produced = jnp.zeros((4 * n, near.shape[1]), near.dtype)
-    produced = lax.dynamic_update_slice_in_dim(produced, near, 2 * core * n, 0)
+    produced = jnp.zeros((4 * n, own_out.shape[1]), own_out.dtype)
+    produced = lax.dynamic_update_slice_in_dim(produced, own_out, (2 * core + high) * n, 0)
+    produced = lax.dynamic_update_slice_in_dim(produced, beside_out, (2 * core + 1 - high) * n, 0)
     produced = lax.dynamic_update_slice_in_dim(produced, far_out, 2 * (1 - core) * n, 0)
     results = produced.reshape(source_count, item_count, feature_local)
     returned = _exchange_rows(results)

time: 164 us -> 169 us (1.030)
  local copies, waits for them, and re-layouts: 10.1 us -> 14.3 us
    unnamed x15 -> x23, local copies, waits for them, and re-layouts: 0.14 us -> 2.87 us
  transfers between devices with their start and end apart: 10 -> 10, of which waited for: 9 -> 8; matrix products, arithmetic and copies ran while one was open for 5% -> 5% of each run, Pallas kernels for 0% -> 0%
where the time goes in v14:
time: 169 us; the launch traced here: 168 us
  waiting for transfers between devices  106 us (63%)
  starting transfers between devices  24.8 us (15%)
  matrix products  15.3 us (9%)
  local copies, waits for them, and re-layouts  14.3 us (8%)
  other arithmetic  7.83 us (5%)
    all_to_all x2, waiting for transfers between devices, _exchange_rows(): lax.all_to_all(packed, 'expert', split_axis=0, concat_axis=0, tiled=True)  70.4 us
    ppermute x8, waiting for transfers between devices, _exchange(): return lax.ppermute(value, 'tensor', [(j, j ^ flip) for j in range(size)])  35.5 us
    all_to_all x2, starting transfers between devices, _exchange_rows(): lax.all_to_all(packed, 'expert', split_axis=0, concat_axis=0, tiled=True)  20.5 us
    dot_general x1, matrix products, _body(): jnp.dot(away_rows, w_in[0], preferred_element_type=jnp.float32)  4.8 us
    ppermute x8, starting transfers between devices, _exchange(): return lax.ppermute(value, 'tensor', [(j, j ^ flip) for j in range(size)])  4.36 us
    dot_general x1, matrix products, _body(): jnp.dot(home_rows, w_in[0], preferred_element_type=jnp.float32)  3.91 us
  transfers between devices with their start and end apart: 10, of which 8 were waited for; matrix products, arithmetic and copies ran while one was open for 5% of the time, Pallas kernels for 0%

profile of v14, /device:TPU:32, one launch (start us, length us, event | category | flops | bytes accessed | tf_op | source)
XLA Modules:
  0.0 168.5 jit_solution(5094219922565831170)
XLA Ops:
  0.0 1.2 dynamic-slice_bitcast_fusion.1
  1.3 0.8 pad_maximum_fusion
  2.3 2.0 %collective-permute-done = bf16[128,2048]{1,0:T(8,128)(2,1)} collective-permute-done((bf16[128,2048]{1,0:T(8,128)(2,1)}, bf16[128,2048]{1,0:T(8,128)(2,1)}, u32[]{:S(2)}, u32[]{:S(2)}) %collective-permute-start) | collective-permute-done | bytes 524320 | tf_op jit(solution)/shard_map/ppermute | solution.py:9
  4.3 1.7 %fusion.38 = bf16[128,1024]{1,0:T(8,128)(2,1)} fusion(bf16[128,2048]{1,0:T(8,128)(2,1)} %collective-permute-done, s32[]{:T(128)S(6)} %select_n.66, bf16[1,128,4096]{2,1,0:T(8,128)(2,1)S(1)} %copy-done.7, s32[]{:T(128)S(6)} %select_n.65), kind=kLoop, calls=%fused_computation.32 | loop fusion | flops 524288 | bytes 786440 | tf_op jit(solution)/shard_map/convert_element_type | solution.py:29
  6.1 1.5 collective-permute-start.1
  7.7 1.2 reduce-window.6
  9.5 5.3 %collective-permute-done.1 = bf16[128,1024]{1,0:T(8,128)(2,1)} collective-permute-done((bf16[128,1024]{1,0:T(8,128)(2,1)}, bf16[128,1024]{1,0:T(8,128)(2,1)}, u32[]{:S(2)}, u32[]{:S(2)}) %collective-permute-start.1) | collective-permute-done | bytes 262176 | tf_op jit(solution)/shard_map/ppermute | solution.py:9
  14.7 1.3 multiply_reduce_fusion
  16.2 1.1 collective-permute-done.2
  17.3 1.5 collective-permute-start.3
  19.0 1.9 %collective-permute-done.3 = f32[128]{0:T(128)S(1)} collective-permute-done((f32[128]{0:T(128)S(1)}, f32[128]{0:T(128)S(1)}, u32[]{:S(2)}, u32[]{:S(2)}) %collective-permute-start.3) | collective-permute-done | bytes 544 | tf_op jit(solution)/shard_map/ppermute | solution.py:9
  21.5 1.4 reshape_reshape.12
  22.9 14.2 %all-to-all-start = ((bf16[64,80,128]{2,1,0:T(8,128)(2,1)}), bf16[64,80,128]{2,1,0:T(8,128)(2,1)S(1)}, u32[]{:S(2)}, u32[]{:S(2)}) async-start(bf16[64,80,128]{2,1,0:T(8,128)(2,1)} %reshape_reshape.12), calls=%async_computation | async-start | bytes 2621440 | tf_op jit(solution)/shard_map/all_to_all | solution.py:36
  37.2 34.9 %all-to-all-done = bf16[64,80,128]{2,1,0:T(8,128)(2,1)S(1)} async-done(((bf16[64,80,128]{2,1,0:T(8,128)(2,1)}), bf16[64,80,128]{2,1,0:T(8,128)(2,1)S(1)}, u32[]{:S(2)}, u32[]{:S(2)}) %all-to-all-start) | async-done | bytes 1310752 | tf_op jit(solution)/shard_map/all_to_all | solution.py:36
  72.1 1.4 reshape_reshape.13
  73.5 2.1 %constant_dynamic-slice_fusion = bf16[320,1024]{1,0:T(8,128)(2,1)} fusion(bf16[640,1024]{1,0:T(8,128)(2,1)} %reshape_reshape.13, s32[]{:T(128)S(6)} %select_n.68), kind=kLoop, calls=%fused_computation.52 | loop fusion | bytes 1310724 | tf_op jit(solution)/shard_map/dynamic_slice | solution.py:13
  75.6 4.8 %fusion.4 = bf16[320,2048]{1,0:T(8,128)(2,1)} fusion(bf16[1,1024,2048]{2,1,0:T(8,128)(2,1)} %param.12, bf16[640,1024]{1,0:T(8,128)(2,1)S(1)} %copy-done.2, s32[]{:T(128)S(6)} %select_n.69), kind=kOutput, calls=%fused_computation.4 | convolution fusion | flops 1342832640 | bytes 6160388 | tf_op jit(solution)/shard_map/dot_general | solution.py:83
  80.4 3.9 %fusion.7 = bf16[320,2048]{1,0:T(8,128)(2,1)S(1)} fusion(bf16[320,1024]{1,0:T(8,128)(2,1)} %constant_dynamic-slice_fusion, bf16[1,1024,2048]{2,1,0:T(8,128)(2,1)} %param.12), kind=kOutput, calls=%fused_computation.5 | convolution fusion | flops 1342832640 | bytes 6160384 | tf_op jit(solution)/shard_map/dot_general | solution.py:86
  85.5 16.6 %collective-permute-done.5 = bf16[160,2048]{1,0:T(8,128)(2,1)S(1)} collective-permute-done((bf16[160,2048]{1,0:T(8,128)(2,1)S(1)}, bf16[160,2048]{1,0:T(8,128)(2,1)S(1)}, u32[]{:S(2)}, u32[]{:S(2)}) %collective-permute-start.5) | collective-permute-done | bytes 655392 | tf_op jit(solution)/shard_map/ppermute | solution.py:9
  102.2 0.9 broadcast_in_dim.26
  103.1 0.9 constant_dynamic-update-slice_fusion.1
  105.4 8.7 %collective-permute-done.6 = bf16[160,1024]{1,0:T(8,128)(2,1)S(1)} collective-permute-done((bf16[160,1024]{1,0:T(8,128)(2,1)S(1)}, bf16[160,1024]{1,0:T(8,128)(2,1)S(1)}, u32[]{:S(2)}, u32[]{:S(2)}) %collective-permute-start.6) | collective-permute-done | bytes 327712 | tf_op jit(solution)/shard_map/ppermute | solution.py:9
  114.0 0.7 copy-done.5
  114.8 0.7 constant_dynamic-update-slice_fusion
  115.7 0.8 copy-done.4
  118.0 1.9 %fusion.19 = bf16[640,1024]{1,0:T(8,128)(2,1)S(1)} fusion(bf16[640,1024]{1,0:T(8,128)(2,1)S(1)} %fusion.32, s32[]{:T(128)S(6)} %select_n.69, bf16[320,1024]{1,0:T(8,128)(2,1)} %collective-permute-done.7, bf16[1,1024,1024]{2,1,0:T(8,128)(2,1)S(1)} %copy-done), kind=kOutput, calls=%fused_computation.14 | convolution fusion | flops 671416320 | bytes 3407876 | tf_op jit(solution)/shard_map/dot_general | solution.py:103
  120.0 1.4 reshape_reshape.14
  121.4 6.2 %all-to-all-start.1 = ((bf16[64,80,128]{2,1,0:T(8,128)(2,1)}), bf16[64,80,128]{2,1,0:T(8,128)(2,1)S(1)}, u32[]{:S(2)}, u32[]{:S(2)}) async-start(bf16[64,80,128]{2,1,0:T(8,128)(2,1)} %reshape_reshape.14), calls=%async_computation.1 | async-start | bytes 2621440 | tf_op jit(solution)/shard_map/all_to_all | solution.py:36
  127.6 0.9 select_reduce_fusion
  128.5 35.4 %all-to-all-done.1 = bf16[64,80,128]{2,1,0:T(8,128)(2,1)S(1)} async-done(((bf16[64,80,128]{2,1,0:T(8,128)(2,1)}), bf16[64,80,128]{2,1,0:T(8,128)(2,1)S(1)}, u32[]{:S(2)}, u32[]{:S(2)}) %all-to-all-start.1) | async-done | bytes 1310752 | tf_op jit(solution)/shard_map/all_to_all | solution.py:36
  164.0 1.4 reshape_reshape.15
  165.4 3.1 %fusion.35 = bf16[128,1024]{1,0:T(8,128)(2,1)} fusion(f32[128,1024]{1,0:T(8,128)} %copy-done.1, f32[640,128]{1,0:T(8,128)} %select_reduce_fusion, bf16[640,1024]{1,0:T(8,128)(2,1)} %reshape_reshape.15), kind=kOutput, calls=%fused_computation.26 | convolution fusion | flops 1006895104 | bytes 2424832 | tf_op jit(solution)/shard_map/dot_general | solution.py:110
  (48 shorter events, 6.0 us)
Async XLA Ops:
  0.0 115.7 %copy-start = (bf16[1,1024,1024]{2,1,0:T(8,128)(2,1)S(1)}, bf16[1,1024,1024]{2,1,0:T(8,128)(2,1)}, u32[]{:S(2)}) copy-start(bf16[1,1024,1024]{2,1,0:T(8,128)(2,1)} %param.13) | copy-start | bytes 6291460
  0.0 4.3 %copy-start.7 = (bf16[1,128,4096]{2,1,0:T(8,128)(2,1)S(1)}, bf16[1,128,4096]{2,1,0:T(8,128)(2,1)}, u32[]{:S(2)}) copy-start(bf16[1,128,4096]{2,1,0:T(8,128)(2,1)} %param.7) | copy-start | bytes 3145732
  0.0 2.1 %copy-start.8 = (s32[128,4]{0,1:T(4,128)S(1)}, s32[128,4]{0,1:T(4,128)}, u32[]{:S(2)}) copy-start(s32[128,4]{0,1:T(4,128)} %param.10) | copy-start | bytes 6148
  2.1 2.3 %collective-permute-start = (bf16[128,2048]{1,0:T(8,128)(2,1)}, bf16[128,2048]{1,0:T(8,128)(2,1)}, u32[]{:S(2)}, u32[]{:S(2)}) collective-permute-start(bf16[128,2048]{1,0:T(8,128)(2,1)} %pad_maximum_fusion), channel_id=1, source_target_pairs={{0,1},{1,0},{2,3},{3,2},{4,5},{5,4},{6,7},{7,6},{8,9},{9,8},{10,11... | collective-permute-start | bytes 1572872 | tf_op jit(solution)/shard_map/ppermute | solution.py:9
  6.1 14.8 %copy-start.9 = (f32[1024]{0:T(1024)S(1)}, f32[1024]{0:T(1024)}, u32[]{:S(2)}) copy-start(f32[1024]{0:T(1024)} %param.9) | copy-start | bytes 12292
  6.1 8.7 %collective-permute-start.1 = (bf16[128,1024]{1,0:T(8,128)(2,1)}, bf16[128,1024]{1,0:T(8,128)(2,1)}, u32[]{:S(2)}, u32[]{:S(2)}) collective-permute-start(bf16[128,1024]{1,0:T(8,128)(2,1)} %fusion.38), channel_id=1, source_target_pairs={{0,2},{1,3},{2,0},{3,1},{4,6},{5,7},{6,4},{7,5},{8,10},{9,11},{10,... | collective-permute-start | bytes 786440 | tf_op jit(solution)/shard_map/ppermute | solution.py:9
  16.1 4.8 %copy-start.1 = (f32[128,1024]{1,0:T(8,128)}, f32[128,1024]{1,0:T(8,128)S(1)}, u32[]{:S(2)}) copy-start(f32[128,1024]{1,0:T(8,128)S(1)} %get-tuple-element.12) | copy-start | bytes 1572868
  16.1 1.2 collective-permute-start.2
  17.3 3.6 %collective-permute-start.3 = (f32[128]{0:T(128)S(1)}, f32[128]{0:T(128)S(1)}, u32[]{:S(2)}, u32[]{:S(2)}) collective-permute-start(f32[128]{0:T(128)S(1)} %add.119), channel_id=1, source_target_pairs={{0,2},{1,3},{2,0},{3,1},{4,6},{5,7},{6,4},{7,5},{8,10},{9,11},{10,... | collective-permute-start | bytes 1544 | tf_op jit(solution)/shard_map/ppermute | solution.py:9
  22.9 49.2 %all-to-all-start = ((bf16[64,80,128]{2,1,0:T(8,128)(2,1)}), bf16[64,80,128]{2,1,0:T(8,128)(2,1)S(1)}, u32[]{:S(2)}, u32[]{:S(2)}) async-start(bf16[64,80,128]{2,1,0:T(8,128)(2,1)} %reshape_reshape.12), calls=%async_computation | async-start | bytes 2621440 | tf_op jit(solution)/shard_map/all_to_all | solution.py:36
  73.5 2.1 %copy-start.2 = (bf16[640,1024]{1,0:T(8,128)(2,1)S(1)}, bf16[640,1024]{1,0:T(8,128)(2,1)}, u32[]{:S(2)}) copy-start(bf16[640,1024]{1,0:T(8,128)(2,1)} %reshape_reshape.13) | copy-start | bytes 3932164
  80.4 3.9 %collective-permute-start.4 = (bf16[320,2048]{1,0:T(8,128)(2,1)}, bf16[320,2048]{1,0:T(8,128)(2,1)S(1)}, u32[]{:S(2)}, u32[]{:S(2)}) collective-permute-start(bf16[320,2048]{1,0:T(8,128)(2,1)} %fusion.4), channel_id=1, source_target_pairs={{0,1},{1,0},{2,3},{3,2},{4,5},{5,4},{6,7},{7,6},{8,9},{9,8},{10,11... | collective-permute-start | bytes 3932168 | tf_op jit(solution)/shard_map/ppermute | solution.py:9
  84.8 17.2 %collective-permute-start.5 = (bf16[160,2048]{1,0:T(8,128)(2,1)S(1)}, bf16[160,2048]{1,0:T(8,128)(2,1)S(1)}, u32[]{:S(2)}, u32[]{:S(2)}) collective-permute-start(bf16[160,2048]{1,0:T(8,128)(2,1)S(1)} %get-tuple-element.13), channel_id=1, source_target_pairs={{0,2},{1,3},{2,0},{3,1},{4,6},{5,7},{6,4},{7,5},{8,10},{9,11},{10,... | collective-permute-start | bytes 1966088 | tf_op jit(solution)/shard_map/ppermute | solution.py:9
  104.0 0.7 copy-start.3
  104.8 9.3 %collective-permute-start.6 = (bf16[160,1024]{1,0:T(8,128)(2,1)S(1)}, bf16[160,1024]{1,0:T(8,128)(2,1)S(1)}, u32[]{:S(2)}, u32[]{:S(2)}) collective-permute-start(bf16[160,1024]{1,0:T(8,128)(2,1)S(1)} %get-tuple-element.10), channel_id=1, source_target_pairs={{0,2},{1,3},{2,0},{3,1},{4,6},{5,7},{6,4},{7,5},{8,10},{9,11},{10,... | collective-permute-start | bytes 983048 | tf_op jit(solution)/shard_map/ppermute | solution.py:9
  114.0 0.7 copy-start.5
  115.5 2.5 %collective-permute-start.7 = (bf16[320,1024]{1,0:T(8,128)(2,1)}, bf16[320,1024]{1,0:T(8,128)(2,1)}, u32[]{:S(2)}, u32[]{:S(2)}) collective-permute-start(bf16[320,1024]{1,0:T(8,128)(2,1)} %constant_dynamic-update-slice_fusion), channel_id=1, source_target_pairs={{0,1},{1,0},{2,3},{3,2},{4,5},{5,4},{6,7},{7,6},{8,9},{9,8},{10,11... | collective-permute-start | bytes 1966088 | tf_op jit(solution)/shard_map/ppermute | solution.py:9
  115.5 1.0 copy-start.4
  116.5 1.0 copy-start.6
  121.4 6.3 %copy-start.10 = (f32[128,4]{0,1:T(4,128)S(1)}, f32[128,4]{0,1:T(4,128)}, u32[]{:S(2)}) copy-start(f32[128,4]{0,1:T(4,128)} %param.11) | copy-start | bytes 6148
  121.4 42.6 %all-to-all-start.1 = ((bf16[64,80,128]{2,1,0:T(8,128)(2,1)}), bf16[64,80,128]{2,1,0:T(8,128)(2,1)S(1)}, u32[]{:S(2)}, u32[]{:S(2)}) async-start(bf16[64,80,128]{2,1,0:T(8,128)(2,1)} %reshape_reshape.14), calls=%async_computation.1 | async-start | bytes 2621440 | tf_op jit(solution)/shard_map/all_to_all | solution.py:36
